TPU v7x, 256 devices: a whole 4x4x8 slice. The times are simulated.
256 devices in a mesh: rep: 64 (over y, x, z_lo), slab: 4 (over z_hi, core).
Axes of the slice: x: 4, y: 4, z: 8 (z_hi: 2, z_lo: 4; z = z_hi * 4 + z_lo), core: 2. Of those that a mesh axis runs over, the one named last changes fastest.
Arguments:
- positions: float32 [64, 3, 16384], P('rep', None, 'slab'), may hold values from 0 to 2
- velocities: float32 [64, 3, 16384], P('rep', None, 'slab'), may hold values from -6 to 6
- inv_mass: float32 [16384], P('slab'), may hold values from 0.5 to 2
- strength: float32 [16384], P('slab'), may hold values from 0.5 to 2
- charge: float32 [16384], P('slab'), may hold values from -1 to 1
- scaling: float32 [64], P('rep'), may hold values from 0.3 to 1
- tile_pairs: int32 [64, 2, 768], P('rep', None, 'slab'), may hold values from 0 to 79, as said below
- tile_counts: int32 [64, 4], P('rep', 'slab'), may hold values from 24 to 192, as said below
- halo_clusters: int32 [64, 64], P('rep', 'slab'), may hold values from 0 to 63, as said below
- swap_pairs: int32 [16, 2], replicated, may hold values from 0 to 63, as said below
Outputs:
- new_positions: float32 [64, 3, 16384], P('rep', None, 'slab')
- new_velocities: float32 [64, 3, 16384], P('rep', None, 'slab')
- potential: float32 [64], P('rep')
Inputs may be any that keep to these rules, and one draw needn't show every extreme that they name: `tile_pairs`: for each replica and slab, the 192 columns are distinct tiles (i, j) with i a cluster of that slab and i <= j; j below 64 is a cluster of the same slab, j = 64 + h is halo slot h. Only the first tile_counts columns are live. `tile_counts`: in every replica some slab has all 192 tiles live. `halo_clusters`: the 16 clusters of each replica and slab are distinct. `swap_pairs`: no replica appears twice. The first pair joins two replicas 64 // 2 apart (counted round), the second two neighbouring replicas (counted round); the others are arbitrary.
All inputs are finite; a program needn't handle non-finite values.
Results may differ from a plain program's by a relative error of at most 0.0003.
Values sent between devices are 32-bit elements; how exact they have to be, the bound alone decides.
No kernel may reach another device: no remote copies, remote signals or barrier semaphores. Data moves between devices by JAX's collectives and lax.ppermute only.
A program may use at most 64 MiB of HBM per device.

v0:
```python
import jax
import jax.numpy as jnp
from jax import lax
from jax.sharding import PartitionSpec as P

CL = 64
CD = 64
STEPS = 4
HALO = 16
NT_MAX = 192


tile_block = 16
time_step = 0.04
half_step = 0.02
soft_sq = 0.25
slab_width = 2.0
exact = lax.Precision.HIGHEST


def from_behind(value, axis, steps):
    count = lax.axis_size(axis)
    pairs = [(source, (source + steps) % count) for source in range(count)]
    return lax.ppermute(value, axis, pairs)


def partner_of(pair_list, replica_ids):
    first_col = pair_list[:, 0]
    second_col = pair_list[:, 1]
    hit_first = replica_ids[:, None] == first_col[None, :]
    hit_second = replica_ids[:, None] == second_col[None, :]
    partner_sum = jnp.sum(jnp.where(hit_first, second_col[None, :], 0), 1) + jnp.sum(
        jnp.where(hit_second, first_col[None, :], 0), 1
    )
    listed = jnp.any(hit_first, 1) | jnp.any(hit_second, 1)
    return jnp.where(listed, partner_sum, replica_ids)


def select_table(index_list, width):
    cluster_ids = jnp.arange(width, dtype=jnp.int32)
    return (index_list[:, None] == cluster_ids[None, :]).astype(jnp.float32)


def pair_block(extended, strength_all, charge_all, ham_scale, tile_first, tile_second, live_mask):
    count_tiles = tile_first.shape[0]
    width = extended.shape[1]
    select_first = select_table(tile_first, width)
    select_second = select_table(tile_second, width)
    coords_i = jnp.einsum("te,xec->xct", select_first, extended, precision=exact)
    coords_j = jnp.einsum("te,xec->xtc", select_second, extended, precision=exact)
    offsets = (coords_i[:, :, :, None] - coords_j[:, None, :, :]).reshape(3, CL, count_tiles * CL)
    sq_dist = offsets[0] * offsets[0] + offsets[1] * offsets[1] + offsets[2] * offsets[2]
    params_all = jnp.stack([strength_all, charge_all], 0)
    params_i = jnp.einsum("te,pec->pct", select_first, params_all, precision=exact)
    params_j = jnp.einsum("te,pec->ptc", select_second, params_all, precision=exact)
    strength_prod = (params_i[0][:, :, None] * params_j[0][None, :, :]).reshape(
        CL, count_tiles * CL
    )
    charge_prod = (params_i[1][:, :, None] * params_j[1][None, :, :]).reshape(CL, count_tiles * CL)
    gauss_term = strength_prod * jnp.exp(-sq_dist)
    inv_root = lax.rsqrt(sq_dist + soft_sq)
    coulomb = ham_scale * charge_prod * inv_root
    same_tile = tile_first == tile_second
    weight_tile = jnp.where(live_mask, jnp.where(same_tile, 0.5, 1.0), 0.0).astype(jnp.float32)
    weight_col = jnp.repeat(weight_tile, CL)[None, :]
    slope = gauss_term + 0.5 * coulomb * inv_root * inv_root
    pushes = (2.0 * slope * weight_col)[None, :, :] * offsets
    force_i = pushes.reshape(3, CL, count_tiles, CL).sum(-1)
    force_j = -pushes.sum(1).reshape(3, count_tiles, CL)
    atom_ids = jnp.arange(CL, dtype=jnp.int32)
    column_ids = jnp.arange(count_tiles * CL, dtype=jnp.int32) % CL
    self_pair = jnp.repeat(same_tile, CL)[None, :] & (atom_ids[:, None] == column_ids[None, :])
    energy = jnp.sum(jnp.where(self_pair, 0.0, (gauss_term + coulomb) * weight_col))
    spread_i = jnp.einsum("te,xct->xec", select_first, force_i, precision=exact)
    spread_j = jnp.einsum("te,xtc->xec", select_second, force_j, precision=exact)
    return (spread_i + spread_j, energy)


def local(
    positions,
    velocities,
    inv_mass,
    strength,
    charge,
    scaling,
    tile_pairs,
    tile_counts,
    halo_clusters,
    swap_pairs,
):
    coords = positions[0]
    speeds = velocities[0]
    ham_scale = scaling[0]
    firsts_flat = tile_pairs[0, 0]
    seconds_flat = tile_pairs[0, 1]
    live_count = tile_counts[0, 0]
    halo_index = halo_clusters[0]
    atoms_here = coords.shape[1]
    halo_table = select_table(halo_index, CD)
    params = jnp.stack([strength, charge], 0).reshape(2, CD, CL)
    sent_params = jnp.einsum("hc,pck->phk", halo_table, params, precision=exact).reshape(
        2, HALO * CL
    )
    got_params = from_behind(sent_params, "slab", -1).reshape(2, HALO, CL)
    strength_all = jnp.concatenate([params[0], got_params[0]], 0)
    charge_all = jnp.concatenate([params[1], got_params[1]], 0)
    lift = jnp.array([0.0, 0.0, slab_width], jnp.float32)[:, None]
    extended_now = [None]

    def add_block(totals, tile_first, tile_second, slot_row):
        spread, energy_part = pair_block(
            extended_now[0],
            strength_all,
            charge_all,
            ham_scale,
            tile_first,
            tile_second,
            slot_row < live_count,
        )
        return (totals[0] + spread, totals[1] + energy_part)

    def evaluate(coords_now):
        blocks = coords_now.reshape(3, CD, CL)
        sent_coords = jnp.einsum("hc,xck->xhk", halo_table, blocks, precision=exact).reshape(
            3, HALO * CL
        )
        from_above = from_behind(sent_coords, "slab", -1) + lift
        extended_now[0] = jnp.concatenate([blocks, from_above.reshape(3, HALO, CL)], 1)
        start_state = (jnp.zeros((3, CD + HALO, CL), jnp.float32), jnp.zeros((), jnp.float32))
        firsts = firsts_flat.reshape(-1, tile_block)
        seconds = seconds_flat.reshape(-1, tile_block)
        slot_ids = jnp.arange(NT_MAX, dtype=jnp.int32).reshape(-1, tile_block)

        def visit_block(totals, inputs):
            return (add_block(totals, inputs[0], inputs[1], inputs[2]), None)

        result, _ = lax.scan(visit_block, start_state, (firsts, seconds, slot_ids))
        forces, energy = result
        returned = from_behind(forces[:, CD:].reshape(3, HALO * CL), "slab", 1)
        back_home = jnp.einsum(
            "hc,xhk->xck", halo_table, returned.reshape(3, HALO, CL), precision=exact
        )
        local_forces = forces[:, :CD] + back_home
        return (local_forces.reshape(3, atoms_here), energy)

    forces, energy = evaluate(coords)
    for step_idx in range(STEPS):
        speeds = speeds + half_step * forces * inv_mass
        coords = coords + time_step * speeds
        forces, energy = evaluate(coords)
        speeds = speeds + half_step * forces * inv_mass
    total_energy = lax.psum(energy, "slab")
    potential = (total_energy / (atoms_here * lax.axis_size("slab"))).reshape(1)
    state = jnp.concatenate([coords, speeds], 0)
    partner_me = partner_of(swap_pairs, lax.axis_index("rep").reshape(1))[0]
    shard_rows = lax.all_gather(state[None], "rep", axis=0, tiled=True)
    row_ids = jnp.arange(shard_rows.shape[0], dtype=jnp.int32)
    chosen = row_ids == partner_me
    swapped = jnp.sum(jnp.where(chosen[:, None, None], shard_rows, 0.0), 0)
    return (swapped[:3][None], swapped[3:][None], potential)


def solution(mesh):
    in_specs = (
        P("rep", None, "slab"),
        P("rep", None, "slab"),
        P("slab"),
        P("slab"),
        P("slab"),
        P("rep"),
        P("rep", None, "slab"),
        P("rep", "slab"),
        P("rep", "slab"),
        P(),
    )
    out_specs = (P("rep", None, "slab"), P("rep", None, "slab"), P("rep"))
    return jax.shard_map(local, mesh=mesh, in_specs=in_specs, out_specs=out_specs, check_vma=False)
```

profile of v0, /device:TPU:0, one launch (start us, length us, event | category | flops | bytes accessed | tf_op | source)
XLA Modules:
  0.0 775.9 jit_solution(11839752525932202935)
XLA Ops:
  9.7 4.9 collective-permute-start
  21.1 60.0 %while.67 = (s32[]{:T(128)}, f32[3,80,64]{1,2,0:T(8,128)S(1)}, s32[12,16]{1,0:T(8,128)S(1)}, f32[2,80,64]{1,2,0:T(8,128)S(1)}, s32[12,16]{1,0:T(8,128)S(1)}, /*i...) while((s32[]{:T(128)}, f32[3,80,64]{1,2,0:T(8,128)S(1)}, ...), condition=%wide.region_7.8_spmd.clone, body=%wide.region_4.7_spmd.clone.sunk | while | flops 17876564 | bytes 2778059 | solution.py:137
  23.6 1.0 fusion.306
  28.6 1.0 fusion.306
  33.6 1.0 fusion.306
  38.6 1.0 fusion.306
  43.6 1.0 fusion.306
  48.6 1.0 fusion.306
  53.6 1.0 fusion.306
  58.6 1.0 fusion.306
  63.6 1.0 fusion.306
  68.6 1.0 fusion.306
  73.6 1.0 fusion.306
  78.6 1.0 fusion.306
  82.1 6.4 collective-permute-done.2
  89.3 1.4 collective-permute-done.3
  91.1 60.0 %while.68 = (s32[]{:T(128)}, f32[3,80,64]{1,2,0:T(8,128)S(1)}, s32[12,16]{1,0:T(8,128)S(1)}, f32[2,80,64]{1,2,0:T(8,128)S(1)}, s32[12,16]{1,0:T(8,128)S(1)}, /*i...) while((s32[]{:T(128)}, f32[3,80,64]{1,2,0:T(8,128)S(1)}, ...), condition=%wide.region_11.12_spmd.clone, body=%wide.region_8.11_spmd.clone.sunk | while | flops 17876564 | bytes 2778059 | solution.py:137
  108.6 1.0 fusion.322
  128.6 1.0 fusion.322
  148.6 1.0 fusion.322
  152.0 6.5 collective-permute-done.4
  159.5 1.4 collective-permute-done.5
  161.3 60.0 %while.69 = (s32[]{:T(128)}, f32[3,80,64]{1,2,0:T(8,128)S(1)}, s32[12,16]{1,0:T(8,128)S(1)}, f32[2,80,64]{1,2,0:T(8,128)S(1)}, s32[12,16]{1,0:T(8,128)S(1)}, /*i...) while((s32[]{:T(128)}, f32[3,80,64]{1,2,0:T(8,128)S(1)}, ...), condition=%wide.region_15.16_spmd.clone, body=%wide.region_12.15_spmd.clone.sunk | while | flops 17876564 | bytes 2778059 | solution.py:137
  168.8 1.0 fusion.338
  188.8 1.0 fusion.338
  208.8 1.0 fusion.338
  222.2 6.5 collective-permute-done.6
  229.5 1.4 collective-permute-done.7
  231.3 60.0 %while.70 = (s32[]{:T(128)}, f32[3,80,64]{1,2,0:T(8,128)S(1)}, s32[12,16]{1,0:T(8,128)S(1)}, f32[2,80,64]{1,2,0:T(8,128)S(1)}, s32[12,16]{1,0:T(8,128)S(1)}, /*i...) while((s32[]{:T(128)}, f32[3,80,64]{1,2,0:T(8,128)S(1)}, ...), condition=%wide.region_19.20_spmd.clone, body=%wide.region_16.19_spmd.clone.sunk | while | flops 17876564 | bytes 2778059 | solution.py:137
  292.1 6.5 collective-permute-done.8
  299.4 1.4 collective-permute-done.9
  301.2 77.0 %while.71 = (s32[]{:T(128)}, f32[3,80,64]{1,2,0:T(8,128)S(1)}, f32[]{:T(128)}, s32[12,16]{1,0:T(8,128)S(1)}, f32[2,80,64]{1,2,0:T(8,128)S(1)}, /*index=5*/s32[12...) while((s32[]{:T(128)}, f32[3,80,64]{1,2,0:T(8,128)S(1)}, ...), condition=%wide.region_24.25_spmd.clone, body=%wide.region_20.24_spmd.clone.sunk | while | flops 18283088 | bytes 2786435 | solution.py:137
  303.7 1.8 select_reduce_fusion.3
  310.1 1.8 select_reduce_fusion.3
  316.5 1.8 select_reduce_fusion.3
  323.0 1.8 select_reduce_fusion.3
  329.4 1.8 select_reduce_fusion.3
  335.8 1.8 select_reduce_fusion.3
  342.2 1.8 select_reduce_fusion.3
  348.6 1.8 select_reduce_fusion.3
  355.0 1.8 select_reduce_fusion.3
  361.5 1.8 select_reduce_fusion.3
  367.9 1.8 select_reduce_fusion.3
  374.3 1.8 select_reduce_fusion.3
  380.1 5.7 collective-permute-done.10
  391.2 10.9 %psum.7 = f32[]{:T(128)} all-reduce(f32[]{:T(128)} %get-tuple-element.598), channel_id=1, replica_groups=mesh['rep'=64,'slab'=4] {'slab'}, use_global_device_ids=true, to_apply=%region_26.27 | all-reduce | flops 1 | bytes 8 | tf_op jit(solution)/shard_map/psum | solution.py:152
  402.8 359.3 %all-gather.4.cloned.1.call-done = f32[64,6,4096]{2,1,0:T(8,128)} async-done(((f32[1,6,4096]{2,1,0:T(8,128)}), f32[64,6,4096]{2,1,0:T(8,128)}) %all-gather.4.cloned.1.call-update) | async-done | bytes 6291472 | tf_op jit(solution)/shard_map/all_gather | solution.py:156
  762.1 4.5 select_reduce_fusion.1
  (1011 shorter events, 287.0 us)
Async XLA Ops:
  7.2 754.9 %all-gather.4.cloned.1.call-start = ((), (), s32[]{:S(2)}) async-start(), calls=%async_computation | async-start | bytes 8519680 | tf_op jit(solution)/shard_map/all_gather | solution.py:156
  9.7 10.2 %collective-permute-start = (f32[2,1024]{1,0:T(2,128)S(1)}, f32[2,1024]{1,0:T(2,128)S(1)}, u32[]{:S(2)}, u32[]{:S(2)}) collective-permute-start(f32[2,1024]{1,0:T(2,128)S(1)} %reshape.1061), channel_id=1, source_target_pairs={{0,3},{1,0},{2,1},{3,2},{4,7},{5,4},{6,5},{7,6},{8,11},{9,8},{10,9... | collective-permute-start | bytes 24584 | tf_op jit(solution)/shard_map/ppermute | solution.py:24
  16.6 3.5 collective-permute-start.1
  21.1 60.4 %copy-start.3 = (f32[4096]{0:T(1024)S(1)}, f32[4096]{0:T(1024)}, u32[]{:S(2)}) copy-start(f32[4096]{0:T(1024)} %param.23) | copy-start | bytes 49156
  21.1 60.7 %copy-start.1 = (f32[1,3,4096]{2,0,1:T(1,128)S(1)}, f32[1,3,4096]{2,0,1:T(1,128)}, u32[]{:S(2)}) copy-start(f32[1,3,4096]{2,0,1:T(1,128)} %param.22) | copy-start | bytes 147460
  21.1 67.5 %copy-start.2 = (s32[1,16]{1,0:T(1,128)S(1)}, s32[1,16]{1,0:T(1,128)}, u32[]{:S(2)}) copy-start(s32[1,16]{1,0:T(1,128)} %param.29) | copy-start | bytes 196
  81.2 9.6 %copy-start.4 = (f32[3]{0:T(128)S(1)}, f32[3]{0:T(128)}, u32[]{:S(2)}) copy-start(f32[3]{0:T(128)} %constant.233.clone) | copy-start | bytes 40
  81.5 7.1 collective-permute-start.2
  89.3 1.5 collective-permute-start.3
  151.4 7.1 collective-permute-start.4
  159.3 1.7 collective-permute-start.5
  221.6 7.1 collective-permute-start.6
  229.4 1.5 collective-permute-start.7
  291.5 7.1 collective-permute-start.8
  299.4 1.5 collective-permute-start.9
  378.2 8.2 %copy-start = (f32[1,3,4096]{2,0,1:T(1,128)S(1)}, f32[1,3,4096]{2,0,1:T(1,128)}, u32[]{:S(2)}) copy-start(f32[1,3,4096]{2,0,1:T(1,128)} %param.21) | copy-start | bytes 147460
  378.4 8.9 %copy-start.5 = (s32[16,2]{0,1:T(2,128)S(1)}, s32[16,2]{0,1:T(2,128)}, u32[]{:S(2)}) copy-start(s32[16,2]{0,1:T(2,128)} %param.30) | copy-start | bytes 388
  378.5 7.3 collective-permute-start.10
Sparse Core Ops, SparseCore 0:
  387.4 374.6 all-gather.3
where the time goes:
time: 778 us; the launch traced here: 776 us
  waiting for transfers between devices  397 us (51%)
  other arithmetic  204 us (26%)
  matrix products  91.9 us (12%)
  local copies, waits for them, and re-layouts  31.6 us (4%)
  between operations  18.9 us (2%)
  loops' own time  12.9 us (2%)
  blocking collectives  10.9 us (1%)
  starting transfers between devices  8.55 us (1%)
    all_gather x1, waiting for transfers between devices, local(): shard_rows = lax.all_gather(state[None], 'rep', axis=0, tiled=True)  359 us
    mul x108, other arithmetic, pair_block(): pushes = (2.0 * slope * weight_col)[None, :, :] * offsets  89 us
    reduce_sum x60, other arithmetic, pair_block(): force_j = -pushes.sum(1).reshape(3, count_tiles, CL)  56.1 us
    ppermute x11, waiting for transfers between devices, from_behind(): return lax.ppermute(value, axis, pairs)  37.5 us
    sub x60, other arithmetic, pair_block(): coords_i[:, :, :, None] - coords_j[:, None, :, :]  28.5 us
    reduce_sum x12, other arithmetic, pair_block(): jnp.sum(jnp.where(self_pair, 0.0, (gauss_term + coulomb) * weight_col))  21.4 us
    dot_general x60, matrix products, pair_block(): jnp.einsum('te,xtc->xec', select_second, force_j, precision=exact)  18.1 us
    dot_general x60, matrix products, pair_block(): jnp.einsum('te,xec->xtc', select_second, extended, precision=exact)  17.7 us
  transfers between devices with their start and end apart: 12, of which 10 were waited for; matrix products, arithmetic and copies ran while one was open for 1% of the time, Pallas kernels for 0%

commit v1 on v0

--- a/solution.py
+++ b/solution.py
@@ -34,6 +34,17 @@
     )
     listed = jnp.any(hit_first, 1) | jnp.any(hit_second, 1)
     return jnp.where(listed, partner_sum, replica_ids)
+
+
+def exchange(state, swap_pairs):
+    count = lax.axis_size("rep")
+    rows, width = state.shape
+    partner = partner_of(swap_pairs, jnp.arange(count, dtype=jnp.int32))
+    chunks = state.reshape(rows, count, width // count).transpose(1, 0, 2)
+    spread = lax.all_to_all(chunks, "rep", 0, 0, tiled=True)
+    routed = jnp.take(spread, partner, axis=0)
+    gathered = lax.all_to_all(routed, "rep", 0, 0, tiled=True)
+    return gathered.transpose(1, 0, 2).reshape(rows, width)
 
 
 def select_table(index_list, width):
@@ -152,11 +163,7 @@
     total_energy = lax.psum(energy, "slab")
     potential = (total_energy / (atoms_here * lax.axis_size("slab"))).reshape(1)
     state = jnp.concatenate([coords, speeds], 0)
-    partner_me = partner_of(swap_pairs, lax.axis_index("rep").reshape(1))[0]
-    shard_rows = lax.all_gather(state[None], "rep", axis=0, tiled=True)
-    row_ids = jnp.arange(shard_rows.shape[0], dtype=jnp.int32)
-    chosen = row_ids == partner_me
-    swapped = jnp.sum(jnp.where(chosen[:, None, None], shard_rows, 0.0), 0)
+    swapped = exchange(state, swap_pairs)
     return (swapped[:3][None], swapped[3:][None], potential)
 
 

time: 778 us -> 427 us (0.55)
  waiting for transfers between devices: 397 us -> 48.3 us
  between operations: 18.9 us -> 2.95 us
  starting transfers between devices: 8.55 us -> 22.4 us
    all_gather x1 -> x0, waiting for transfers between devices: 359 us -> none  [local(): shard_rows = lax.all_gather(state[None], 'rep', axis=0, tiled=True)]
    all_to_all x0 -> x2, starting transfers between devices: none -> 13.9 us  [the longest x1 9.28 us: exchange(): spread = lax.all_to_all(chunks, 'rep', 0, 0, tiled=True)]
    all_to_all x0 -> x2, waiting for transfers between devices: none -> 10.2 us  [the longest x1 10.2 us: exchange(): spread = lax.all_to_all(chunks, 'rep', 0, 0, tiled=True)]
  transfers between devices with their start and end apart: 12 -> 13, of which waited for: 10 -> 10; matrix products, arithmetic and copies ran while one was open for 1% -> 1% of each run, Pallas kernels for 0% -> 0%
where the time goes in v1:
time: 427 us; the launch traced here: 423 us
  other arithmetic  204 us (48%)
  matrix products  85.8 us (20%)
  waiting for transfers between devices  48.3 us (11%)
  local copies, waits for them, and re-layouts  36.2 us (8%)
  starting transfers between devices  22.4 us (5%)
  loops' own time  13.2 us (3%)
  blocking collectives  11 us (3%)
    mul x108, other arithmetic, pair_block(): pushes = (2.0 * slope * weight_col)[None, :, :] * offsets  91.2 us
    reduce_sum x60, other arithmetic, pair_block(): force_j = -pushes.sum(1).reshape(3, count_tiles, CL)  56.2 us
    ppermute x11, waiting for transfers between devices, from_behind(): return lax.ppermute(value, axis, pairs)  38.1 us
    sub x60, other arithmetic, pair_block(): coords_i[:, :, :, None] - coords_j[:, None, :, :]  29.5 us
    reduce_sum x12, other arithmetic, pair_block(): jnp.sum(jnp.where(self_pair, 0.0, (gauss_term + coulomb) * weight_col))  21.4 us
    dot_general x60, matrix products, pair_block(): jnp.einsum('te,xtc->xec', select_second, force_j, precision=exact)  18 us
    dot_general x60, matrix products, pair_block(): jnp.einsum('te,xec->xtc', select_second, extended, precision=exact)  15.1 us
    dot_general x60, matrix products, pair_block(): jnp.einsum('te,xec->xct', select_first, extended, precision=exact)  14.8 us
  transfers between devices with their start and end apart: 13, of which 10 were waited for; matrix products, arithmetic and copies ran while one was open for 1% of the time, Pallas kernels for 0%

profile of v1, /device:TPU:0, one launch (start us, length us, event | category | flops | bytes accessed | tf_op | source)
XLA Modules:
  0.0 423.4 jit_solution(4065141461597668866)
XLA Ops:
  3.1 4.9 %collective-permute-start = (f32[2,1024]{1,0:T(2,128)S(1)}, f32[2,1024]{1,0:T(2,128)S(1)}, u32[]{:S(2)}, u32[]{:S(2)}) collective-permute-start(f32[2,1024]{1,0:T(2,128)S(1)} %reshape.1077), channel_id=1, source_target_pairs={{0,3},{1,0},{2,1},{3,2},{4,7},{5,4},{6,5},{7,6},{8,11},{9,8},{10,9... | collective-permute-start | bytes 24584 | tf_op jit(solution)/shard_map/ppermute | solution.py:24
  14.6 60.1 %while.67 = (s32[]{:T(128)}, f32[3,80,64]{1,2,0:T(8,128)S(1)}, s32[12,16]{1,0:T(8,128)S(1)}, f32[2,80,64]{1,2,0:T(8,128)S(1)}, s32[12,16]{1,0:T(8,128)S(1)}, /*i...) while((s32[]{:T(128)}, f32[3,80,64]{1,2,0:T(8,128)S(1)}, ...), condition=%wide.region_7.8_spmd.clone, body=%wide.region_4.7_spmd.clone.sunk | while | flops 17876564 | bytes 2778051 | solution.py:148
  17.0 1.1 fusion.309
  22.0 1.1 fusion.309
  27.0 1.1 fusion.309
  32.0 1.1 fusion.309
  37.0 1.1 fusion.309
  42.0 1.1 fusion.309
  47.0 1.1 fusion.309
  52.0 1.1 fusion.309
  57.1 1.1 fusion.309
  62.1 1.1 fusion.309
  67.1 1.1 fusion.309
  72.1 1.1 fusion.309
  75.6 6.4 %collective-permute-done.2 = f32[3,1024]{1,0:T(4,128)S(1)} collective-permute-done((f32[3,1024]{1,0:T(4,128)S(1)}, f32[3,1024]{1,0:T(4,128)S(1)}, u32[]{:S(2)}, u32[]{:S(2)}) %collective-permute-start.2) | collective-permute-done | bytes 12320 | tf_op jit(solution)/shard_map/ppermute | solution.py:24
  82.8 1.4 collective-permute-done.3
  84.6 60.1 %while.68 = (s32[]{:T(128)}, f32[3,80,64]{1,2,0:T(8,128)S(1)}, s32[12,16]{1,0:T(8,128)S(1)}, f32[2,80,64]{1,2,0:T(8,128)S(1)}, s32[12,16]{1,0:T(8,128)S(1)}, /*i...) while((s32[]{:T(128)}, f32[3,80,64]{1,2,0:T(8,128)S(1)}, ...), condition=%wide.region_11.12_spmd.clone, body=%wide.region_8.11_spmd.clone.sunk | while | flops 17876564 | bytes 2778051 | solution.py:148
  107.1 1.1 fusion.325
  112.1 1.1 fusion.325
  127.1 1.1 fusion.325
  132.1 1.1 fusion.325
  145.5 6.5 %collective-permute-done.4 = f32[3,1024]{1,0:T(4,128)S(1)} collective-permute-done((f32[3,1024]{1,0:T(4,128)S(1)}, f32[3,1024]{1,0:T(4,128)S(1)}, u32[]{:S(2)}, u32[]{:S(2)}) %collective-permute-start.4) | collective-permute-done | bytes 12320 | tf_op jit(solution)/shard_map/ppermute | solution.py:24
  153.0 1.4 collective-permute-done.5
  154.8 60.1 %while.69 = (s32[]{:T(128)}, f32[3,80,64]{1,2,0:T(8,128)S(1)}, s32[12,16]{1,0:T(8,128)S(1)}, f32[2,80,64]{1,2,0:T(8,128)S(1)}, s32[12,16]{1,0:T(8,128)S(1)}, /*i...) while((s32[]{:T(128)}, f32[3,80,64]{1,2,0:T(8,128)S(1)}, ...), condition=%wide.region_15.16_spmd.clone, body=%wide.region_12.15_spmd.clone.sunk | while | flops 17876564 | bytes 2778051 | solution.py:148
  167.3 1.1 fusion.341
  215.8 6.5 %collective-permute-done.6 = f32[3,1024]{1,0:T(4,128)S(1)} collective-permute-done((f32[3,1024]{1,0:T(4,128)S(1)}, f32[3,1024]{1,0:T(4,128)S(1)}, u32[]{:S(2)}, u32[]{:S(2)}) %collective-permute-start.6) | collective-permute-done | bytes 12320 | tf_op jit(solution)/shard_map/ppermute | solution.py:24
  223.2 1.3 collective-permute-done.7
  224.9 60.1 %while.70 = (s32[]{:T(128)}, f32[3,80,64]{1,2,0:T(8,128)S(1)}, s32[12,16]{1,0:T(8,128)S(1)}, f32[2,80,64]{1,2,0:T(8,128)S(1)}, s32[12,16]{1,0:T(8,128)S(1)}, /*i...) while((s32[]{:T(128)}, f32[3,80,64]{1,2,0:T(8,128)S(1)}, ...), condition=%wide.region_19.20_spmd.clone, body=%wide.region_16.19_spmd.clone.sunk | while | flops 17876564 | bytes 2778051 | solution.py:148
  285.9 6.4 %collective-permute-done.8 = f32[3,1024]{1,0:T(4,128)S(1)} collective-permute-done((f32[3,1024]{1,0:T(4,128)S(1)}, f32[3,1024]{1,0:T(4,128)S(1)}, u32[]{:S(2)}, u32[]{:S(2)}) %collective-permute-start.8) | collective-permute-done | bytes 12320 | tf_op jit(solution)/shard_map/ppermute | solution.py:24
  293.1 1.4 collective-permute-done.9
  294.9 77.1 %while.71 = (s32[]{:T(128)}, f32[3,80,64]{1,2,0:T(8,128)S(1)}, f32[]{:T(128)}, s32[12,16]{1,0:T(8,128)S(1)}, f32[2,80,64]{1,2,0:T(8,128)S(1)}, /*index=5*/s32[12...) while((s32[]{:T(128)}, f32[3,80,64]{1,2,0:T(8,128)S(1)}, ...), condition=%wide.region_24.25_spmd.clone, body=%wide.region_20.24_spmd.clone.sunk | while | flops 18283088 | bytes 2786427 | solution.py:148
  297.4 1.8 select_reduce_fusion.4
  303.8 1.8 select_reduce_fusion.4
  310.2 1.8 select_reduce_fusion.4
  316.7 1.8 select_reduce_fusion.4
  323.1 1.8 select_reduce_fusion.4
  329.5 1.8 select_reduce_fusion.4
  335.9 1.8 select_reduce_fusion.4
  342.4 1.8 select_reduce_fusion.4
  348.8 1.8 select_reduce_fusion.4
  355.2 1.8 select_reduce_fusion.4
  361.6 1.8 select_reduce_fusion.4
  368.0 1.8 select_reduce_fusion.4
  373.0 6.5 %collective-permute-done.10 = f32[3,1024]{1,0:T(4,128)S(1)} collective-permute-done((f32[3,1024]{1,0:T(4,128)S(1)}, f32[3,1024]{1,0:T(4,128)S(1)}, u32[]{:S(2)}, u32[]{:S(2)}) %collective-permute-start.10) | collective-permute-done | bytes 12320 | tf_op jit(solution)/shard_map/ppermute | solution.py:24
  380.9 9.3 %all-to-all-start = ((f32[64,1,384]{2,1,0:T(1,128)}), f32[64,1,384]{2,1,0:T(1,128)S(1)}, u32[]{:S(2)}, u32[]{:S(2)}) async-start(f32[64,1,384]{2,1,0:T(1,128)} %reshape.1170), calls=%async_computation | async-start | bytes 196608 | tf_op jit(solution)/shard_map/all_to_all | solution.py:44
  390.2 10.2 %all-to-all-done = f32[64,1,384]{2,1,0:T(1,128)S(1)} async-done(((f32[64,1,384]{2,1,0:T(1,128)}), f32[64,1,384]{2,1,0:T(1,128)S(1)}, u32[]{:S(2)}, u32[]{:S(2)}) %all-to-all-start) | async-done | bytes 98336 | tf_op jit(solution)/shard_map/all_to_all | solution.py:44
  403.5 4.6 %all-to-all-start.1 = ((f32[64,1,384]{2,1,0:T(1,128)}), f32[64,1,384]{2,1,0:T(1,128)S(1)}, u32[]{:S(2)}, u32[]{:S(2)}) async-start(f32[64,1,384]{2,1,0:T(1,128)} %reshape.1172), calls=%async_computation.1 | async-start | bytes 196608 | tf_op jit(solution)/shard_map/all_to_all | solution.py:46
  408.1 11.0 %psum.7 = f32[]{:T(128)} all-reduce(f32[]{:T(128)} %get-tuple-element.598), channel_id=1, replica_groups=mesh['rep'=64,'slab'=4] {'slab'}, use_global_device_ids=true, to_apply=%region_25.26 | all-reduce | flops 1 | bytes 8 | tf_op jit(solution)/shard_map/psum | solution.py:163
  (1013 shorter events, 289.5 us)
Async XLA Ops:
  3.1 10.2 %collective-permute-start = (f32[2,1024]{1,0:T(2,128)S(1)}, f32[2,1024]{1,0:T(2,128)S(1)}, u32[]{:S(2)}, u32[]{:S(2)}) collective-permute-start(f32[2,1024]{1,0:T(2,128)S(1)} %reshape.1077), channel_id=1, source_target_pairs={{0,3},{1,0},{2,1},{3,2},{4,7},{5,4},{6,5},{7,6},{8,11},{9,8},{10,9... | collective-permute-start | bytes 24584 | tf_op jit(solution)/shard_map/ppermute | solution.py:24
  10.1 3.5 collective-permute-start.1
  14.5 60.5 %copy-start.2 = (f32[4096]{0:T(1024)S(1)}, f32[4096]{0:T(1024)}, u32[]{:S(2)}) copy-start(f32[4096]{0:T(1024)} %param.23) | copy-start | bytes 49156
  14.5 60.7 %copy-start.1 = (f32[1,3,4096]{2,0,1:T(1,128)S(1)}, f32[1,3,4096]{2,0,1:T(1,128)}, u32[]{:S(2)}) copy-start(f32[1,3,4096]{2,0,1:T(1,128)} %param.22) | copy-start | bytes 147460
  14.5 67.6 %copy-start = (s32[1,16]{1,0:T(1,128)S(1)}, s32[1,16]{1,0:T(1,128)}, u32[]{:S(2)}) copy-start(s32[1,16]{1,0:T(1,128)} %param.29) | copy-start | bytes 196
  74.7 9.6 %copy-start.3 = (f32[3]{0:T(128)S(1)}, f32[3]{0:T(128)}, u32[]{:S(2)}) copy-start(f32[3]{0:T(128)} %constant.242.clone) | copy-start | bytes 40
  74.9 7.1 %collective-permute-start.2 = (f32[3,1024]{1,0:T(4,128)S(1)}, f32[3,1024]{1,0:T(4,128)S(1)}, u32[]{:S(2)}, u32[]{:S(2)}) collective-permute-start(f32[3,1024]{1,0:T(4,128)S(1)} %reshape.1083), channel_id=1, source_target_pairs={{0,1},{1,2},{2,3},{3,0},{4,5},{5,6},{6,7},{7,4},{8,9},{9,10},{10,1... | collective-permute-start | bytes 36872 | tf_op jit(solution)/shard_map/ppermute | solution.py:24
  82.8 1.5 collective-permute-start.3
  145.0 7.1 %collective-permute-start.4 = (f32[3,1024]{1,0:T(4,128)S(1)}, f32[3,1024]{1,0:T(4,128)S(1)}, u32[]{:S(2)}, u32[]{:S(2)}) collective-permute-start(f32[3,1024]{1,0:T(4,128)S(1)} %reshape.1087), channel_id=1, source_target_pairs={{0,1},{1,2},{2,3},{3,0},{4,5},{5,6},{6,7},{7,4},{8,9},{9,10},{10,1... | collective-permute-start | bytes 36872 | tf_op jit(solution)/shard_map/ppermute | solution.py:24
  152.8 1.7 collective-permute-start.5
  154.8 60.9 %copy-start.4 = (s32[16,2]{0,1:T(2,128)S(1)}, s32[16,2]{0,1:T(2,128)}, u32[]{:S(2)}) copy-start(s32[16,2]{0,1:T(2,128)} %param.30) | copy-start | bytes 388
  215.2 7.1 %collective-permute-start.6 = (f32[3,1024]{1,0:T(4,128)S(1)}, f32[3,1024]{1,0:T(4,128)S(1)}, u32[]{:S(2)}, u32[]{:S(2)}) collective-permute-start(f32[3,1024]{1,0:T(4,128)S(1)} %reshape.1091), channel_id=1, source_target_pairs={{0,1},{1,2},{2,3},{3,0},{4,5},{5,6},{6,7},{7,4},{8,9},{9,10},{10,1... | collective-permute-start | bytes 36872 | tf_op jit(solution)/shard_map/ppermute | solution.py:24
  223.0 1.5 collective-permute-start.7
  285.2 7.1 %collective-permute-start.8 = (f32[3,1024]{1,0:T(4,128)S(1)}, f32[3,1024]{1,0:T(4,128)S(1)}, u32[]{:S(2)}, u32[]{:S(2)}) collective-permute-start(f32[3,1024]{1,0:T(4,128)S(1)} %reshape.1095), channel_id=1, source_target_pairs={{0,1},{1,2},{2,3},{3,0},{4,5},{5,6},{6,7},{7,4},{8,9},{9,10},{10,1... | collective-permute-start | bytes 36872 | tf_op jit(solution)/shard_map/ppermute | solution.py:24
  293.1 1.5 collective-permute-start.9
  372.2 7.3 %collective-permute-start.10 = (f32[3,1024]{1,0:T(4,128)S(1)}, f32[3,1024]{1,0:T(4,128)S(1)}, u32[]{:S(2)}, u32[]{:S(2)}) collective-permute-start(f32[3,1024]{1,0:T(4,128)S(1)} %reshape.1099), channel_id=1, source_target_pairs={{0,1},{1,2},{2,3},{3,0},{4,5},{5,6},{6,7},{7,4},{8,9},{9,10},{10,1... | collective-permute-start | bytes 36872 | tf_op jit(solution)/shard_map/ppermute | solution.py:24
  380.9 19.5 %all-to-all-start = ((f32[64,1,384]{2,1,0:T(1,128)}), f32[64,1,384]{2,1,0:T(1,128)S(1)}, u32[]{:S(2)}, u32[]{:S(2)}) async-start(f32[64,1,384]{2,1,0:T(1,128)} %reshape.1170), calls=%async_computation | async-start | bytes 196608 | tf_op jit(solution)/shard_map/all_to_all | solution.py:44
  403.5 16.3 %all-to-all-start.1 = ((f32[64,1,384]{2,1,0:T(1,128)}), f32[64,1,384]{2,1,0:T(1,128)S(1)}, u32[]{:S(2)}, u32[]{:S(2)}) async-start(f32[64,1,384]{2,1,0:T(1,128)} %reshape.1172), calls=%async_computation.1 | async-start | bytes 196608 | tf_op jit(solution)/shard_map/all_to_all | solution.py:46

commit v2 on v1

--- a/solution.py
+++ b/solution.py
@@ -2,12 +2,15 @@
 import jax.numpy as jnp
 from jax import lax
 from jax.sharding import PartitionSpec as P
+from jax.experimental import pallas as pl
+from jax.experimental.pallas import tpu as pltpu
 
 CL = 64
 CD = 64
 STEPS = 4
 HALO = 16
 NT_MAX = 192
+HALF = CL // 2
 
 
 tile_block = 16
@@ -16,6 +19,78 @@
 soft_sq = 0.25
 slab_width = 2.0
 exact = lax.Precision.HIGHEST
+
+
+def pair_kernel(tiles_ref, count_ref, xcol_ref, xrow_ref, pcol_ref, prow_ref, wsame_ref,
+                fcol_ref, frow_ref, en_ref):
+    fcol_ref[...] = jnp.zeros(fcol_ref.shape, jnp.float32)
+    frow_ref[...] = jnp.zeros(frow_ref.shape, jnp.float32)
+
+    def body(t, acc):
+        i = tiles_ref[0, t]
+        j = tiles_ref[1, t]
+        dx = xcol_ref[0, i] - xrow_ref[0, j]
+        dy = xcol_ref[1, i] - xrow_ref[1, j]
+        dz = xcol_ref[2, i] - xrow_ref[2, j]
+        sq = dx * dx + dy * dy + dz * dz
+        gauss = pcol_ref[0, i] * prow_ref[0, j] * jnp.exp(-sq)
+        inv_root = lax.rsqrt(sq + soft_sq)
+        coulomb = pcol_ref[1, i] * prow_ref[1, j] * inv_root
+        same = i == j
+        w_force = jnp.where(same, 0.5, 1.0).astype(jnp.float32)
+        w_energy = jnp.where(same, wsame_ref[...], 1.0)
+        slope = w_force * (2.0 * gauss + coulomb * inv_root * inv_root)
+        px = slope * dx
+        py = slope * dy
+        pz = slope * dz
+        fcol_ref[0, i] += px
+        fcol_ref[1, i] += py
+        fcol_ref[2, i] += pz
+        frow_ref[0, j] -= jnp.sum(px, axis=0, keepdims=True)
+        frow_ref[1, j] -= jnp.sum(py, axis=0, keepdims=True)
+        frow_ref[2, j] -= jnp.sum(pz, axis=0, keepdims=True)
+        return acc + w_energy * (gauss + coulomb)
+
+    acc = lax.fori_loop(0, count_ref[0], body, jnp.zeros((HALF, 2 * CL), jnp.float32))
+    en_ref[...] = acc
+
+
+def self_weights():
+    rows = lax.broadcasted_iota(jnp.int32, (HALF, 2 * CL), 0)
+    lanes = lax.broadcasted_iota(jnp.int32, (HALF, 2 * CL), 1)
+    return jnp.where(2 * rows + lanes // CL == lanes % CL, 0.0, 0.5).astype(jnp.float32)
+
+
+def as_columns(values):
+    lead = values.shape[:-1]
+    return jnp.repeat(values.reshape(lead + (HALF, 2)), CL, axis=-1)
+
+
+def as_rows(values):
+    lead = values.shape[:-1]
+    return jnp.concatenate([values, values], -1).reshape(lead + (1, 2 * CL))
+
+
+def slab_pairs(extended, pcol, prow, tiles, count):
+    width = extended.shape[1]
+    xcol = as_columns(extended)
+    xrow = as_rows(extended)
+    smem = pl.BlockSpec(memory_space=pltpu.SMEM)
+    vmem = pl.BlockSpec(memory_space=pltpu.VMEM)
+    fcol, frow, acc = pl.pallas_call(
+        pair_kernel,
+        out_shape=(
+            jax.ShapeDtypeStruct((3, width, HALF, 2 * CL), jnp.float32),
+            jax.ShapeDtypeStruct((3, width, 1, 2 * CL), jnp.float32),
+            jax.ShapeDtypeStruct((HALF, 2 * CL), jnp.float32),
+        ),
+        in_specs=[smem, smem, vmem, vmem, vmem, vmem, vmem],
+        out_specs=(vmem, vmem, vmem),
+        compiler_params=pltpu.CompilerParams(vmem_limit_bytes=48 * 1024 * 1024),
+    )(tiles, count.reshape(1), xcol, xrow, pcol, prow, self_weights())
+    f_i = fcol.reshape(3, width, HALF, 2, CL).sum(-1).reshape(3, width, CL)
+    f_j = frow.reshape(3, width, 2, CL).sum(2)
+    return f_i + f_j, jnp.sum(acc)
 
 
 def from_behind(value, axis, steps):
@@ -116,19 +191,9 @@
     strength_all = jnp.concatenate([params[0], got_params[0]], 0)
     charge_all = jnp.concatenate([params[1], got_params[1]], 0)
     lift = jnp.array([0.0, 0.0, slab_width], jnp.float32)[:, None]
-    extended_now = [None]
-
-    def add_block(totals, tile_first, tile_second, slot_row):
-        spread, energy_part = pair_block(
-            extended_now[0],
-            strength_all,
-            charge_all,
-            ham_scale,
-            tile_first,
-            tile_second,
-            slot_row < live_count,
-        )
-        return (totals[0] + spread, totals[1] + energy_part)
+    param_cols = jnp.stack([as_columns(strength_all), as_columns(ham_scale * charge_all)], 0)
+    param_rows = jnp.stack([as_rows(strength_all), as_rows(charge_all)], 0)
+    tile_list = jnp.stack([firsts_flat, seconds_flat], 0)
 
     def evaluate(coords_now):
         blocks = coords_now.reshape(3, CD, CL)
@@ -136,17 +201,8 @@
             3, HALO * CL
         )
         from_above = from_behind(sent_coords, "slab", -1) + lift
-        extended_now[0] = jnp.concatenate([blocks, from_above.reshape(3, HALO, CL)], 1)
-        start_state = (jnp.zeros((3, CD + HALO, CL), jnp.float32), jnp.zeros((), jnp.float32))
-        firsts = firsts_flat.reshape(-1, tile_block)
-        seconds = seconds_flat.reshape(-1, tile_block)
-        slot_ids = jnp.arange(NT_MAX, dtype=jnp.int32).reshape(-1, tile_block)
-
-        def visit_block(totals, inputs):
-            return (add_block(totals, inputs[0], inputs[1], inputs[2]), None)
-
-        result, _ = lax.scan(visit_block, start_state, (firsts, seconds, slot_ids))
-        forces, energy = result
+        extended = jnp.concatenate([blocks, from_above.reshape(3, HALO, CL)], 1)
+        forces, energy = slab_pairs(extended, param_cols, param_rows, tile_list, live_count)
         returned = from_behind(forces[:, CD:].reshape(3, HALO * CL), "slab", 1)
         back_home = jnp.einsum(
             "hc,xhk->xck", halo_table, returned.reshape(3, HALO, CL), precision=exact
@@ -154,12 +210,18 @@
         local_forces = forces[:, :CD] + back_home
         return (local_forces.reshape(3, atoms_here), energy)
 
-    forces, energy = evaluate(coords)
-    for step_idx in range(STEPS):
+    def verlet_step(step_idx, carry):
+        coords, speeds, forces, energy = carry
         speeds = speeds + half_step * forces * inv_mass
         coords = coords + time_step * speeds
         forces, energy = evaluate(coords)
         speeds = speeds + half_step * forces * inv_mass
+        return (coords, speeds, forces, energy)
+
+    forces, energy = evaluate(coords)
+    coords, speeds, forces, energy = lax.fori_loop(
+        0, STEPS, verlet_step, (coords, speeds, forces, energy)
+    )
     total_energy = lax.psum(energy, "slab")
     potential = (total_energy / (atoms_here * lax.axis_size("slab"))).reshape(1)
     state = jnp.concatenate([coords, speeds], 0)

time: 427 us -> 363 us (0.85)
  other arithmetic: 204 us -> 67.2 us
  local copies, waits for them, and re-layouts: 36.2 us -> 158 us
  matrix products: 85.8 us -> 4.31 us
  Pallas kernels: 0 us -> 29.6 us
  loops' own time: 13.2 us -> 0.6 us
  starting transfers between devices: 22.4 us -> 34.3 us
    mul x109 -> x10, other arithmetic: 91.2 us -> 2.98 us  [the longest x4 2.88 us: verlet_step(): speeds = speeds + half_step * forces * inv_mass]
    dot_general x360 -> x0, matrix products: 81.7 us -> none  [the longest x60 18 us: pair_block(): jnp.einsum('te,xtc->xec', select_second, force_j, precision=exact)]
    reduce_sum x72 -> x15, other arithmetic: 77.6 us -> 23.9 us  [the longest x5 20.8 us: slab_pairs(): f_i = fcol.reshape(3, width, HALF, 2, CL).sum(-1).reshape(3, width, CL)]
    concatenate x0 -> x22, local copies, waits for them, and re-layouts: none -> 47.1 us  [the longest x15 41.5 us: evaluate(): extended = jnp.concatenate([blocks, from_above.reshape(3, HALO, CL)], 1)]
    reshape x9 -> x21, local copies, waits for them, and re-layouts: 0.79 us -> 35.4 us  [the longest x5 30.7 us: as_columns(): return jnp.repeat(values.reshape(lead + (HALF, 2)), CL, axis=-1)]
    pallas_call x0 -> x10, local copies, waits for them, and re-layouts: none -> 30.7 us  [slab_pairs(): pl.pallas_call(pair_kernel, out_shape=(jax.ShapeDtypeStruct((3, width, HA...]
    pallas_call x0 -> x5, Pallas kernels: none -> 29.6 us  [slab_pairs(): pl.pallas_call(pair_kernel, out_shape=(jax.ShapeDtypeStruct((3, width, HA...]
    sub x60 -> x0, other arithmetic: 29.5 us -> none  [pair_block(): coords_i[:, :, :, None] - coords_j[:, None, :, :]]
  transfers between devices with their start and end apart: 13 -> 13, of which waited for: 10 -> 6; matrix products, arithmetic and copies ran while one was open for 1% -> 12% of each run, Pallas kernels for 0% -> 0%
where the time goes in v2:
time: 363 us; the launch traced here: 358 us
  local copies, waits for them, and re-layouts  158 us (44%)
  other arithmetic  67.2 us (19%)
  waiting for transfers between devices  49.8 us (14%)
  starting transfers between devices  34.3 us (9%)
  Pallas kernels  29.6 us (8%)
  blocking collectives  10.5 us (3%)
  matrix products  4.31 us (1%)
  between operations  4.09 us (1%)
    concatenate x15, local copies, waits for them, and re-layouts, evaluate(): extended = jnp.concatenate([blocks, from_above.reshape(3, HALO, CL)], 1)  41.5 us
    ppermute x11, waiting for transfers between devices, from_behind(): return lax.ppermute(value, axis, pairs)  40.3 us
    pallas_call x10, local copies, waits for them, and re-layouts, slab_pairs(): pl.pallas_call(pair_kernel, out_shape=(jax.ShapeDtypeStruct((3, width, HA...  30.7 us
    reshape x5, local copies, waits for them, and re-layouts, as_columns(): return jnp.repeat(values.reshape(lead + (HALF, 2)), CL, axis=-1)  30.7 us
    pallas_call x5, Pallas kernels, slab_pairs(): pl.pallas_call(pair_kernel, out_shape=(jax.ShapeDtypeStruct((3, width, HA...  29.6 us
    all_to_all x1, starting transfers between devices, exchange(): spread = lax.all_to_all(chunks, 'rep', 0, 0, tiled=True)  21.5 us
    reduce_sum x5, other arithmetic, slab_pairs(): f_i = fcol.reshape(3, width, HALF, 2, CL).sum(-1).reshape(3, width, CL)  20.8 us
    concatenate x5, other arithmetic, evaluate(): extended = jnp.concatenate([blocks, from_above.reshape(3, HALO, CL)], 1)  18.6 us
  transfers between devices with their start and end apart: 13, of which 6 were waited for; matrix products, arithmetic and copies ran while one was open for 12% of the time, Pallas kernels for 0%

profile of v2, /device:TPU:0, one launch (start us, length us, event | category | flops | bytes accessed | tf_op | source)
XLA Modules:
  0.0 358.2 jit_solution(12700034912988614687)
XLA Ops:
  3.1 4.9 %collective-permute-start.3 = (f32[2,1024]{1,0:T(2,128)S(1)}, f32[2,1024]{1,0:T(2,128)S(1)}, u32[]{:S(2)}, u32[]{:S(2)}) collective-permute-start(f32[2,1024]{1,0:T(2,128)S(1)} %reshape.210), channel_id=1, source_target_pairs={{0,3},{1,0},{2,1},{3,2},{4,7},{5,4},{6,5},{7,6},{8,11},{9,8},{10,9... | collective-permute-start | bytes 24584 | tf_op jit(solution)/shard_map/ppermute | solution.py:99
  18.6 4.9 %concatenate.65 = f32[3,64,32,2]{3,2,1,0:T(8,128)} reshape(f32[3,4096]{1,0:T(4,128)S(1)} %reduce) | data formatting | bytes 98304 | tf_op jit(solution)/shard_map/concatenate | solution.py:204
  36.1 4.6 %pad_maximum_fusion.1 = f32[3,80,32,2]{3,2,1,0:T(8,128)} fusion(f32[3,16,32,2]{3,2,1,0:T(8,128)} %concatenate.66, f32[3,64,32,2]{3,2,1,0:T(8,128)} %concatenate.65), kind=kLoop, calls=%fused_computation.32 | loop fusion | flops 15360 | bytes 122880 | tf_op jit(solution)/shard_map/concatenate | solution.py:204
  40.7 3.1 copy.86
  46.9 6.0 %copy.93.xcol_ref = f32[3,80,32,128]{3,2,1,0:T(8,128)} copy(f32[3,80,32,128]{1,3,2,0:T(8,128)} %bitcast.109) | data formatting | bytes 7864320 | tf_op jit(solution)/shard_map/reshape | solution.py:66
  52.9 5.5 %shard_map.130 = (f32[3,80,32,128]{3,2,1,0:T(8,128)S(1)}, f32[3,80,1,128]{3,2,1,0:T(1,128)S(1)}, f32[32,128]{1,0:T(8,128)S(1)}) custom-call(s32[2,192]{1,0:T(2,128)S(1)} %pad_add_fusion.tiles_ref, s32[1]{0:T(128)} %bitcast.105.count_ref, f32[3,80,32,128]{3,2,1,0:T(8,128)} %copy.93.xcol_ref, f32[3,80,1,128]{3,2,1,0:T(1,128)S(1)} %bitcast.107, ...), custom_call_target="tpu_custom_call" | custom-call | tf_op jit(solution)/shard_map/pallas_call | solution.py:80
  60.4 6.0 %copy.94 = f32[3,80,32,128]{1,3,2,0:T(8,128)} copy(f32[3,80,32,128]{3,2,1,0:T(8,128)} %copy-done.1) | data formatting | bytes 7864320 | tf_op jit(solution)/shard_map/pallas_call | solution.py:80
  66.4 4.2 %bitcast_reduce_fusion.1 = f32[3,80,32,2]{1,3,2,0:T(2,128)S(1)} fusion(f32[3,80,32,128]{1,3,2,0:T(8,128)} %copy.94), kind=kLoop, calls=%fused_computation.31 | loop fusion | flops 967680 | bytes 3993600 | tf_op jit(solution)/shard_map/reduce_sum | solution.py:91
  72.3 5.9 %collective-permute-done.4 = f32[3,1024]{1,0:T(4,128)S(1)} collective-permute-done((f32[3,1024]{1,0:T(4,128)S(1)}, f32[3,1024]{1,0:T(4,128)S(1)}, u32[]{:S(2)}, u32[]{:S(2)}) %collective-permute-start.4) | collective-permute-done | bytes 12320 | tf_op jit(solution)/shard_map/ppermute | solution.py:99
  79.3 223.7 %while.19 = (s32[]{:T(128)}, f32[3,4096]{1,0:T(4,128)S(1)}, f32[3,4096]{1,0:T(4,128)S(1)}, f32[3,4096]{1,0:T(4,128)}, f32[]{:T(128)}, /*index=5*/f32[4096]{0:T(1...) while((s32[]{:T(128)}, f32[3,4096]{1,0:T(4,128)S(1)}, ...), condition=%wide.region_11.12_spmd.clone, body=%wide.region_7.11_spmd.clone.sunk | while | flops 5972641 | bytes 62915776 | solution.py:222
  81.6 3.2 concatenate.89
  88.9 3.5 pad_maximum_fusion.7
  92.4 3.1 copy.115
  98.5 6.2 %copy.116.xcol_ref = f32[3,80,32,128]{3,2,1,0:T(8,128)} copy(f32[3,80,32,128]{1,3,2,0:T(8,128)} %bitcast.108) | data formatting | bytes 7864320 | tf_op jit(solution)/shard_map/while/body/eval_jaxpr/reshape | solution.py:66
  104.7 6.0 %eval_jaxpr.4 = (f32[3,80,32,128]{3,2,1,0:T(8,128)S(1)}, f32[3,80,1,128]{3,2,1,0:T(1,128)S(1)}, f32[32,128]{1,0:T(8,128)S(1)}) custom-call(s32[2,192]{1,0:T(2,128)S(1)} %get-tuple-element.367.tiles_ref, s32[1]{0:T(128)} %bitcast.99.count_ref, f32[3,80,32,128]{3,2,1,0:T(8,128)} %copy.116.xcol_ref, f32[3,80,1,128]{3,2,1,0:T(1,128)S(1)} %bitcast.106, ...), custom_call_target="tpu_custom_call" | custom-call | tf_op jit(solution)/shard_map/while/body/eval_jaxpr/pallas_call | solution.py:80
  112.7 6.0 %copy.117 = f32[3,80,32,128]{1,3,2,0:T(8,128)} copy(f32[3,80,32,128]{3,2,1,0:T(8,128)} %copy-done) | data formatting | bytes 7864320 | tf_op jit(solution)/shard_map/while/body/eval_jaxpr/pallas_call | solution.py:80
  118.7 4.2 %bitcast_reduce_fusion.3 = f32[3,80,32,2]{1,3,2,0:T(2,128)S(1)} fusion(f32[3,80,32,128]{1,3,2,0:T(8,128)} %copy.117), kind=kLoop, calls=%fused_computation.3.clone.1 | loop fusion | flops 967680 | bytes 3993600 | tf_op jit(solution)/shard_map/while/body/eval_jaxpr/reduce_sum | solution.py:91
  124.5 8.6 %collective-permute-done.1 = f32[3,1024]{1,0:T(4,128)S(1)} collective-permute-done((f32[3,1024]{1,0:T(4,128)S(1)}, f32[3,1024]{1,0:T(4,128)S(1)}, u32[]{:S(2)}, u32[]{:S(2)}) %collective-permute-start.1) | collective-permute-done | bytes 12320 | tf_op jit(solution)/shard_map/while/body/eval_jaxpr/ppermute | solution.py:99
  137.5 3.2 concatenate.89
  144.8 3.5 pad_maximum_fusion.7
  148.3 3.1 copy.115
  151.4 3.1 broadcast_in_dim.102
  154.4 6.2 %copy.116.xcol_ref = f32[3,80,32,128]{3,2,1,0:T(8,128)} copy(f32[3,80,32,128]{1,3,2,0:T(8,128)} %bitcast.108) | data formatting | bytes 7864320 | tf_op jit(solution)/shard_map/while/body/eval_jaxpr/reshape | solution.py:66
  160.6 6.0 %eval_jaxpr.4 = (f32[3,80,32,128]{3,2,1,0:T(8,128)S(1)}, f32[3,80,1,128]{3,2,1,0:T(1,128)S(1)}, f32[32,128]{1,0:T(8,128)S(1)}) custom-call(s32[2,192]{1,0:T(2,128)S(1)} %get-tuple-element.367.tiles_ref, s32[1]{0:T(128)} %bitcast.99.count_ref, f32[3,80,32,128]{3,2,1,0:T(8,128)} %copy.116.xcol_ref, f32[3,80,1,128]{3,2,1,0:T(1,128)S(1)} %bitcast.106, ...), custom_call_target="tpu_custom_call" | custom-call | tf_op jit(solution)/shard_map/while/body/eval_jaxpr/pallas_call | solution.py:80
  168.6 6.0 %copy.117 = f32[3,80,32,128]{1,3,2,0:T(8,128)} copy(f32[3,80,32,128]{3,2,1,0:T(8,128)} %copy-done) | data formatting | bytes 7864320 | tf_op jit(solution)/shard_map/while/body/eval_jaxpr/pallas_call | solution.py:80
  174.6 4.2 %bitcast_reduce_fusion.3 = f32[3,80,32,2]{1,3,2,0:T(2,128)S(1)} fusion(f32[3,80,32,128]{1,3,2,0:T(8,128)} %copy.117), kind=kLoop, calls=%fused_computation.3.clone.1 | loop fusion | flops 967680 | bytes 3993600 | tf_op jit(solution)/shard_map/while/body/eval_jaxpr/reduce_sum | solution.py:91
  180.4 8.6 %collective-permute-done.1 = f32[3,1024]{1,0:T(4,128)S(1)} collective-permute-done((f32[3,1024]{1,0:T(4,128)S(1)}, f32[3,1024]{1,0:T(4,128)S(1)}, u32[]{:S(2)}, u32[]{:S(2)}) %collective-permute-start.1) | collective-permute-done | bytes 12320 | tf_op jit(solution)/shard_map/while/body/eval_jaxpr/ppermute | solution.py:99
  193.5 3.2 concatenate.89
  200.7 3.5 pad_maximum_fusion.7
  204.2 3.1 copy.115
  207.3 3.1 broadcast_in_dim.102
  210.4 6.2 %copy.116.xcol_ref = f32[3,80,32,128]{3,2,1,0:T(8,128)} copy(f32[3,80,32,128]{1,3,2,0:T(8,128)} %bitcast.108) | data formatting | bytes 7864320 | tf_op jit(solution)/shard_map/while/body/eval_jaxpr/reshape | solution.py:66
  216.5 6.0 %eval_jaxpr.4 = (f32[3,80,32,128]{3,2,1,0:T(8,128)S(1)}, f32[3,80,1,128]{3,2,1,0:T(1,128)S(1)}, f32[32,128]{1,0:T(8,128)S(1)}) custom-call(s32[2,192]{1,0:T(2,128)S(1)} %get-tuple-element.367.tiles_ref, s32[1]{0:T(128)} %bitcast.99.count_ref, f32[3,80,32,128]{3,2,1,0:T(8,128)} %copy.116.xcol_ref, f32[3,80,1,128]{3,2,1,0:T(1,128)S(1)} %bitcast.106, ...), custom_call_target="tpu_custom_call" | custom-call | tf_op jit(solution)/shard_map/while/body/eval_jaxpr/pallas_call | solution.py:80
  224.5 6.0 %copy.117 = f32[3,80,32,128]{1,3,2,0:T(8,128)} copy(f32[3,80,32,128]{3,2,1,0:T(8,128)} %copy-done) | data formatting | bytes 7864320 | tf_op jit(solution)/shard_map/while/body/eval_jaxpr/pallas_call | solution.py:80
  230.5 4.2 %bitcast_reduce_fusion.3 = f32[3,80,32,2]{1,3,2,0:T(2,128)S(1)} fusion(f32[3,80,32,128]{1,3,2,0:T(8,128)} %copy.117), kind=kLoop, calls=%fused_computation.3.clone.1 | loop fusion | flops 967680 | bytes 3993600 | tf_op jit(solution)/shard_map/while/body/eval_jaxpr/reduce_sum | solution.py:91
  236.3 8.6 %collective-permute-done.1 = f32[3,1024]{1,0:T(4,128)S(1)} collective-permute-done((f32[3,1024]{1,0:T(4,128)S(1)}, f32[3,1024]{1,0:T(4,128)S(1)}, u32[]{:S(2)}, u32[]{:S(2)}) %collective-permute-start.1) | collective-permute-done | bytes 12320 | tf_op jit(solution)/shard_map/while/body/eval_jaxpr/ppermute | solution.py:99
  249.4 3.2 concatenate.89
  256.6 3.5 pad_maximum_fusion.7
  260.1 3.1 copy.115
  266.3 6.2 %copy.116.xcol_ref = f32[3,80,32,128]{3,2,1,0:T(8,128)} copy(f32[3,80,32,128]{1,3,2,0:T(8,128)} %bitcast.108) | data formatting | bytes 7864320 | tf_op jit(solution)/shard_map/while/body/eval_jaxpr/reshape | solution.py:66
  272.4 6.0 %eval_jaxpr.4 = (f32[3,80,32,128]{3,2,1,0:T(8,128)S(1)}, f32[3,80,1,128]{3,2,1,0:T(1,128)S(1)}, f32[32,128]{1,0:T(8,128)S(1)}) custom-call(s32[2,192]{1,0:T(2,128)S(1)} %get-tuple-element.367.tiles_ref, s32[1]{0:T(128)} %bitcast.99.count_ref, f32[3,80,32,128]{3,2,1,0:T(8,128)} %copy.116.xcol_ref, f32[3,80,1,128]{3,2,1,0:T(1,128)S(1)} %bitcast.106, ...), custom_call_target="tpu_custom_call" | custom-call | tf_op jit(solution)/shard_map/while/body/eval_jaxpr/pallas_call | solution.py:80
  280.4 6.0 %copy.117 = f32[3,80,32,128]{1,3,2,0:T(8,128)} copy(f32[3,80,32,128]{3,2,1,0:T(8,128)} %copy-done) | data formatting | bytes 7864320 | tf_op jit(solution)/shard_map/while/body/eval_jaxpr/pallas_call | solution.py:80
  286.4 4.2 %bitcast_reduce_fusion.3 = f32[3,80,32,2]{1,3,2,0:T(2,128)S(1)} fusion(f32[3,80,32,128]{1,3,2,0:T(8,128)} %copy.117), kind=kLoop, calls=%fused_computation.3.clone.1 | loop fusion | flops 967680 | bytes 3993600 | tf_op jit(solution)/shard_map/while/body/eval_jaxpr/reduce_sum | solution.py:91
  292.2 8.6 %collective-permute-done.1 = f32[3,1024]{1,0:T(4,128)S(1)} collective-permute-done((f32[3,1024]{1,0:T(4,128)S(1)}, f32[3,1024]{1,0:T(4,128)S(1)}, u32[]{:S(2)}, u32[]{:S(2)}) %collective-permute-start.1) | collective-permute-done | bytes 12320 | tf_op jit(solution)/shard_map/while/body/eval_jaxpr/ppermute | solution.py:99
  304.0 21.5 %all-to-all-start = ((f32[64,1,384]{2,1,0:T(1,128)}), f32[64,1,384]{2,1,0:T(1,128)S(1)}, u32[]{:S(2)}, u32[]{:S(2)}) async-start(f32[64,1,384]{2,1,0:T(1,128)} %reshape.260), calls=%async_computation | async-start | bytes 196608 | tf_op jit(solution)/shard_map/all_to_all | solution.py:119
  326.2 9.6 %all-to-all-done = f32[64,1,384]{2,1,0:T(1,128)S(1)} async-done(((f32[64,1,384]{2,1,0:T(1,128)}), f32[64,1,384]{2,1,0:T(1,128)S(1)}, u32[]{:S(2)}, u32[]{:S(2)}) %all-to-all-start) | async-done | bytes 98336 | tf_op jit(solution)/shard_map/all_to_all | solution.py:119
  338.8 4.6 %all-to-all-start.1 = ((f32[64,1,384]{2,1,0:T(1,128)}), f32[64,1,384]{2,1,0:T(1,128)S(1)}, u32[]{:S(2)}, u32[]{:S(2)}) async-start(f32[64,1,384]{2,1,0:T(1,128)} %reshape.262), calls=%async_computation.1 | async-start | bytes 196608 | tf_op jit(solution)/shard_map/all_to_all | solution.py:121
  343.4 10.5 %psum.7 = f32[]{:T(128)} all-reduce(f32[]{:T(128)} %get-tuple-element.161), channel_id=1, replica_groups=mesh['rep'=64,'slab'=4] {'slab'}, use_global_device_ids=true, to_apply=%region_12.13 | all-reduce | flops 1 | bytes 8 | tf_op jit(solution)/shard_map/psum | solution.py:225
  (243 shorter events, 92.8 us)
Async XLA Ops:
  3.1 22.3 %collective-permute-start.3 = (f32[2,1024]{1,0:T(2,128)S(1)}, f32[2,1024]{1,0:T(2,128)S(1)}, u32[]{:S(2)}, u32[]{:S(2)}) collective-permute-start(f32[2,1024]{1,0:T(2,128)S(1)} %reshape.210), channel_id=1, source_target_pairs={{0,3},{1,0},{2,1},{3,2},{4,7},{5,4},{6,5},{7,6},{8,11},{9,8},{10,9... | collective-permute-start | bytes 24584 | tf_op jit(solution)/shard_map/ppermute | solution.py:99
  10.1 24.1 %collective-permute-start.2 = (f32[3,1024]{1,0:T(4,128)S(1)}, f32[3,1024]{1,0:T(4,128)S(1)}, u32[]{:S(2)}, u32[]{:S(2)}) collective-permute-start(f32[3,1024]{1,0:T(4,128)S(1)} %reshape.206), channel_id=1, source_target_pairs={{0,3},{1,0},{2,1},{3,2},{4,7},{5,4},{6,5},{7,6},{8,11},{9,8},{10,9... | collective-permute-start | bytes 36872 | tf_op jit(solution)/shard_map/ppermute | solution.py:99
  11.7 14.2 %copy-start.5 = (s32[64]{0:T(128)}, s32[64]{0:T(128)S(1)}, u32[]{:S(2)}) copy-start(s32[64]{0:T(128)S(1)} %get-tuple-element.201) | copy-start | bytes 772
  11.7 14.2 %copy-start.6 = (s32[64]{0:T(128)}, s32[64]{0:T(128)S(1)}, u32[]{:S(2)}) copy-start(s32[64]{0:T(128)S(1)} %get-tuple-element.202) | copy-start | bytes 772
  11.8 14.1 %copy-start.7 = (pred[64]{0:T(512)(128)(4,1)}, pred[64]{0:T(512)(128)(4,1)S(1)}, u32[]{:S(2)}) copy-start(pred[64]{0:T(512)(128)(4,1)S(1)} %get-tuple-element.247) | copy-start | bytes 196
  11.8 14.1 %copy-start.8 = (pred[64]{0:T(512)(128)(4,1)}, pred[64]{0:T(512)(128)(4,1)S(1)}, u32[]{:S(2)}) copy-start(pred[64]{0:T(512)(128)(4,1)S(1)} %get-tuple-element.248) | copy-start | bytes 196
  29.4 4.8 %copy-start.9 = (f32[3]{0:T(128)S(1)}, f32[3]{0:T(128)}, u32[]{:S(2)}) copy-start(f32[3]{0:T(128)} %constant.135.clone) | copy-start | bytes 40
  58.4 1.9 copy-start.1
  66.4 11.8 %copy-start.4 = (s32[1,16]{1,0:T(1,128)S(1)}, s32[1,16]{1,0:T(1,128)}, u32[]{:S(2)}) copy-start(s32[1,16]{1,0:T(1,128)} %param.21) | copy-start | bytes 196
  71.0 7.1 %collective-permute-start.4 = (f32[3,1024]{1,0:T(4,128)S(1)}, f32[3,1024]{1,0:T(4,128)S(1)}, u32[]{:S(2)}, u32[]{:S(2)}) collective-permute-start(f32[3,1024]{1,0:T(4,128)S(1)} %reshape.214), channel_id=1, source_target_pairs={{0,1},{1,2},{2,3},{3,0},{4,5},{5,6},{6,7},{7,4},{8,9},{9,10},{10,1... | collective-permute-start | bytes 36872 | tf_op jit(solution)/shard_map/ppermute | solution.py:99
  79.3 2.2 copy-start.2
  81.4 3.4 collective-permute-start
  98.5 6.2 %copy-start.3 = (f32[2,80,32,128]{3,2,1,0:T(8,128)S(1)}, f32[2,80,32,128]{3,2,1,0:T(8,128)}, u32[]{:S(2)}) copy-start(f32[2,80,32,128]{3,2,1,0:T(8,128)} %copy-done.2) | copy-start | bytes 7864324 | tf_op jit(solution)/shard_map/while
  110.7 1.9 copy-start
  123.3 9.8 %collective-permute-start.1 = (f32[3,1024]{1,0:T(4,128)S(1)}, f32[3,1024]{1,0:T(4,128)S(1)}, u32[]{:S(2)}, u32[]{:S(2)}) collective-permute-start(f32[3,1024]{1,0:T(4,128)S(1)} %reshape.273), channel_id=1, source_target_pairs={{0,1},{1,2},{2,3},{3,0},{4,5},{5,6},{6,7},{7,4},{8,9},{9,10},{10,1... | collective-permute-start | bytes 36872 | tf_op jit(solution)/shard_map/while/body/eval_jaxpr/ppermute | solution.py:99
  135.2 2.2 copy-start.2
  137.4 3.4 collective-permute-start
  154.4 6.2 %copy-start.3 = (f32[2,80,32,128]{3,2,1,0:T(8,128)S(1)}, f32[2,80,32,128]{3,2,1,0:T(8,128)}, u32[]{:S(2)}) copy-start(f32[2,80,32,128]{3,2,1,0:T(8,128)} %copy-done.2) | copy-start | bytes 7864324 | tf_op jit(solution)/shard_map/while
  166.6 1.9 copy-start
  179.2 9.8 %collective-permute-start.1 = (f32[3,1024]{1,0:T(4,128)S(1)}, f32[3,1024]{1,0:T(4,128)S(1)}, u32[]{:S(2)}, u32[]{:S(2)}) collective-permute-start(f32[3,1024]{1,0:T(4,128)S(1)} %reshape.273), channel_id=1, source_target_pairs={{0,1},{1,2},{2,3},{3,0},{4,5},{5,6},{6,7},{7,4},{8,9},{9,10},{10,1... | collective-permute-start | bytes 36872 | tf_op jit(solution)/shard_map/while/body/eval_jaxpr/ppermute | solution.py:99
  191.2 2.2 copy-start.2
  193.3 3.4 collective-permute-start
  210.4 6.2 %copy-start.3 = (f32[2,80,32,128]{3,2,1,0:T(8,128)S(1)}, f32[2,80,32,128]{3,2,1,0:T(8,128)}, u32[]{:S(2)}) copy-start(f32[2,80,32,128]{3,2,1,0:T(8,128)} %copy-done.2) | copy-start | bytes 7864324 | tf_op jit(solution)/shard_map/while
  222.5 1.9 copy-start
  235.1 9.8 %collective-permute-start.1 = (f32[3,1024]{1,0:T(4,128)S(1)}, f32[3,1024]{1,0:T(4,128)S(1)}, u32[]{:S(2)}, u32[]{:S(2)}) collective-permute-start(f32[3,1024]{1,0:T(4,128)S(1)} %reshape.273), channel_id=1, source_target_pairs={{0,1},{1,2},{2,3},{3,0},{4,5},{5,6},{6,7},{7,4},{8,9},{9,10},{10,1... | collective-permute-start | bytes 36872 | tf_op jit(solution)/shard_map/while/body/eval_jaxpr/ppermute | solution.py:99
  247.1 2.2 copy-start.2
  249.2 3.4 collective-permute-start
  266.3 6.2 %copy-start.3 = (f32[2,80,32,128]{3,2,1,0:T(8,128)S(1)}, f32[2,80,32,128]{3,2,1,0:T(8,128)}, u32[]{:S(2)}) copy-start(f32[2,80,32,128]{3,2,1,0:T(8,128)} %copy-done.2) | copy-start | bytes 7864324 | tf_op jit(solution)/shard_map/while
  278.5 1.9 copy-start
  291.0 9.8 %collective-permute-start.1 = (f32[3,1024]{1,0:T(4,128)S(1)}, f32[3,1024]{1,0:T(4,128)S(1)}, u32[]{:S(2)}, u32[]{:S(2)}) collective-permute-start(f32[3,1024]{1,0:T(4,128)S(1)} %reshape.273), channel_id=1, source_target_pairs={{0,1},{1,2},{2,3},{3,0},{4,5},{5,6},{6,7},{7,4},{8,9},{9,10},{10,1... | collective-permute-start | bytes 36872 | tf_op jit(solution)/shard_map/while/body/eval_jaxpr/ppermute | solution.py:99
  304.0 31.7 %all-to-all-start = ((f32[64,1,384]{2,1,0:T(1,128)}), f32[64,1,384]{2,1,0:T(1,128)S(1)}, u32[]{:S(2)}, u32[]{:S(2)}) async-start(f32[64,1,384]{2,1,0:T(1,128)} %reshape.260), calls=%async_computation | async-start | bytes 196608 | tf_op jit(solution)/shard_map/all_to_all | solution.py:119
  338.8 15.8 %all-to-all-start.1 = ((f32[64,1,384]{2,1,0:T(1,128)}), f32[64,1,384]{2,1,0:T(1,128)S(1)}, u32[]{:S(2)}, u32[]{:S(2)}) async-start(f32[64,1,384]{2,1,0:T(1,128)} %reshape.262), calls=%async_computation.1 | async-start | bytes 196608 | tf_op jit(solution)/shard_map/all_to_all | solution.py:121

commit v3 on v2

--- a/solution.py
+++ b/solution.py
@@ -21,10 +21,51 @@
 exact = lax.Precision.HIGHEST
 
 
-def pair_kernel(tiles_ref, count_ref, xcol_ref, xrow_ref, pcol_ref, prow_ref, wsame_ref,
-                fcol_ref, frow_ref, en_ref):
+def spread_masks():
+    rows = lax.broadcasted_iota(jnp.int32, (HALF, CL), 0)
+    atoms = lax.broadcasted_iota(jnp.int32, (HALF, CL), 1)
+    pick = (atoms // 2 == rows).astype(jnp.float32)
+    atoms_t = lax.broadcasted_iota(jnp.int32, (CL, 2 * CL), 0)
+    lanes_t = lax.broadcasted_iota(jnp.int32, (CL, 2 * CL), 1)
+    place = (atoms_t % 2 == lanes_t // CL).astype(jnp.float32)
+    return pick, place
+
+
+def to_columns(values, pick, place):
+    width = values.shape[0]
+    picked = (values[:, None, :] * pick[None]).reshape(width * HALF, CL)
+    place_b = place.astype(jnp.bfloat16)
+    hi = picked.astype(jnp.bfloat16)
+    rest = picked - hi.astype(jnp.float32)
+    mid = rest.astype(jnp.bfloat16)
+    lo = (rest - mid.astype(jnp.float32)).astype(jnp.bfloat16)
+    spread = jnp.dot(hi, place_b, preferred_element_type=jnp.float32)
+    spread = spread + jnp.dot(mid, place_b, preferred_element_type=jnp.float32)
+    spread = spread + jnp.dot(lo, place_b, preferred_element_type=jnp.float32)
+    return spread.reshape(width, HALF, 2 * CL)
+
+
+def from_columns(blocks, pick, place):
+    width = blocks.shape[0]
+    folded = lax.dot_general(
+        blocks.reshape(width * HALF, 2 * CL), place, (((1,), (1,)), ((), ())),
+        precision=exact, preferred_element_type=jnp.float32,
+    )
+    return jnp.sum(folded.reshape(width, HALF, CL) * pick[None], axis=1)
+
+
+def pair_kernel(tiles_ref, count_ref, ext_ref, prm_ref, xrow_ref, prow_ref,
+                fi_ref, frow_ref, en_ref, xcol_ref, pcol_ref, fcol_ref):
+    pick, place = spread_masks()
+    for c in range(3):
+        xcol_ref[c] = to_columns(ext_ref[c], pick, place)
+    for c in range(2):
+        pcol_ref[c] = to_columns(prm_ref[c], pick, place)
     fcol_ref[...] = jnp.zeros(fcol_ref.shape, jnp.float32)
     frow_ref[...] = jnp.zeros(frow_ref.shape, jnp.float32)
+    rows = lax.broadcasted_iota(jnp.int32, (HALF, 2 * CL), 0)
+    lanes = lax.broadcasted_iota(jnp.int32, (HALF, 2 * CL), 1)
+    w_same = jnp.where(2 * rows + lanes // CL == lanes % CL, 0.0, 0.5).astype(jnp.float32)
 
     def body(t, acc):
         i = tiles_ref[0, t]
@@ -38,7 +79,7 @@
         coulomb = pcol_ref[1, i] * prow_ref[1, j] * inv_root
         same = i == j
         w_force = jnp.where(same, 0.5, 1.0).astype(jnp.float32)
-        w_energy = jnp.where(same, wsame_ref[...], 1.0)
+        w_energy = jnp.where(same, w_same, 1.0)
         slope = w_force * (2.0 * gauss + coulomb * inv_root * inv_root)
         px = slope * dx
         py = slope * dy
@@ -53,17 +94,8 @@
 
     acc = lax.fori_loop(0, count_ref[0], body, jnp.zeros((HALF, 2 * CL), jnp.float32))
     en_ref[...] = acc
-
-
-def self_weights():
-    rows = lax.broadcasted_iota(jnp.int32, (HALF, 2 * CL), 0)
-    lanes = lax.broadcasted_iota(jnp.int32, (HALF, 2 * CL), 1)
-    return jnp.where(2 * rows + lanes // CL == lanes % CL, 0.0, 0.5).astype(jnp.float32)
-
-
-def as_columns(values):
-    lead = values.shape[:-1]
-    return jnp.repeat(values.reshape(lead + (HALF, 2)), CL, axis=-1)
+    for c in range(3):
+        fi_ref[c] = from_columns(fcol_ref[c], pick, place)
 
 
 def as_rows(values):
@@ -71,24 +103,27 @@
     return jnp.concatenate([values, values], -1).reshape(lead + (1, 2 * CL))
 
 
-def slab_pairs(extended, pcol, prow, tiles, count):
+def slab_pairs(extended, prm_cols, prow, tiles, count):
     width = extended.shape[1]
-    xcol = as_columns(extended)
     xrow = as_rows(extended)
     smem = pl.BlockSpec(memory_space=pltpu.SMEM)
     vmem = pl.BlockSpec(memory_space=pltpu.VMEM)
-    fcol, frow, acc = pl.pallas_call(
+    f_i, frow, acc = pl.pallas_call(
         pair_kernel,
         out_shape=(
-            jax.ShapeDtypeStruct((3, width, HALF, 2 * CL), jnp.float32),
+            jax.ShapeDtypeStruct((3, width, CL), jnp.float32),
             jax.ShapeDtypeStruct((3, width, 1, 2 * CL), jnp.float32),
             jax.ShapeDtypeStruct((HALF, 2 * CL), jnp.float32),
         ),
-        in_specs=[smem, smem, vmem, vmem, vmem, vmem, vmem],
+        in_specs=[smem, smem, vmem, vmem, vmem, vmem],
         out_specs=(vmem, vmem, vmem),
+        scratch_shapes=[
+            pltpu.VMEM((3, width, HALF, 2 * CL), jnp.float32),
+            pltpu.VMEM((2, width, HALF, 2 * CL), jnp.float32),
+            pltpu.VMEM((3, width, HALF, 2 * CL), jnp.float32),
+        ],
         compiler_params=pltpu.CompilerParams(vmem_limit_bytes=48 * 1024 * 1024),
-    )(tiles, count.reshape(1), xcol, xrow, pcol, prow, self_weights())
-    f_i = fcol.reshape(3, width, HALF, 2, CL).sum(-1).reshape(3, width, CL)
+    )(tiles, count.reshape(1), extended, prm_cols, xrow, prow)
     f_j = frow.reshape(3, width, 2, CL).sum(2)
     return f_i + f_j, jnp.sum(acc)
 
@@ -191,7 +226,7 @@
     strength_all = jnp.concatenate([params[0], got_params[0]], 0)
     charge_all = jnp.concatenate([params[1], got_params[1]], 0)
     lift = jnp.array([0.0, 0.0, slab_width], jnp.float32)[:, None]
-    param_cols = jnp.stack([as_columns(strength_all), as_columns(ham_scale * charge_all)], 0)
+    param_cols = jnp.stack([strength_all, ham_scale * charge_all], 0)
     param_rows = jnp.stack([as_rows(strength_all), as_rows(charge_all)], 0)
     tile_list = jnp.stack([firsts_flat, seconds_flat], 0)
 

time: 363 us -> 195 us (0.54)
  local copies, waits for them, and re-layouts: 158 us -> 14 us
  other arithmetic: 67.2 us -> 6.96 us
  Pallas kernels: 29.6 us -> 85.1 us
  starting transfers between devices: 34.3 us -> 19.8 us
    pallas_call x5, Pallas kernels: 29.6 us -> 85.1 us  [slab_pairs(): pl.pallas_call(pair_kernel, out_shape=(jax.ShapeDtypeStruct((3, width, CL...]
    concatenate x15 -> x5, local copies, waits for them, and re-layouts: 41.5 us -> 0.03 us  [evaluate(): extended = jnp.concatenate([blocks, from_above.reshape(3, HALO, CL)], 1)]
    reshape x5 -> x0, local copies, waits for them, and re-layouts: 30.7 us -> none  [as_columns(): return jnp.repeat(values.reshape(lead + (HALF, 2)), CL, axis=-1)]
    pallas_call x10 -> x5, local copies, waits for them, and re-layouts: 30.7 us -> 0.61 us  [slab_pairs(): pl.pallas_call(pair_kernel, out_shape=(jax.ShapeDtypeStruct((3, width, CL...]
    reduce_sum x5 -> x0, other arithmetic: 20.8 us -> none  [slab_pairs(): f_i = fcol.reshape(3, width, HALF, 2, CL).sum(-1).reshape(3, width, CL)]
    concatenate x6 -> x0, other arithmetic: 18.8 us -> none  [the longest x5 18.6 us: evaluate(): extended = jnp.concatenate([blocks, from_above.reshape(3, HALO, CL)], 1)]
    broadcast_in_dim x7 -> x0, local copies, waits for them, and re-layouts: 15.6 us -> none  [as_columns(): return jnp.repeat(values.reshape(lead + (HALF, 2)), CL, axis=-1)]
    all_to_all x1, starting transfers between devices: 21.5 us -> 9.02 us  [exchange(): spread = lax.all_to_all(chunks, 'rep', 0, 0, tiled=True)]
  transfers between devices with their start and end apart: 13 -> 13, of which waited for: 6 -> 10; matrix products, arithmetic and copies ran while one was open for 12% -> 2% of each run, Pallas kernels for 0% -> 0%
where the time goes in v3:
time: 195 us; the launch traced here: 192 us
  Pallas kernels  85.1 us (44%)
  waiting for transfers between devices  48.2 us (25%)
  starting transfers between devices  19.8 us (10%)
  local copies, waits for them, and re-layouts  14 us (7%)
  blocking collectives  10.5 us (5%)
  other arithmetic  6.96 us (4%)
  between operations  4.02 us (2%)
  matrix products  3.03 us (2%)
    pallas_call x5, Pallas kernels, slab_pairs(): pl.pallas_call(pair_kernel, out_shape=(jax.ShapeDtypeStruct((3, width, CL...  85.1 us
    ppermute x11, waiting for transfers between devices, from_behind(): return lax.ppermute(value, axis, pairs)  37.9 us
    psum x1, blocking collectives, local(): total_energy = lax.psum(energy, 'slab')  10.5 us
    all_to_all x1, waiting for transfers between devices, exchange(): spread = lax.all_to_all(chunks, 'rep', 0, 0, tiled=True)  10.2 us
    all_to_all x1, starting transfers between devices, exchange(): spread = lax.all_to_all(chunks, 'rep', 0, 0, tiled=True)  9.02 us
    ppermute x11, starting transfers between devices, from_behind(): return lax.ppermute(value, axis, pairs)  6.16 us
    unnamed x27, local copies, waits for them, and re-layouts  5.72 us
    all_to_all x1, starting transfers between devices, exchange(): gathered = lax.all_to_all(routed, 'rep', 0, 0, tiled=True)  4.62 us
  transfers between devices with their start and end apart: 13, of which 10 were waited for; matrix products, arithmetic and copies ran while one was open for 2% of the time, Pallas kernels for 0%

profile of v3, /device:TPU:0, one launch (start us, length us, event | category | flops | bytes accessed | tf_op | source)
XLA Modules:
  0.0 192.0 jit_solution(15246736781246230858)
XLA Ops:
  0.6 0.8 stack.24
  1.5 0.7 copy-done.2
  2.4 4.9 %collective-permute-start.3 = (f32[2,1024]{1,0:T(2,128)S(1)}, f32[2,1024]{1,0:T(2,128)S(1)}, u32[]{:S(2)}, u32[]{:S(2)}) collective-permute-start(f32[2,1024]{1,0:T(2,128)S(1)} %reshape.168), channel_id=1, source_target_pairs={{0,3},{1,0},{2,1},{3,2},{4,7},{5,4},{6,5},{7,6},{8,11},{9,8},{10,9... | collective-permute-start | bytes 24584 | tf_op jit(solution)/shard_map/ppermute | solution.py:134
  7.9 0.7 collective-permute-start.2
  8.7 0.7 copy-done.8
  9.6 0.7 copy-done.7
  10.4 0.7 copy-done.4
  13.0 0.6 copy-done.9
  13.8 16.5 %shard_map.130 = (f32[3,80,64]{2,1,0:T(8,128)S(1)}, f32[3,80,1,128]{3,2,1,0:T(1,128)S(1)}, f32[32,128]{1,0:T(8,128)S(1)}) custom-call(s32[2,192]{1,0:T(2,128)S(1)} %pad_add_fusion.tiles_ref, s32[1]{0:T(128)} %bitcast.89.count_ref, f32[3,80,64]{2,1,0:T(8,128)S(1)} %constant_dynamic-update-slice_fusion.2.ext_ref, f32[2,80,64]{2,1,0:T(8,128)S(1)} %pad_maximum_fusion.3.prm_ref, ...), custom_call_target="tpu_custom_call" | custom-call | tf_op jit(solution)/shard_map/pallas_call | solution.py:111
  30.9 0.6 reduce_sum.57
  31.5 6.4 %collective-permute-done.4 = f32[3,1024]{1,0:T(4,128)S(1)} collective-permute-done((f32[3,1024]{1,0:T(4,128)S(1)}, f32[3,1024]{1,0:T(4,128)S(1)}, u32[]{:S(2)}, u32[]{:S(2)}) %collective-permute-start.4) | collective-permute-done | bytes 12320 | tf_op jit(solution)/shard_map/ppermute | solution.py:134
  38.0 0.3 fusion.11
  38.5 0.6 copy-done
  39.1 110.0 %while.17 = (s32[]{:T(128)}, f32[3,4096]{1,0:T(4,128)S(1)}, f32[3,4096]{1,0:T(4,128)S(1)}, f32[3,4096]{1,0:T(4,128)S(1)}, f32[]{:T(128)}, /*index=5*/f32[4096]{0...) while((s32[]{:T(128)}, f32[3,4096]{1,0:T(4,128)S(1)}, ...), condition=%wide.region_9.10_spmd.clone, body=%wide.region_6.9_spmd.clone.sunk | while | flops 4905985 | bytes 2306413 | solution.py:257
  39.7 1.4 collective-permute-done
  41.4 17.1 %eval_jaxpr.1 = (f32[3,80,64]{2,1,0:T(8,128)S(1)}, f32[3,80,1,128]{3,2,1,0:T(1,128)S(1)}, f32[32,128]{1,0:T(8,128)S(1)}) custom-call(s32[2,192]{1,0:T(2,128)S(1)} %get-tuple-element.258.tiles_ref, s32[1]{0:T(128)} %bitcast.85.count_ref, f32[3,80,64]{2,1,0:T(8,128)S(1)} %constant_dynamic-update-slice_fusion.9.ext_ref, ...), custom_call_target="tpu_custom_call" | custom-call | tf_op jit(solution)/shard_map/while/body/eval_jaxpr/pallas_call | solution.py:111
  58.9 0.6 reduce_sum.65
  59.6 6.5 %collective-permute-done.1 = f32[3,1024]{1,0:T(4,128)S(1)} collective-permute-done((f32[3,1024]{1,0:T(4,128)S(1)}, f32[3,1024]{1,0:T(4,128)S(1)}, u32[]{:S(2)}, u32[]{:S(2)}) %collective-permute-start.1) | collective-permute-done | bytes 12320 | tf_op jit(solution)/shard_map/while/body/eval_jaxpr/ppermute | solution.py:134
  66.1 0.4 fusion.40
  66.8 0.2 convolution_bitcast_fusion.6
  67.2 1.4 collective-permute-done
  68.9 17.1 %eval_jaxpr.1 = (f32[3,80,64]{2,1,0:T(8,128)S(1)}, f32[3,80,1,128]{3,2,1,0:T(1,128)S(1)}, f32[32,128]{1,0:T(8,128)S(1)}) custom-call(s32[2,192]{1,0:T(2,128)S(1)} %get-tuple-element.258.tiles_ref, s32[1]{0:T(128)} %bitcast.85.count_ref, f32[3,80,64]{2,1,0:T(8,128)S(1)} %constant_dynamic-update-slice_fusion.9.ext_ref, ...), custom_call_target="tpu_custom_call" | custom-call | tf_op jit(solution)/shard_map/while/body/eval_jaxpr/pallas_call | solution.py:111
  86.5 0.6 reduce_sum.65
  87.1 6.5 %collective-permute-done.1 = f32[3,1024]{1,0:T(4,128)S(1)} collective-permute-done((f32[3,1024]{1,0:T(4,128)S(1)}, f32[3,1024]{1,0:T(4,128)S(1)}, u32[]{:S(2)}, u32[]{:S(2)}) %collective-permute-start.1) | collective-permute-done | bytes 12320 | tf_op jit(solution)/shard_map/while/body/eval_jaxpr/ppermute | solution.py:134
  93.6 0.4 fusion.40
  94.3 0.2 convolution_bitcast_fusion.6
  94.7 1.4 collective-permute-done
  96.4 17.1 %eval_jaxpr.1 = (f32[3,80,64]{2,1,0:T(8,128)S(1)}, f32[3,80,1,128]{3,2,1,0:T(1,128)S(1)}, f32[32,128]{1,0:T(8,128)S(1)}) custom-call(s32[2,192]{1,0:T(2,128)S(1)} %get-tuple-element.258.tiles_ref, s32[1]{0:T(128)} %bitcast.85.count_ref, f32[3,80,64]{2,1,0:T(8,128)S(1)} %constant_dynamic-update-slice_fusion.9.ext_ref, ...), custom_call_target="tpu_custom_call" | custom-call | tf_op jit(solution)/shard_map/while/body/eval_jaxpr/pallas_call | solution.py:111
  114.0 0.6 reduce_sum.65
  114.6 6.5 %collective-permute-done.1 = f32[3,1024]{1,0:T(4,128)S(1)} collective-permute-done((f32[3,1024]{1,0:T(4,128)S(1)}, f32[3,1024]{1,0:T(4,128)S(1)}, u32[]{:S(2)}, u32[]{:S(2)}) %collective-permute-start.1) | collective-permute-done | bytes 12320 | tf_op jit(solution)/shard_map/while/body/eval_jaxpr/ppermute | solution.py:134
  121.1 0.4 fusion.40
  122.2 1.4 collective-permute-done
  123.9 17.1 %eval_jaxpr.1 = (f32[3,80,64]{2,1,0:T(8,128)S(1)}, f32[3,80,1,128]{3,2,1,0:T(1,128)S(1)}, f32[32,128]{1,0:T(8,128)S(1)}) custom-call(s32[2,192]{1,0:T(2,128)S(1)} %get-tuple-element.258.tiles_ref, s32[1]{0:T(128)} %bitcast.85.count_ref, f32[3,80,64]{2,1,0:T(8,128)S(1)} %constant_dynamic-update-slice_fusion.9.ext_ref, ...), custom_call_target="tpu_custom_call" | custom-call | tf_op jit(solution)/shard_map/while/body/eval_jaxpr/pallas_call | solution.py:111
  141.5 0.6 reduce_sum.65
  142.1 6.5 %collective-permute-done.1 = f32[3,1024]{1,0:T(4,128)S(1)} collective-permute-done((f32[3,1024]{1,0:T(4,128)S(1)}, f32[3,1024]{1,0:T(4,128)S(1)}, u32[]{:S(2)}, u32[]{:S(2)}) %collective-permute-start.1) | collective-permute-done | bytes 12320 | tf_op jit(solution)/shard_map/while/body/eval_jaxpr/ppermute | solution.py:134
  148.6 0.4 fusion.40
  149.4 0.8 reshape.210
  150.2 9.0 %all-to-all-start = ((f32[64,1,384]{2,1,0:T(1,128)}), f32[64,1,384]{2,1,0:T(1,128)S(1)}, u32[]{:S(2)}, u32[]{:S(2)}) async-start(f32[64,1,384]{2,1,0:T(1,128)} %reshape.210), calls=%async_computation | async-start | bytes 196608 | tf_op jit(solution)/shard_map/all_to_all | solution.py:154
  159.3 10.2 %all-to-all-done = f32[64,1,384]{2,1,0:T(1,128)S(1)} async-done(((f32[64,1,384]{2,1,0:T(1,128)}), f32[64,1,384]{2,1,0:T(1,128)S(1)}, u32[]{:S(2)}, u32[]{:S(2)}) %all-to-all-start) | async-done | bytes 98336 | tf_op jit(solution)/shard_map/all_to_all | solution.py:154
  169.5 0.5 broadcast.55
  170.0 0.9 reduce.11
  171.0 0.6 gather_fusion
  171.8 0.8 reshape.212
  172.5 4.6 %all-to-all-start.1 = ((f32[64,1,384]{2,1,0:T(1,128)}), f32[64,1,384]{2,1,0:T(1,128)S(1)}, u32[]{:S(2)}, u32[]{:S(2)}) async-start(f32[64,1,384]{2,1,0:T(1,128)} %reshape.212), calls=%async_computation.1 | async-start | bytes 196608 | tf_op jit(solution)/shard_map/all_to_all | solution.py:156
  177.2 10.5 %psum.7 = f32[]{:T(128)} all-reduce(f32[]{:T(128)} %get-tuple-element.77), channel_id=1, replica_groups=mesh['rep'=64,'slab'=4] {'slab'}, use_global_device_ids=true, to_apply=%region_10.11 | all-reduce | flops 1 | bytes 8 | tf_op jit(solution)/shard_map/psum | solution.py:260
  188.3 0.9 reduce.12
  189.4 0.7 broadcast_in_dim.44
  190.1 0.7 broadcast_in_dim.45
  (155 shorter events, 8.8 us)
Async XLA Ops:
  0.6 0.8 copy-start.3
  1.5 0.7 copy-start.2
  2.2 5.2 %copy-start.1 = (f32[1,3,4096]{2,0,1:T(1,128)S(1)}, f32[1,3,4096]{2,0,1:T(1,128)}, u32[]{:S(2)}) copy-start(f32[1,3,4096]{2,0,1:T(1,128)} %param.13) | copy-start | bytes 147460
  2.4 10.0 %collective-permute-start.3 = (f32[2,1024]{1,0:T(2,128)S(1)}, f32[2,1024]{1,0:T(2,128)S(1)}, u32[]{:S(2)}, u32[]{:S(2)}) collective-permute-start(f32[2,1024]{1,0:T(2,128)S(1)} %reshape.168), channel_id=1, source_target_pairs={{0,3},{1,0},{2,1},{3,2},{4,7},{5,4},{6,5},{7,6},{8,11},{9,8},{10,9... | collective-permute-start | bytes 24584 | tf_op jit(solution)/shard_map/ppermute | solution.py:134
  7.9 5.0 %collective-permute-start.2 = (f32[3,1024]{1,0:T(4,128)S(1)}, f32[3,1024]{1,0:T(4,128)S(1)}, u32[]{:S(2)}, u32[]{:S(2)}) collective-permute-start(f32[3,1024]{1,0:T(4,128)S(1)} %reshape.166), channel_id=1, source_target_pairs={{0,3},{1,0},{2,1},{3,2},{4,7},{5,4},{6,5},{7,6},{8,11},{9,8},{10,9... | collective-permute-start | bytes 36872 | tf_op jit(solution)/shard_map/ppermute | solution.py:134
  8.7 0.7 copy-start.8
  9.4 0.9 copy-start.5
  9.6 0.7 copy-start.7
  10.3 0.7 copy-start.4
  12.9 0.7 copy-start.9
  30.7 7.3 %collective-permute-start.4 = (f32[3,1024]{1,0:T(4,128)S(1)}, f32[3,1024]{1,0:T(4,128)S(1)}, u32[]{:S(2)}, u32[]{:S(2)}) collective-permute-start(f32[3,1024]{1,0:T(4,128)S(1)} %reshape.171), channel_id=1, source_target_pairs={{0,1},{1,2},{2,3},{3,0},{4,5},{5,6},{6,7},{7,4},{8,9},{9,10},{10,1... | collective-permute-start | bytes 36872 | tf_op jit(solution)/shard_map/ppermute | solution.py:134
  38.4 0.7 copy-start
  38.5 0.7 copy-start.6
  39.6 1.5 collective-permute-start
  58.9 7.1 %collective-permute-start.1 = (f32[3,1024]{1,0:T(4,128)S(1)}, f32[3,1024]{1,0:T(4,128)S(1)}, u32[]{:S(2)}, u32[]{:S(2)}) collective-permute-start(f32[3,1024]{1,0:T(4,128)S(1)} %reshape.223), channel_id=1, source_target_pairs={{0,1},{1,2},{2,3},{3,0},{4,5},{5,6},{6,7},{7,4},{8,9},{9,10},{10,1... | collective-permute-start | bytes 36872 | tf_op jit(solution)/shard_map/while/body/eval_jaxpr/ppermute | solution.py:134
  67.1 1.5 collective-permute-start
  86.4 7.1 %collective-permute-start.1 = (f32[3,1024]{1,0:T(4,128)S(1)}, f32[3,1024]{1,0:T(4,128)S(1)}, u32[]{:S(2)}, u32[]{:S(2)}) collective-permute-start(f32[3,1024]{1,0:T(4,128)S(1)} %reshape.223), channel_id=1, source_target_pairs={{0,1},{1,2},{2,3},{3,0},{4,5},{5,6},{6,7},{7,4},{8,9},{9,10},{10,1... | collective-permute-start | bytes 36872 | tf_op jit(solution)/shard_map/while/body/eval_jaxpr/ppermute | solution.py:134
  94.6 1.5 collective-permute-start
  113.9 7.1 %collective-permute-start.1 = (f32[3,1024]{1,0:T(4,128)S(1)}, f32[3,1024]{1,0:T(4,128)S(1)}, u32[]{:S(2)}, u32[]{:S(2)}) collective-permute-start(f32[3,1024]{1,0:T(4,128)S(1)} %reshape.223), channel_id=1, source_target_pairs={{0,1},{1,2},{2,3},{3,0},{4,5},{5,6},{6,7},{7,4},{8,9},{9,10},{10,1... | collective-permute-start | bytes 36872 | tf_op jit(solution)/shard_map/while/body/eval_jaxpr/ppermute | solution.py:134
  122.2 1.5 collective-permute-start
  141.4 7.1 %collective-permute-start.1 = (f32[3,1024]{1,0:T(4,128)S(1)}, f32[3,1024]{1,0:T(4,128)S(1)}, u32[]{:S(2)}, u32[]{:S(2)}) collective-permute-start(f32[3,1024]{1,0:T(4,128)S(1)} %reshape.223), channel_id=1, source_target_pairs={{0,1},{1,2},{2,3},{3,0},{4,5},{5,6},{6,7},{7,4},{8,9},{9,10},{10,1... | collective-permute-start | bytes 36872 | tf_op jit(solution)/shard_map/while/body/eval_jaxpr/ppermute | solution.py:134
  150.2 19.3 %all-to-all-start = ((f32[64,1,384]{2,1,0:T(1,128)}), f32[64,1,384]{2,1,0:T(1,128)S(1)}, u32[]{:S(2)}, u32[]{:S(2)}) async-start(f32[64,1,384]{2,1,0:T(1,128)} %reshape.210), calls=%async_computation | async-start | bytes 196608 | tf_op jit(solution)/shard_map/all_to_all | solution.py:154
  172.5 15.8 %all-to-all-start.1 = ((f32[64,1,384]{2,1,0:T(1,128)}), f32[64,1,384]{2,1,0:T(1,128)S(1)}, u32[]{:S(2)}, u32[]{:S(2)}) async-start(f32[64,1,384]{2,1,0:T(1,128)} %reshape.212), calls=%async_computation.1 | async-start | bytes 196608 | tf_op jit(solution)/shard_map/all_to_all | solution.py:156

commit v4 on v3

--- a/solution.py
+++ b/solution.py
@@ -162,41 +162,6 @@
     return (index_list[:, None] == cluster_ids[None, :]).astype(jnp.float32)
 
 
-def pair_block(extended, strength_all, charge_all, ham_scale, tile_first, tile_second, live_mask):
-    count_tiles = tile_first.shape[0]
-    width = extended.shape[1]
-    select_first = select_table(tile_first, width)
-    select_second = select_table(tile_second, width)
-    coords_i = jnp.einsum("te,xec->xct", select_first, extended, precision=exact)
-    coords_j = jnp.einsum("te,xec->xtc", select_second, extended, precision=exact)
-    offsets = (coords_i[:, :, :, None] - coords_j[:, None, :, :]).reshape(3, CL, count_tiles * CL)
-    sq_dist = offsets[0] * offsets[0] + offsets[1] * offsets[1] + offsets[2] * offsets[2]
-    params_all = jnp.stack([strength_all, charge_all], 0)
-    params_i = jnp.einsum("te,pec->pct", select_first, params_all, precision=exact)
-    params_j = jnp.einsum("te,pec->ptc", select_second, params_all, precision=exact)
-    strength_prod = (params_i[0][:, :, None] * params_j[0][None, :, :]).reshape(
-        CL, count_tiles * CL
-    )
-    charge_prod = (params_i[1][:, :, None] * params_j[1][None, :, :]).reshape(CL, count_tiles * CL)
-    gauss_term = strength_prod * jnp.exp(-sq_dist)
-    inv_root = lax.rsqrt(sq_dist + soft_sq)
-    coulomb = ham_scale * charge_prod * inv_root
-    same_tile = tile_first == tile_second
-    weight_tile = jnp.where(live_mask, jnp.where(same_tile, 0.5, 1.0), 0.0).astype(jnp.float32)
-    weight_col = jnp.repeat(weight_tile, CL)[None, :]
-    slope = gauss_term + 0.5 * coulomb * inv_root * inv_root
-    pushes = (2.0 * slope * weight_col)[None, :, :] * offsets
-    force_i = pushes.reshape(3, CL, count_tiles, CL).sum(-1)
-    force_j = -pushes.sum(1).reshape(3, count_tiles, CL)
-    atom_ids = jnp.arange(CL, dtype=jnp.int32)
-    column_ids = jnp.arange(count_tiles * CL, dtype=jnp.int32) % CL
-    self_pair = jnp.repeat(same_tile, CL)[None, :] & (atom_ids[:, None] == column_ids[None, :])
-    energy = jnp.sum(jnp.where(self_pair, 0.0, (gauss_term + coulomb) * weight_col))
-    spread_i = jnp.einsum("te,xct->xec", select_first, force_i, precision=exact)
-    spread_j = jnp.einsum("te,xtc->xec", select_second, force_j, precision=exact)
-    return (spread_i + spread_j, energy)
-
-
 def local(
     positions,
     velocities,
@@ -209,59 +174,76 @@
     halo_clusters,
     swap_pairs,
 ):
-    coords = positions[0]
-    speeds = velocities[0]
     ham_scale = scaling[0]
-    firsts_flat = tile_pairs[0, 0]
-    seconds_flat = tile_pairs[0, 1]
+    tile_list = tile_pairs[0]
     live_count = tile_counts[0, 0]
     halo_index = halo_clusters[0]
-    atoms_here = coords.shape[1]
-    halo_table = select_table(halo_index, CD)
-    params = jnp.stack([strength, charge], 0).reshape(2, CD, CL)
-    sent_params = jnp.einsum("hc,pck->phk", halo_table, params, precision=exact).reshape(
-        2, HALO * CL
-    )
-    got_params = from_behind(sent_params, "slab", -1).reshape(2, HALO, CL)
-    strength_all = jnp.concatenate([params[0], got_params[0]], 0)
-    charge_all = jnp.concatenate([params[1], got_params[1]], 0)
-    lift = jnp.array([0.0, 0.0, slab_width], jnp.float32)[:, None]
+    atoms_here = positions.shape[2]
+    own = jnp.concatenate(
+        [
+            positions[0].reshape(3, CD, CL),
+            velocities[0].reshape(3, CD, CL),
+            jnp.stack([inv_mass, strength, charge], 0).reshape(3, CD, CL),
+        ],
+        0,
+    )
+    sent = jnp.take(own, halo_index, axis=1)
+    got = from_behind(sent, "slab", -1)
+    full = jnp.concatenate([own, got], 1)
+    coords = full[0:3]
+    speeds = full[3:6]
+    inv_mass_all = full[6]
+    strength_all = full[7]
+    charge_all = full[8]
+    cluster_ids = lax.broadcasted_iota(jnp.int32, (3, CD + HALO, CL), 1)
+    lift_all = jnp.where(
+        (cluster_ids >= CD) & (lax.broadcasted_iota(jnp.int32, (3, CD + HALO, CL), 0) == 2),
+        slab_width,
+        0.0,
+    ).astype(jnp.float32)
     param_cols = jnp.stack([strength_all, ham_scale * charge_all], 0)
     param_rows = jnp.stack([as_rows(strength_all), as_rows(charge_all)], 0)
-    tile_list = jnp.stack([firsts_flat, seconds_flat], 0)
+    halo_table = select_table(halo_index, CD)
 
     def evaluate(coords_now):
-        blocks = coords_now.reshape(3, CD, CL)
-        sent_coords = jnp.einsum("hc,xck->xhk", halo_table, blocks, precision=exact).reshape(
-            3, HALO * CL
-        )
-        from_above = from_behind(sent_coords, "slab", -1) + lift
-        extended = jnp.concatenate([blocks, from_above.reshape(3, HALO, CL)], 1)
+        extended = coords_now + lift_all
         forces, energy = slab_pairs(extended, param_cols, param_rows, tile_list, live_count)
-        returned = from_behind(forces[:, CD:].reshape(3, HALO * CL), "slab", 1)
-        back_home = jnp.einsum(
-            "hc,xhk->xck", halo_table, returned.reshape(3, HALO, CL), precision=exact
-        )
-        local_forces = forces[:, :CD] + back_home
-        return (local_forces.reshape(3, atoms_here), energy)
+        owned_part = jnp.take(forces[:, :CD], halo_index, axis=1)
+        returned = from_behind(forces[:, CD:], "slab", 1)
+        from_owner = from_behind(owned_part, "slab", -1)
+        back_home = jnp.einsum("hc,xhk->xck", halo_table, returned, precision=exact)
+        total = jnp.concatenate([forces[:, :CD] + back_home, forces[:, CD:] + from_owner], 1)
+        return (total, energy)
 
     def verlet_step(step_idx, carry):
         coords, speeds, forces, energy = carry
-        speeds = speeds + half_step * forces * inv_mass
+        speeds = speeds + half_step * forces * inv_mass_all
         coords = coords + time_step * speeds
         forces, energy = evaluate(coords)
-        speeds = speeds + half_step * forces * inv_mass
+        speeds = speeds + half_step * forces * inv_mass_all
         return (coords, speeds, forces, energy)
 
     forces, energy = evaluate(coords)
     coords, speeds, forces, energy = lax.fori_loop(
         0, STEPS, verlet_step, (coords, speeds, forces, energy)
     )
-    total_energy = lax.psum(energy, "slab")
+    total_energy = slab_sum(energy)
     potential = (total_energy / (atoms_here * lax.axis_size("slab"))).reshape(1)
-    state = jnp.concatenate([coords, speeds], 0)
+    state = jnp.concatenate(
+        [coords[:, :CD].reshape(3, atoms_here), speeds[:, :CD].reshape(3, atoms_here)], 0
+    )
     swapped = exchange(state, swap_pairs)
     return (swapped[:3][None], swapped[3:][None], potential)
+
+
+def slab_sum(value):
+    count = lax.axis_size("slab")
+    stride = 1
+    while stride < count:
+        pairs = [(source, source ^ stride) for source in range(count)]
+        value = value + lax.ppermute(value, "slab", pairs)
+        stride *= 2
+    return value
 
 
 def solution(mesh):

time: 195 us -> 204 us (1.046)
  blocking collectives: 10.5 us -> 0 us
  starting transfers between devices: 19.8 us -> 28 us
  waiting for transfers between devices: 48.2 us -> 56.1 us
  other arithmetic: 6.96 us -> 9.31 us
    psum x1 -> x0, blocking collectives: 10.5 us -> none  [local(): total_energy = lax.psum(energy, 'slab')]
    ppermute x0 -> x2, waiting for transfers between devices: none -> 7.69 us  [slab_sum(): value = value + lax.ppermute(value, 'slab', pairs)]
    all_to_all x1, starting transfers between devices: 9.02 us -> 15 us  [exchange(): spread = lax.all_to_all(chunks, 'rep', 0, 0, tiled=True)]
    gather x0 -> x6, local copies, waits for them, and re-layouts: none -> 3.5 us  [the longest x5 2.94 us: evaluate(): owned_part = jnp.take(forces[:, :CD], halo_index, axis=1)]
    reshape x32 -> x0, local copies, waits for them, and re-layouts: 2.97 us -> none  [the longest x5 0.51 us: evaluate(): return (local_forces.reshape(3, atoms_here), energy)]
    unnamed x27 -> x24, local copies, waits for them, and re-layouts: 5.72 us -> 6.44 us
  transfers between devices with their start and end apart: 13 -> 15, of which waited for: 10 -> 13; matrix products, arithmetic and copies ran while one was open for 2% -> 2% of each run, Pallas kernels for 0% -> 0%
where the time goes in v4:
time: 204 us; the launch traced here: 202 us
  Pallas kernels  85.1 us (42%)
  waiting for transfers between devices  56.1 us (28%)
  starting transfers between devices  28 us (14%)
  local copies, waits for them, and re-layouts  15.8 us (8%)
  other arithmetic  9.31 us (5%)
  between operations  5.2 us (3%)
    pallas_call x5, Pallas kernels, slab_pairs(): pl.pallas_call(pair_kernel, out_shape=(jax.ShapeDtypeStruct((3, width, CL...  85.1 us
    ppermute x11, waiting for transfers between devices, from_behind(): return lax.ppermute(value, axis, pairs)  38.4 us
    all_to_all x1, starting transfers between devices, exchange(): spread = lax.all_to_all(chunks, 'rep', 0, 0, tiled=True)  15 us
    all_to_all x1, waiting for transfers between devices, exchange(): spread = lax.all_to_all(chunks, 'rep', 0, 0, tiled=True)  10 us
    ppermute x2, waiting for transfers between devices, slab_sum(): value = value + lax.ppermute(value, 'slab', pairs)  7.69 us
    ppermute x11, starting transfers between devices, from_behind(): return lax.ppermute(value, axis, pairs)  6.96 us
    unnamed x24, local copies, waits for them, and re-layouts  6.44 us
    all_to_all x1, starting transfers between devices, exchange(): gathered = lax.all_to_all(routed, 'rep', 0, 0, tiled=True)  4.62 us
  transfers between devices with their start and end apart: 15, of which 13 were waited for; matrix products, arithmetic and copies ran while one was open for 2% of the time, Pallas kernels for 0%

profile of v4, /device:TPU:0, one launch (start us, length us, event | category | flops | bytes accessed | tf_op | source)
XLA Modules:
  0.0 201.8 jit_solution(16072327403970261828)
XLA Ops:
  0.6 0.7 fusion.21
  1.4 0.9 reduce
  2.4 0.8 copy-done.2
  3.5 0.6 copy-done.4
  4.2 0.6 copy-done.5
  4.9 0.6 copy-done.6
  6.5 5.0 %collective-permute-start.2 = (f32[9,16,64]{2,1,0:T(8,128)S(1)}, f32[9,16,64]{2,1,0:T(8,128)S(1)}, u32[]{:S(2)}, u32[]{:S(2)}) collective-permute-start(f32[9,16,64]{2,1,0:T(8,128)S(1)} %fusion.12), channel_id=1, source_target_pairs={{0,3},{1,0},{2,1},{3,2},{4,7},{5,4},{6,5},{7,6},{8,11},{9,8},{10,9... | collective-permute-start | bytes 110600 | tf_op jit(solution)/shard_map/ppermute | solution.py:134
  11.5 0.7 copy-done.7
  14.1 0.7 copy-done.1
  14.8 16.5 %shard_map.121 = (f32[3,80,64]{2,1,0:T(8,128)S(1)}, f32[3,80,1,128]{3,2,1,0:T(1,128)S(1)}, f32[32,128]{1,0:T(8,128)S(1)}) custom-call(s32[2,192]{1,0:T(2,128)S(1)} %bitcast.95, s32[1]{0:T(128)} %bitcast.86.count_ref, f32[3,80,64]{2,1,0:T(8,128)S(1)} %get-tuple-element.194.ext_ref, f32[2,80,64]{2,1,0:T(8,128)S(1)} %pad_maximum_fusion.4.prm_ref, ...), custom_call_target="tpu_custom_call" | custom-call | tf_op jit(solution)/shard_map/pallas_call | solution.py:111
  31.7 0.6 gather_fusion.3
  32.4 1.5 collective-permute-done.4
  33.9 1.9 collective-permute-start.3
  35.8 0.6 reduce_sum.57
  36.4 4.7 %collective-permute-done.3 = f32[3,16,64]{2,1,0:T(8,128)S(1)} collective-permute-done((f32[3,16,64]{2,1,0:T(8,128)S(1)}, f32[3,16,64]{2,1,0:T(8,128)S(1)}, u32[]{:S(2)}, u32[]{:S(2)}) %collective-permute-start.3) | collective-permute-done | bytes 12320 | tf_op jit(solution)/shard_map/ppermute | solution.py:134
  41.4 110.5 %while.18 = (s32[]{:T(128)}, f32[3,80,64]{2,1,0:T(8,128)S(1)}, f32[3,80,64]{2,1,0:T(8,128)S(1)}, f32[3,80,64]{2,1,0:T(8,128)S(1)}, f32[]{:T(128)}, /*index=5*/f3...) while((s32[]{:T(128)}, f32[3,80,64]{2,1,0:T(8,128)S(1)}, ...), condition=%wide.region_9.11_spmd.clone.clone, body=%wide.region_6.0_spmd.clone.clone.sunk | while | flops 2635921 | bytes 2142940 | solution.py:227
  41.7 17.1 %eval_jaxpr.1 = (f32[3,80,64]{2,1,0:T(8,128)S(1)}, f32[3,80,1,128]{3,2,1,0:T(1,128)S(1)}, f32[32,128]{1,0:T(8,128)S(1)}) custom-call(s32[2,192]{1,0:T(2,128)S(1)} %get-tuple-element.343.tiles_ref, s32[1]{0:T(128)} %bitcast.82.count_ref, f32[3,80,64]{2,1,0:T(8,128)S(1)} %get-tuple-element.298.ext_ref, f32[2,80,64]{2,1,0:T(8,128)S(1)} %get-tuple-element.344.prm_ref, ...), custom_call_target="tpu_custom_call" | custom-call | tf_op jit(solution)/shard_map/while/body/eval_jaxpr/pallas_call | solution.py:111
  59.2 0.6 gather_fusion
  59.9 1.5 collective-permute-done
  61.4 0.6 reduce_sum.67
  62.0 6.6 %collective-permute-done.1 = f32[3,16,64]{2,1,0:T(8,128)S(1)} collective-permute-done((f32[3,16,64]{2,1,0:T(8,128)S(1)}, f32[3,16,64]{2,1,0:T(8,128)S(1)}, u32[]{:S(2)}, u32[]{:S(2)}) %collective-permute-start.1) | collective-permute-done | bytes 12320 | tf_op jit(solution)/shard_map/while/body/eval_jaxpr/ppermute | solution.py:134
  69.3 17.1 %eval_jaxpr.1 = (f32[3,80,64]{2,1,0:T(8,128)S(1)}, f32[3,80,1,128]{3,2,1,0:T(1,128)S(1)}, f32[32,128]{1,0:T(8,128)S(1)}) custom-call(s32[2,192]{1,0:T(2,128)S(1)} %get-tuple-element.343.tiles_ref, s32[1]{0:T(128)} %bitcast.82.count_ref, f32[3,80,64]{2,1,0:T(8,128)S(1)} %get-tuple-element.298.ext_ref, f32[2,80,64]{2,1,0:T(8,128)S(1)} %get-tuple-element.344.prm_ref, ...), custom_call_target="tpu_custom_call" | custom-call | tf_op jit(solution)/shard_map/while/body/eval_jaxpr/pallas_call | solution.py:111
  87.5 1.5 collective-permute-done
  89.0 0.6 reduce_sum.67
  89.7 6.6 %collective-permute-done.1 = f32[3,16,64]{2,1,0:T(8,128)S(1)} collective-permute-done((f32[3,16,64]{2,1,0:T(8,128)S(1)}, f32[3,16,64]{2,1,0:T(8,128)S(1)}, u32[]{:S(2)}, u32[]{:S(2)}) %collective-permute-start.1) | collective-permute-done | bytes 12320 | tf_op jit(solution)/shard_map/while/body/eval_jaxpr/ppermute | solution.py:134
  96.9 17.1 %eval_jaxpr.1 = (f32[3,80,64]{2,1,0:T(8,128)S(1)}, f32[3,80,1,128]{3,2,1,0:T(1,128)S(1)}, f32[32,128]{1,0:T(8,128)S(1)}) custom-call(s32[2,192]{1,0:T(2,128)S(1)} %get-tuple-element.343.tiles_ref, s32[1]{0:T(128)} %bitcast.82.count_ref, f32[3,80,64]{2,1,0:T(8,128)S(1)} %get-tuple-element.298.ext_ref, f32[2,80,64]{2,1,0:T(8,128)S(1)} %get-tuple-element.344.prm_ref, ...), custom_call_target="tpu_custom_call" | custom-call | tf_op jit(solution)/shard_map/while/body/eval_jaxpr/pallas_call | solution.py:111
  115.1 1.5 collective-permute-done
  116.7 0.6 reduce_sum.67
  117.3 6.6 %collective-permute-done.1 = f32[3,16,64]{2,1,0:T(8,128)S(1)} collective-permute-done((f32[3,16,64]{2,1,0:T(8,128)S(1)}, f32[3,16,64]{2,1,0:T(8,128)S(1)}, u32[]{:S(2)}, u32[]{:S(2)}) %collective-permute-start.1) | collective-permute-done | bytes 12320 | tf_op jit(solution)/shard_map/while/body/eval_jaxpr/ppermute | solution.py:134
  124.5 17.1 %eval_jaxpr.1 = (f32[3,80,64]{2,1,0:T(8,128)S(1)}, f32[3,80,1,128]{3,2,1,0:T(1,128)S(1)}, f32[32,128]{1,0:T(8,128)S(1)}) custom-call(s32[2,192]{1,0:T(2,128)S(1)} %get-tuple-element.343.tiles_ref, s32[1]{0:T(128)} %bitcast.82.count_ref, f32[3,80,64]{2,1,0:T(8,128)S(1)} %get-tuple-element.298.ext_ref, f32[2,80,64]{2,1,0:T(8,128)S(1)} %get-tuple-element.344.prm_ref, ...), custom_call_target="tpu_custom_call" | custom-call | tf_op jit(solution)/shard_map/while/body/eval_jaxpr/pallas_call | solution.py:111
  142.8 1.5 collective-permute-done
  144.3 0.6 reduce_sum.67
  144.9 6.6 %collective-permute-done.1 = f32[3,16,64]{2,1,0:T(8,128)S(1)} collective-permute-done((f32[3,16,64]{2,1,0:T(8,128)S(1)}, f32[3,16,64]{2,1,0:T(8,128)S(1)}, u32[]{:S(2)}, u32[]{:S(2)}) %collective-permute-start.1) | collective-permute-done | bytes 12320 | tf_op jit(solution)/shard_map/while/body/eval_jaxpr/ppermute | solution.py:134
  152.0 0.6 copy-done
  152.7 0.9 slice-done
  153.7 0.8 reshape.182
  154.5 15.0 %all-to-all-start = ((f32[64,1,384]{2,1,0:T(1,128)}), f32[64,1,384]{2,1,0:T(1,128)S(1)}, u32[]{:S(2)}, u32[]{:S(2)}) async-start(f32[64,1,384]{2,1,0:T(1,128)} %reshape.182), calls=%async_computation | async-start | bytes 196608 | tf_op jit(solution)/shard_map/all_to_all | solution.py:154
  169.5 10.0 %all-to-all-done = f32[64,1,384]{2,1,0:T(1,128)S(1)} async-done(((f32[64,1,384]{2,1,0:T(1,128)}), f32[64,1,384]{2,1,0:T(1,128)S(1)}, u32[]{:S(2)}, u32[]{:S(2)}) %all-to-all-start) | async-done | bytes 98336 | tf_op jit(solution)/shard_map/all_to_all | solution.py:154
  180.0 0.9 reduce.2
  181.0 0.6 gather_fusion.2
  181.7 0.8 reshape.184
  182.5 4.6 %all-to-all-start.1 = ((f32[64,1,384]{2,1,0:T(1,128)}), f32[64,1,384]{2,1,0:T(1,128)S(1)}, u32[]{:S(2)}, u32[]{:S(2)}) async-start(f32[64,1,384]{2,1,0:T(1,128)} %reshape.184), calls=%async_computation.1 | async-start | bytes 196608 | tf_op jit(solution)/shard_map/all_to_all | solution.py:156
  187.2 1.4 collective-permute-done.5
  189.9 1.4 collective-permute-start.6
  191.3 6.3 %collective-permute-done.6 = f32[]{:T(128)} collective-permute-done((f32[]{:T(128)}, f32[]{:T(128)}, u32[]{:S(2)}, u32[]{:S(2)}) %collective-permute-start.6) | collective-permute-done | bytes 36 | tf_op jit(solution)/shard_map/ppermute | solution.py:244
  198.1 0.9 reduce.3
  199.2 0.7 broadcast_in_dim.82
  199.9 0.7 broadcast_in_dim.83
  (143 shorter events, 10.3 us)
Async XLA Ops:
  0.6 0.7 copy-start.3
  2.4 0.8 copy-start.2
  3.4 0.7 copy-start.4
  4.1 0.7 copy-start.5
  4.8 0.7 copy-start.6
  6.5 7.2 %collective-permute-start.2 = (f32[9,16,64]{2,1,0:T(8,128)S(1)}, f32[9,16,64]{2,1,0:T(8,128)S(1)}, u32[]{:S(2)}, u32[]{:S(2)}) collective-permute-start(f32[9,16,64]{2,1,0:T(8,128)S(1)} %fusion.12), channel_id=1, source_target_pairs={{0,3},{1,0},{2,1},{3,2},{4,7},{5,4},{6,5},{7,6},{8,11},{9,8},{10,9... | collective-permute-start | bytes 110600 | tf_op jit(solution)/shard_map/ppermute | solution.py:134
  11.5 0.7 copy-start.7
  14.1 0.7 copy-start.1
  32.4 1.5 collective-permute-start.4
  33.9 7.2 %collective-permute-start.3 = (f32[3,16,64]{2,1,0:T(8,128)S(1)}, f32[3,16,64]{2,1,0:T(8,128)S(1)}, u32[]{:S(2)}, u32[]{:S(2)}) collective-permute-start(f32[3,16,64]{2,1,0:T(8,128)S(1)} %get-tuple-element.205), channel_id=1, source_target_pairs={{0,1},{1,2},{2,3},{3,0},{4,5},{5,6},{6,7},{7,4},{8,9},{9,10},{10,1... | collective-permute-start | bytes 36872 | tf_op jit(solution)/shard_map/ppermute | solution.py:134
  59.9 1.5 collective-permute-start
  61.4 7.2 %collective-permute-start.1 = (f32[3,16,64]{2,1,0:T(8,128)S(1)}, f32[3,16,64]{2,1,0:T(8,128)S(1)}, u32[]{:S(2)}, u32[]{:S(2)}) collective-permute-start(f32[3,16,64]{2,1,0:T(8,128)S(1)} %get-tuple-element.302), channel_id=1, source_target_pairs={{0,1},{1,2},{2,3},{3,0},{4,5},{5,6},{6,7},{7,4},{8,9},{9,10},{10,1... | collective-permute-start | bytes 36872 | tf_op jit(solution)/shard_map/while/body/eval_jaxpr/ppermute | solution.py:134
  87.5 1.5 collective-permute-start
  89.0 7.2 %collective-permute-start.1 = (f32[3,16,64]{2,1,0:T(8,128)S(1)}, f32[3,16,64]{2,1,0:T(8,128)S(1)}, u32[]{:S(2)}, u32[]{:S(2)}) collective-permute-start(f32[3,16,64]{2,1,0:T(8,128)S(1)} %get-tuple-element.302), channel_id=1, source_target_pairs={{0,1},{1,2},{2,3},{3,0},{4,5},{5,6},{6,7},{7,4},{8,9},{9,10},{10,1... | collective-permute-start | bytes 36872 | tf_op jit(solution)/shard_map/while/body/eval_jaxpr/ppermute | solution.py:134
  115.1 1.5 collective-permute-start
  116.7 7.2 %collective-permute-start.1 = (f32[3,16,64]{2,1,0:T(8,128)S(1)}, f32[3,16,64]{2,1,0:T(8,128)S(1)}, u32[]{:S(2)}, u32[]{:S(2)}) collective-permute-start(f32[3,16,64]{2,1,0:T(8,128)S(1)} %get-tuple-element.302), channel_id=1, source_target_pairs={{0,1},{1,2},{2,3},{3,0},{4,5},{5,6},{6,7},{7,4},{8,9},{9,10},{10,1... | collective-permute-start | bytes 36872 | tf_op jit(solution)/shard_map/while/body/eval_jaxpr/ppermute | solution.py:134
  142.7 1.5 collective-permute-start
  144.3 7.2 %collective-permute-start.1 = (f32[3,16,64]{2,1,0:T(8,128)S(1)}, f32[3,16,64]{2,1,0:T(8,128)S(1)}, u32[]{:S(2)}, u32[]{:S(2)}) collective-permute-start(f32[3,16,64]{2,1,0:T(8,128)S(1)} %get-tuple-element.302), channel_id=1, source_target_pairs={{0,1},{1,2},{2,3},{3,0},{4,5},{5,6},{6,7},{7,4},{8,9},{9,10},{10,1... | collective-permute-start | bytes 36872 | tf_op jit(solution)/shard_map/while/body/eval_jaxpr/ppermute | solution.py:134
  152.0 0.7 copy-start
  152.7 0.9 slice-start
  154.5 25.0 %all-to-all-start = ((f32[64,1,384]{2,1,0:T(1,128)}), f32[64,1,384]{2,1,0:T(1,128)S(1)}, u32[]{:S(2)}, u32[]{:S(2)}) async-start(f32[64,1,384]{2,1,0:T(1,128)} %reshape.182), calls=%async_computation | async-start | bytes 196608 | tf_op jit(solution)/shard_map/all_to_all | solution.py:154
  182.5 15.6 %all-to-all-start.1 = ((f32[64,1,384]{2,1,0:T(1,128)}), f32[64,1,384]{2,1,0:T(1,128)S(1)}, u32[]{:S(2)}, u32[]{:S(2)}) async-start(f32[64,1,384]{2,1,0:T(1,128)} %reshape.184), calls=%async_computation.1 | async-start | bytes 196608 | tf_op jit(solution)/shard_map/all_to_all | solution.py:156
  187.1 1.5 collective-permute-start.5
  189.9 7.7 %collective-permute-start.6 = (f32[]{:T(128)}, f32[]{:T(128)}, u32[]{:S(2)}, u32[]{:S(2)}) collective-permute-start(f32[]{:T(128)} %add.108), channel_id=1, source_target_pairs={{0,2},{1,3},{2,0},{3,1},{4,6},{5,7},{6,4},{7,5},{8,10},{9,11},{10,... | collective-permute-start | bytes 20 | tf_op jit(solution)/shard_map/ppermute | solution.py:244

commit v5 on v3

--- a/solution.py
+++ b/solution.py
@@ -28,20 +28,27 @@
     atoms_t = lax.broadcasted_iota(jnp.int32, (CL, 2 * CL), 0)
     lanes_t = lax.broadcasted_iota(jnp.int32, (CL, 2 * CL), 1)
     place = (atoms_t % 2 == lanes_t // CL).astype(jnp.float32)
-    return pick, place
+    twice = (atoms_t == lanes_t % CL).astype(jnp.float32)
+    return pick, place, twice
+
+
+def split_dot(values, matrix, dims):
+    matrix_b = matrix.astype(jnp.bfloat16)
+    hi = values.astype(jnp.bfloat16)
+    rest = values - hi.astype(jnp.float32)
+    mid = rest.astype(jnp.bfloat16)
+    lo = (rest - mid.astype(jnp.float32)).astype(jnp.bfloat16)
+    total = None
+    for part in (hi, mid, lo):
+        term = lax.dot_general(part, matrix_b, (dims, ((), ())), preferred_element_type=jnp.float32)
+        total = term if total is None else total + term
+    return total
 
 
 def to_columns(values, pick, place):
     width = values.shape[0]
     picked = (values[:, None, :] * pick[None]).reshape(width * HALF, CL)
-    place_b = place.astype(jnp.bfloat16)
-    hi = picked.astype(jnp.bfloat16)
-    rest = picked - hi.astype(jnp.float32)
-    mid = rest.astype(jnp.bfloat16)
-    lo = (rest - mid.astype(jnp.float32)).astype(jnp.bfloat16)
-    spread = jnp.dot(hi, place_b, preferred_element_type=jnp.float32)
-    spread = spread + jnp.dot(mid, place_b, preferred_element_type=jnp.float32)
-    spread = spread + jnp.dot(lo, place_b, preferred_element_type=jnp.float32)
+    spread = split_dot(picked, place, ((1,), (0,)))
     return spread.reshape(width, HALF, 2 * CL)
 
 
@@ -54,13 +61,15 @@
     return jnp.sum(folded.reshape(width, HALF, CL) * pick[None], axis=1)
 
 
-def pair_kernel(tiles_ref, count_ref, ext_ref, prm_ref, xrow_ref, prow_ref,
-                fi_ref, frow_ref, en_ref, xcol_ref, pcol_ref, fcol_ref):
-    pick, place = spread_masks()
+def pair_kernel(tiles_ref, count_ref, ext_ref, prm_ref, force_ref, en_ref,
+                xcol_ref, pcol_ref, xrow_ref, prow_ref, fcol_ref, frow_ref):
+    pick, place, twice = spread_masks()
     for c in range(3):
         xcol_ref[c] = to_columns(ext_ref[c], pick, place)
+        xrow_ref[c] = split_dot(ext_ref[c], twice, ((1,), (0,)))
     for c in range(2):
         pcol_ref[c] = to_columns(prm_ref[c], pick, place)
+        prow_ref[c] = split_dot(prm_ref[2 * c], twice, ((1,), (0,)))
     fcol_ref[...] = jnp.zeros(fcol_ref.shape, jnp.float32)
     frow_ref[...] = jnp.zeros(frow_ref.shape, jnp.float32)
     rows = lax.broadcasted_iota(jnp.int32, (HALF, 2 * CL), 0)
@@ -70,13 +79,14 @@
     def body(t, acc):
         i = tiles_ref[0, t]
         j = tiles_ref[1, t]
-        dx = xcol_ref[0, i] - xrow_ref[0, j]
-        dy = xcol_ref[1, i] - xrow_ref[1, j]
-        dz = xcol_ref[2, i] - xrow_ref[2, j]
+        row = pl.ds(j, 1)
+        dx = xcol_ref[0, i] - xrow_ref[0, row, :]
+        dy = xcol_ref[1, i] - xrow_ref[1, row, :]
+        dz = xcol_ref[2, i] - xrow_ref[2, row, :]
         sq = dx * dx + dy * dy + dz * dz
-        gauss = pcol_ref[0, i] * prow_ref[0, j] * jnp.exp(-sq)
+        gauss = pcol_ref[0, i] * prow_ref[0, row, :] * jnp.exp(-sq)
         inv_root = lax.rsqrt(sq + soft_sq)
-        coulomb = pcol_ref[1, i] * prow_ref[1, j] * inv_root
+        coulomb = pcol_ref[1, i] * prow_ref[1, row, :] * inv_root
         same = i == j
         w_force = jnp.where(same, 0.5, 1.0).astype(jnp.float32)
         w_energy = jnp.where(same, w_same, 1.0)
@@ -87,45 +97,44 @@
         fcol_ref[0, i] += px
         fcol_ref[1, i] += py
         fcol_ref[2, i] += pz
-        frow_ref[0, j] -= jnp.sum(px, axis=0, keepdims=True)
-        frow_ref[1, j] -= jnp.sum(py, axis=0, keepdims=True)
-        frow_ref[2, j] -= jnp.sum(pz, axis=0, keepdims=True)
+        frow_ref[0, row, :] -= jnp.sum(px, axis=0, keepdims=True)
+        frow_ref[1, row, :] -= jnp.sum(py, axis=0, keepdims=True)
+        frow_ref[2, row, :] -= jnp.sum(pz, axis=0, keepdims=True)
         return acc + w_energy * (gauss + coulomb)
 
     acc = lax.fori_loop(0, count_ref[0], body, jnp.zeros((HALF, 2 * CL), jnp.float32))
     en_ref[...] = acc
     for c in range(3):
-        fi_ref[c] = from_columns(fcol_ref[c], pick, place)
-
-
-def as_rows(values):
-    lead = values.shape[:-1]
-    return jnp.concatenate([values, values], -1).reshape(lead + (1, 2 * CL))
-
-
-def slab_pairs(extended, prm_cols, prow, tiles, count):
+        f_j = lax.dot_general(
+            frow_ref[c], twice, (((1,), (1,)), ((), ())),
+            precision=exact, preferred_element_type=jnp.float32,
+        )
+        force_ref[c] = from_columns(fcol_ref[c], pick, place) + f_j
+
+
+def slab_pairs(extended, prm, tiles, count):
     width = extended.shape[1]
-    xrow = as_rows(extended)
     smem = pl.BlockSpec(memory_space=pltpu.SMEM)
     vmem = pl.BlockSpec(memory_space=pltpu.VMEM)
-    f_i, frow, acc = pl.pallas_call(
+    forces, acc = pl.pallas_call(
         pair_kernel,
         out_shape=(
             jax.ShapeDtypeStruct((3, width, CL), jnp.float32),
-            jax.ShapeDtypeStruct((3, width, 1, 2 * CL), jnp.float32),
             jax.ShapeDtypeStruct((HALF, 2 * CL), jnp.float32),
         ),
-        in_specs=[smem, smem, vmem, vmem, vmem, vmem],
-        out_specs=(vmem, vmem, vmem),
+        in_specs=[smem, smem, vmem, vmem],
+        out_specs=(vmem, vmem),
         scratch_shapes=[
             pltpu.VMEM((3, width, HALF, 2 * CL), jnp.float32),
             pltpu.VMEM((2, width, HALF, 2 * CL), jnp.float32),
+            pltpu.VMEM((3, width, 2 * CL), jnp.float32),
+            pltpu.VMEM((2, width, 2 * CL), jnp.float32),
             pltpu.VMEM((3, width, HALF, 2 * CL), jnp.float32),
+            pltpu.VMEM((3, width, 2 * CL), jnp.float32),
         ],
         compiler_params=pltpu.CompilerParams(vmem_limit_bytes=48 * 1024 * 1024),
-    )(tiles, count.reshape(1), extended, prm_cols, xrow, prow)
-    f_j = frow.reshape(3, width, 2, CL).sum(2)
-    return f_i + f_j, jnp.sum(acc)
+    )(tiles, count.reshape(1), extended, prm)
+    return forces, jnp.sum(acc)
 
 
 def from_behind(value, axis, steps):
@@ -226,8 +235,7 @@
     strength_all = jnp.concatenate([params[0], got_params[0]], 0)
     charge_all = jnp.concatenate([params[1], got_params[1]], 0)
     lift = jnp.array([0.0, 0.0, slab_width], jnp.float32)[:, None]
-    param_cols = jnp.stack([strength_all, ham_scale * charge_all], 0)
-    param_rows = jnp.stack([as_rows(strength_all), as_rows(charge_all)], 0)
+    param_all = jnp.stack([strength_all, ham_scale * charge_all, charge_all], 0)
     tile_list = jnp.stack([firsts_flat, seconds_flat], 0)
 
     def evaluate(coords_now):
@@ -237,7 +245,7 @@
         )
         from_above = from_behind(sent_coords, "slab", -1) + lift
         extended = jnp.concatenate([blocks, from_above.reshape(3, HALO, CL)], 1)
-        forces, energy = slab_pairs(extended, param_cols, param_rows, tile_list, live_count)
+        forces, energy = slab_pairs(extended, param_all, tile_list, live_count)
         returned = from_behind(forces[:, CD:].reshape(3, HALO * CL), "slab", 1)
         back_home = jnp.einsum(
             "hc,xhk->xck", halo_table, returned.reshape(3, HALO, CL), precision=exact

time: 195 us -> 190 us (0.974)
  starting transfers between devices: 19.8 us -> 73.7 us
  waiting for transfers between devices: 48.2 us -> 18.7 us
  Pallas kernels: 85.1 us -> 59.7 us
  local copies, waits for them, and re-layouts: 14 us -> 11.5 us
    ppermute x11, starting transfers between devices: 6.16 us -> 53.5 us  [from_behind(): return lax.ppermute(value, axis, pairs)]
    ppermute x11, waiting for transfers between devices: 37.9 us -> 8.47 us  [from_behind(): return lax.ppermute(value, axis, pairs)]
    pallas_call x5, Pallas kernels: 85.1 us -> 59.7 us  [slab_pairs(): pl.pallas_call(pair_kernel, out_shape=(jax.ShapeDtypeStruct((3, width, CL...]
    all_to_all x1, starting transfers between devices: 9.02 us -> 15.5 us  [exchange(): spread = lax.all_to_all(chunks, 'rep', 0, 0, tiled=True)]
    unnamed x27 -> x25, local copies, waits for them, and re-layouts: 5.72 us -> 4.41 us
where the time goes in v5:
time: 190 us; the launch traced here: 187 us
  starting transfers between devices  73.7 us (39%)
  Pallas kernels  59.7 us (31%)
  waiting for transfers between devices  18.7 us (10%)
  local copies, waits for them, and re-layouts  11.5 us (6%)
  blocking collectives  10.5 us (6%)
  other arithmetic  6.11 us (3%)
  between operations  3.98 us (2%)
  matrix products  3.04 us (2%)
    pallas_call x5, Pallas kernels, slab_pairs(): pl.pallas_call(pair_kernel, out_shape=(jax.ShapeDtypeStruct((3, width, CL...  59.7 us
    ppermute x11, starting transfers between devices, from_behind(): return lax.ppermute(value, axis, pairs)  53.5 us
    all_to_all x1, starting transfers between devices, exchange(): spread = lax.all_to_all(chunks, 'rep', 0, 0, tiled=True)  15.5 us
    psum x1, blocking collectives, local(): total_energy = lax.psum(energy, 'slab')  10.5 us
    all_to_all x1, waiting for transfers between devices, exchange(): spread = lax.all_to_all(chunks, 'rep', 0, 0, tiled=True)  10.2 us
    ppermute x11, waiting for transfers between devices, from_behind(): return lax.ppermute(value, axis, pairs)  8.47 us
    all_to_all x1, starting transfers between devices, exchange(): gathered = lax.all_to_all(routed, 'rep', 0, 0, tiled=True)  4.62 us
    unnamed x25, local copies, waits for them, and re-layouts  4.41 us
  transfers between devices with their start and end apart: 13, of which 10 were waited for; matrix products, arithmetic and copies ran while one was open for 2% of the time, Pallas kernels for 0%

profile of v5, /device:TPU:0, one launch (start us, length us, event | category | flops | bytes accessed | tf_op | source)
XLA Modules:
  0.0 187.4 jit_solution(14837466684778029128)
XLA Ops:
  0.6 0.8 stack.24
  1.5 0.7 copy-done.2
  2.4 4.9 %collective-permute-start.3 = (f32[2,1024]{1,0:T(2,128)S(1)}, f32[2,1024]{1,0:T(2,128)S(1)}, u32[]{:S(2)}, u32[]{:S(2)}) collective-permute-start(f32[2,1024]{1,0:T(2,128)S(1)} %reshape.156), channel_id=1, source_target_pairs={{0,3},{1,0},{2,1},{3,2},{4,7},{5,4},{6,5},{7,6},{8,11},{9,8},{10,9... | collective-permute-start | bytes 24584 | tf_op jit(solution)/shard_map/ppermute | solution.py:143
  7.9 0.7 collective-permute-start.2
  9.0 0.6 copy-done.4
  11.4 0.6 copy-done.9
  12.2 11.4 %shard_map.130 = (f32[3,80,64]{2,1,0:T(8,128)S(1)}, f32[32,128]{1,0:T(8,128)S(1)}) custom-call(s32[2,192]{1,0:T(2,128)S(1)} %pad_add_fusion.tiles_ref, s32[1]{0:T(128)} %bitcast.82.count_ref, f32[3,80,64]{2,1,0:T(8,128)S(1)} %pad_maximum_fusion.2.ext_ref, f32[3,80,64]{2,1,0:T(8,128)S(1)} %pad_maximum_fusion.3.prm_ref), custom_call_target="tpu_custom_call" | custom-call | tf_op jit(solution)/shard_map/pallas_call | solution.py:119
  23.7 4.9 %collective-permute-start.4 = (f32[3,1024]{1,0:T(4,128)S(1)}, f32[3,1024]{1,0:T(4,128)S(1)}, u32[]{:S(2)}, u32[]{:S(2)}) collective-permute-start(f32[3,1024]{1,0:T(4,128)S(1)} %reshape.157), channel_id=1, source_target_pairs={{0,1},{1,2},{2,3},{3,0},{4,5},{5,6},{6,7},{7,4},{8,9},{9,10},{10,1... | collective-permute-start | bytes 36872 | tf_op jit(solution)/shard_map/ppermute | solution.py:143
  28.6 0.6 reduce_sum.38
  29.2 1.8 collective-permute-done.4
  31.1 0.3 fusion.11
  31.5 0.6 copy-done
  32.2 106.0 %while.17 = (s32[]{:T(128)}, f32[3,4096]{1,0:T(4,128)S(1)}, f32[3,4096]{1,0:T(4,128)S(1)}, f32[3,4096]{1,0:T(4,128)S(1)}, f32[]{:T(128)}, /*index=5*/f32[4096]{0...) while((s32[]{:T(128)}, f32[3,4096]{1,0:T(4,128)S(1)}, ...), condition=%wide.region_7.8_spmd.clone, body=%wide.region_5.0_spmd.clone.sunk | while | flops 4859905 | bytes 1311073 | solution.py:265
  32.7 1.4 collective-permute-done
  34.3 12.1 %eval_jaxpr.1 = (f32[3,80,64]{2,1,0:T(8,128)S(1)}, f32[32,128]{1,0:T(8,128)S(1)}) custom-call(s32[2,192]{1,0:T(2,128)S(1)} %get-tuple-element.234.tiles_ref, s32[1]{0:T(128)} %bitcast.80.count_ref, f32[3,80,64]{2,1,0:T(8,128)S(1)} %pad_maximum_fusion.5.ext_ref, f32[3,80,64]{2,1,0:T(8,128)S(1)} %get-tuple-element.235.prm_ref), custom_call_target="tpu_custom_call" | custom-call | tf_op jit(solution)/shard_map/while/body/eval_jaxpr/pallas_call | solution.py:119
  46.5 9.6 %collective-permute-start.1 = (f32[3,1024]{1,0:T(4,128)S(1)}, f32[3,1024]{1,0:T(4,128)S(1)}, u32[]{:S(2)}, u32[]{:S(2)}) collective-permute-start(f32[3,1024]{1,0:T(4,128)S(1)} %reshape.207), channel_id=1, source_target_pairs={{0,1},{1,2},{2,3},{3,0},{4,5},{5,6},{6,7},{7,4},{8,9},{9,10},{10,1... | collective-permute-start | bytes 36872 | tf_op jit(solution)/shard_map/while/body/eval_jaxpr/ppermute | solution.py:143
  56.0 0.6 reduce_sum.43
  56.6 0.2 collective-permute-done.1
  56.9 0.4 fusion.40
  58.0 1.4 collective-permute-done
  59.6 12.1 %eval_jaxpr.1 = (f32[3,80,64]{2,1,0:T(8,128)S(1)}, f32[32,128]{1,0:T(8,128)S(1)}) custom-call(s32[2,192]{1,0:T(2,128)S(1)} %get-tuple-element.234.tiles_ref, s32[1]{0:T(128)} %bitcast.80.count_ref, f32[3,80,64]{2,1,0:T(8,128)S(1)} %pad_maximum_fusion.5.ext_ref, f32[3,80,64]{2,1,0:T(8,128)S(1)} %get-tuple-element.235.prm_ref), custom_call_target="tpu_custom_call" | custom-call | tf_op jit(solution)/shard_map/while/body/eval_jaxpr/pallas_call | solution.py:119
  71.8 11.1 %collective-permute-start.1 = (f32[3,1024]{1,0:T(4,128)S(1)}, f32[3,1024]{1,0:T(4,128)S(1)}, u32[]{:S(2)}, u32[]{:S(2)}) collective-permute-start(f32[3,1024]{1,0:T(4,128)S(1)} %reshape.207), channel_id=1, source_target_pairs={{0,1},{1,2},{2,3},{3,0},{4,5},{5,6},{6,7},{7,4},{8,9},{9,10},{10,1... | collective-permute-start | bytes 36872 | tf_op jit(solution)/shard_map/while/body/eval_jaxpr/ppermute | solution.py:143
  82.9 0.6 reduce_sum.43
  83.5 0.2 collective-permute-done.1
  83.8 0.4 fusion.40
  84.9 1.4 collective-permute-done
  86.5 12.1 %eval_jaxpr.1 = (f32[3,80,64]{2,1,0:T(8,128)S(1)}, f32[32,128]{1,0:T(8,128)S(1)}) custom-call(s32[2,192]{1,0:T(2,128)S(1)} %get-tuple-element.234.tiles_ref, s32[1]{0:T(128)} %bitcast.80.count_ref, f32[3,80,64]{2,1,0:T(8,128)S(1)} %pad_maximum_fusion.5.ext_ref, f32[3,80,64]{2,1,0:T(8,128)S(1)} %get-tuple-element.235.prm_ref), custom_call_target="tpu_custom_call" | custom-call | tf_op jit(solution)/shard_map/while/body/eval_jaxpr/pallas_call | solution.py:119
  98.7 11.1 %collective-permute-start.1 = (f32[3,1024]{1,0:T(4,128)S(1)}, f32[3,1024]{1,0:T(4,128)S(1)}, u32[]{:S(2)}, u32[]{:S(2)}) collective-permute-start(f32[3,1024]{1,0:T(4,128)S(1)} %reshape.207), channel_id=1, source_target_pairs={{0,1},{1,2},{2,3},{3,0},{4,5},{5,6},{6,7},{7,4},{8,9},{9,10},{10,1... | collective-permute-start | bytes 36872 | tf_op jit(solution)/shard_map/while/body/eval_jaxpr/ppermute | solution.py:143
  109.8 0.6 reduce_sum.43
  110.7 0.4 fusion.40
  111.8 1.4 collective-permute-done
  113.4 12.1 %eval_jaxpr.1 = (f32[3,80,64]{2,1,0:T(8,128)S(1)}, f32[32,128]{1,0:T(8,128)S(1)}) custom-call(s32[2,192]{1,0:T(2,128)S(1)} %get-tuple-element.234.tiles_ref, s32[1]{0:T(128)} %bitcast.80.count_ref, f32[3,80,64]{2,1,0:T(8,128)S(1)} %pad_maximum_fusion.5.ext_ref, f32[3,80,64]{2,1,0:T(8,128)S(1)} %get-tuple-element.235.prm_ref), custom_call_target="tpu_custom_call" | custom-call | tf_op jit(solution)/shard_map/while/body/eval_jaxpr/pallas_call | solution.py:119
  125.6 11.1 %collective-permute-start.1 = (f32[3,1024]{1,0:T(4,128)S(1)}, f32[3,1024]{1,0:T(4,128)S(1)}, u32[]{:S(2)}, u32[]{:S(2)}) collective-permute-start(f32[3,1024]{1,0:T(4,128)S(1)} %reshape.207), channel_id=1, source_target_pairs={{0,1},{1,2},{2,3},{3,0},{4,5},{5,6},{6,7},{7,4},{8,9},{9,10},{10,1... | collective-permute-start | bytes 36872 | tf_op jit(solution)/shard_map/while/body/eval_jaxpr/ppermute | solution.py:143
  136.7 0.6 reduce_sum.43
  137.3 0.2 collective-permute-done.1
  137.6 0.4 fusion.40
  138.4 0.8 reshape.194
  139.2 15.5 %all-to-all-start = ((f32[64,1,384]{2,1,0:T(1,128)}), f32[64,1,384]{2,1,0:T(1,128)S(1)}, u32[]{:S(2)}, u32[]{:S(2)}) async-start(f32[64,1,384]{2,1,0:T(1,128)} %reshape.194), calls=%async_computation | async-start | bytes 196608 | tf_op jit(solution)/shard_map/all_to_all | solution.py:163
  154.7 10.2 %all-to-all-done = f32[64,1,384]{2,1,0:T(1,128)S(1)} async-done(((f32[64,1,384]{2,1,0:T(1,128)}), f32[64,1,384]{2,1,0:T(1,128)S(1)}, u32[]{:S(2)}, u32[]{:S(2)}) %all-to-all-start) | async-done | bytes 98336 | tf_op jit(solution)/shard_map/all_to_all | solution.py:163
  164.9 0.5 broadcast.55
  165.4 0.9 reduce.11
  166.4 0.6 gather_fusion
  167.2 0.8 reshape.196
  168.0 4.6 %all-to-all-start.1 = ((f32[64,1,384]{2,1,0:T(1,128)}), f32[64,1,384]{2,1,0:T(1,128)S(1)}, u32[]{:S(2)}, u32[]{:S(2)}) async-start(f32[64,1,384]{2,1,0:T(1,128)} %reshape.196), calls=%async_computation.1 | async-start | bytes 196608 | tf_op jit(solution)/shard_map/all_to_all | solution.py:165
  172.6 10.5 %psum.7 = f32[]{:T(128)} all-reduce(f32[]{:T(128)} %get-tuple-element.69), channel_id=1, replica_groups=mesh['rep'=64,'slab'=4] {'slab'}, use_global_device_ids=true, to_apply=%region_8.9 | all-reduce | flops 1 | bytes 8 | tf_op jit(solution)/shard_map/psum | solution.py:268
  183.8 0.9 reduce.12
  184.8 0.7 broadcast_in_dim.44
  185.6 0.7 broadcast_in_dim.45
  (121 shorter events, 7.0 us)
Async XLA Ops:
  0.6 0.8 copy-start.3
  1.5 0.7 copy-start.2
  2.2 5.2 %copy-start.1 = (f32[1,3,4096]{2,0,1:T(1,128)S(1)}, f32[1,3,4096]{2,0,1:T(1,128)}, u32[]{:S(2)}) copy-start(f32[1,3,4096]{2,0,1:T(1,128)} %param.13) | copy-start | bytes 147460
  2.4 8.6 %collective-permute-start.3 = (f32[2,1024]{1,0:T(2,128)S(1)}, f32[2,1024]{1,0:T(2,128)S(1)}, u32[]{:S(2)}, u32[]{:S(2)}) collective-permute-start(f32[2,1024]{1,0:T(2,128)S(1)} %reshape.156), channel_id=1, source_target_pairs={{0,3},{1,0},{2,1},{3,2},{4,7},{5,4},{6,5},{7,6},{8,11},{9,8},{10,9... | collective-permute-start | bytes 24584 | tf_op jit(solution)/shard_map/ppermute | solution.py:143
  7.6 1.0 copy-start.8
  7.6 1.2 copy-start.7
  7.8 1.0 copy-start.5
  7.9 3.4 %collective-permute-start.2 = (f32[3,1024]{1,0:T(4,128)S(1)}, f32[3,1024]{1,0:T(4,128)S(1)}, u32[]{:S(2)}, u32[]{:S(2)}) collective-permute-start(f32[3,1024]{1,0:T(4,128)S(1)} %reshape.154), channel_id=1, source_target_pairs={{0,3},{1,0},{2,1},{3,2},{4,7},{5,4},{6,5},{7,6},{8,11},{9,8},{10,9... | collective-permute-start | bytes 36872 | tf_op jit(solution)/shard_map/ppermute | solution.py:143
  9.0 0.7 copy-start.4
  11.3 0.7 copy-start.9
  23.7 7.3 %collective-permute-start.4 = (f32[3,1024]{1,0:T(4,128)S(1)}, f32[3,1024]{1,0:T(4,128)S(1)}, u32[]{:S(2)}, u32[]{:S(2)}) collective-permute-start(f32[3,1024]{1,0:T(4,128)S(1)} %reshape.157), channel_id=1, source_target_pairs={{0,1},{1,2},{2,3},{3,0},{4,5},{5,6},{6,7},{7,4},{8,9},{9,10},{10,1... | collective-permute-start | bytes 36872 | tf_op jit(solution)/shard_map/ppermute | solution.py:143
  31.4 0.7 copy-start
  31.5 0.7 copy-start.6
  32.6 1.5 collective-permute-start
  46.5 10.4 %collective-permute-start.1 = (f32[3,1024]{1,0:T(4,128)S(1)}, f32[3,1024]{1,0:T(4,128)S(1)}, u32[]{:S(2)}, u32[]{:S(2)}) collective-permute-start(f32[3,1024]{1,0:T(4,128)S(1)} %reshape.207), channel_id=1, source_target_pairs={{0,1},{1,2},{2,3},{3,0},{4,5},{5,6},{6,7},{7,4},{8,9},{9,10},{10,1... | collective-permute-start | bytes 36872 | tf_op jit(solution)/shard_map/while/body/eval_jaxpr/ppermute | solution.py:143
  58.0 1.5 collective-permute-start
  71.8 11.9 %collective-permute-start.1 = (f32[3,1024]{1,0:T(4,128)S(1)}, f32[3,1024]{1,0:T(4,128)S(1)}, u32[]{:S(2)}, u32[]{:S(2)}) collective-permute-start(f32[3,1024]{1,0:T(4,128)S(1)} %reshape.207), channel_id=1, source_target_pairs={{0,1},{1,2},{2,3},{3,0},{4,5},{5,6},{6,7},{7,4},{8,9},{9,10},{10,1... | collective-permute-start | bytes 36872 | tf_op jit(solution)/shard_map/while/body/eval_jaxpr/ppermute | solution.py:143
  84.9 1.5 collective-permute-start
  98.7 11.9 %collective-permute-start.1 = (f32[3,1024]{1,0:T(4,128)S(1)}, f32[3,1024]{1,0:T(4,128)S(1)}, u32[]{:S(2)}, u32[]{:S(2)}) collective-permute-start(f32[3,1024]{1,0:T(4,128)S(1)} %reshape.207), channel_id=1, source_target_pairs={{0,1},{1,2},{2,3},{3,0},{4,5},{5,6},{6,7},{7,4},{8,9},{9,10},{10,1... | collective-permute-start | bytes 36872 | tf_op jit(solution)/shard_map/while/body/eval_jaxpr/ppermute | solution.py:143
  111.8 1.5 collective-permute-start
  125.6 11.9 %collective-permute-start.1 = (f32[3,1024]{1,0:T(4,128)S(1)}, f32[3,1024]{1,0:T(4,128)S(1)}, u32[]{:S(2)}, u32[]{:S(2)}) collective-permute-start(f32[3,1024]{1,0:T(4,128)S(1)} %reshape.207), channel_id=1, source_target_pairs={{0,1},{1,2},{2,3},{3,0},{4,5},{5,6},{6,7},{7,4},{8,9},{9,10},{10,1... | collective-permute-start | bytes 36872 | tf_op jit(solution)/shard_map/while/body/eval_jaxpr/ppermute | solution.py:143
  139.2 25.7 %all-to-all-start = ((f32[64,1,384]{2,1,0:T(1,128)}), f32[64,1,384]{2,1,0:T(1,128)S(1)}, u32[]{:S(2)}, u32[]{:S(2)}) async-start(f32[64,1,384]{2,1,0:T(1,128)} %reshape.194), calls=%async_computation | async-start | bytes 196608 | tf_op jit(solution)/shard_map/all_to_all | solution.py:163
  168.0 15.8 %all-to-all-start.1 = ((f32[64,1,384]{2,1,0:T(1,128)}), f32[64,1,384]{2,1,0:T(1,128)S(1)}, u32[]{:S(2)}, u32[]{:S(2)}) async-start(f32[64,1,384]{2,1,0:T(1,128)} %reshape.196), calls=%async_computation.1 | async-start | bytes 196608 | tf_op jit(solution)/shard_map/all_to_all | solution.py:165

commit v6 on v5

--- a/solution.py
+++ b/solution.py
@@ -64,11 +64,12 @@
 def pair_kernel(tiles_ref, count_ref, ext_ref, prm_ref, force_ref, en_ref,
                 xcol_ref, pcol_ref, xrow_ref, prow_ref, fcol_ref, frow_ref):
     pick, place, twice = spread_masks()
+    owned = xcol_ref.shape[1]
     for c in range(3):
-        xcol_ref[c] = to_columns(ext_ref[c], pick, place)
+        xcol_ref[c] = to_columns(ext_ref[c, :owned], pick, place)
         xrow_ref[c] = split_dot(ext_ref[c], twice, ((1,), (0,)))
     for c in range(2):
-        pcol_ref[c] = to_columns(prm_ref[c], pick, place)
+        pcol_ref[c] = to_columns(prm_ref[c, :owned], pick, place)
         prow_ref[c] = split_dot(prm_ref[2 * c], twice, ((1,), (0,)))
     fcol_ref[...] = jnp.zeros(fcol_ref.shape, jnp.float32)
     frow_ref[...] = jnp.zeros(frow_ref.shape, jnp.float32)
@@ -109,7 +110,8 @@
             frow_ref[c], twice, (((1,), (1,)), ((), ())),
             precision=exact, preferred_element_type=jnp.float32,
         )
-        force_ref[c] = from_columns(fcol_ref[c], pick, place) + f_j
+        force_ref[c, :owned] = from_columns(fcol_ref[c], pick, place) + f_j[:owned]
+        force_ref[c, owned:] = f_j[owned:]
 
 
 def slab_pairs(extended, prm, tiles, count):
@@ -125,11 +127,11 @@
         in_specs=[smem, smem, vmem, vmem],
         out_specs=(vmem, vmem),
         scratch_shapes=[
-            pltpu.VMEM((3, width, HALF, 2 * CL), jnp.float32),
-            pltpu.VMEM((2, width, HALF, 2 * CL), jnp.float32),
+            pltpu.VMEM((3, CD, HALF, 2 * CL), jnp.float32),
+            pltpu.VMEM((2, CD, HALF, 2 * CL), jnp.float32),
             pltpu.VMEM((3, width, 2 * CL), jnp.float32),
             pltpu.VMEM((2, width, 2 * CL), jnp.float32),
-            pltpu.VMEM((3, width, HALF, 2 * CL), jnp.float32),
+            pltpu.VMEM((3, CD, HALF, 2 * CL), jnp.float32),
             pltpu.VMEM((3, width, 2 * CL), jnp.float32),
         ],
         compiler_params=pltpu.CompilerParams(vmem_limit_bytes=48 * 1024 * 1024),
@@ -265,11 +267,21 @@
     coords, speeds, forces, energy = lax.fori_loop(
         0, STEPS, verlet_step, (coords, speeds, forces, energy)
     )
-    total_energy = lax.psum(energy, "slab")
+    total_energy = slab_sum(energy)
     potential = (total_energy / (atoms_here * lax.axis_size("slab"))).reshape(1)
     state = jnp.concatenate([coords, speeds], 0)
     swapped = exchange(state, swap_pairs)
     return (swapped[:3][None], swapped[3:][None], potential)
+
+
+def slab_sum(value):
+    count = lax.axis_size("slab")
+    stride = 1
+    while stride < count:
+        pairs = [(source, source ^ stride) for source in range(count)]
+        value = value + lax.ppermute(value, "slab", pairs)
+        stride *= 2
+    return value
 
 
 def solution(mesh):

time: 190 us -> 181 us (0.953)
  waiting for transfers between devices: 18.7 us -> 77.2 us
  starting transfers between devices: 73.7 us -> 28.3 us
  Pallas kernels: 59.7 us -> 47 us
  blocking collectives: 10.5 us -> 0 us
    ppermute x11, waiting for transfers between devices: 8.47 us -> 61.7 us  [from_behind(): return lax.ppermute(value, axis, pairs)]
    ppermute x11, starting transfers between devices: 53.5 us -> 9.71 us  [from_behind(): return lax.ppermute(value, axis, pairs)]
    pallas_call x5, Pallas kernels: 59.7 us -> 47 us  [slab_pairs(): pl.pallas_call(pair_kernel, out_shape=(jax.ShapeDtypeStruct((3, width, CL...]
    psum x1 -> x0, blocking collectives: 10.5 us -> none  [local(): total_energy = lax.psum(energy, 'slab')]
    all_to_all x1, starting transfers between devices: 15.5 us -> 10.1 us  [exchange(): spread = lax.all_to_all(chunks, 'rep', 0, 0, tiled=True)]
    ppermute x0 -> x2, waiting for transfers between devices: none -> 5.29 us  [slab_sum(): value = value + lax.ppermute(value, 'slab', pairs)]
    ppermute x0 -> x2, starting transfers between devices: none -> 3.88 us  [slab_sum(): value = value + lax.ppermute(value, 'slab', pairs)]
  transfers between devices with their start and end apart: 13 -> 15, of which waited for: 10 -> 12; matrix products, arithmetic and copies ran while one was open for 2% -> 2% of each run, Pallas kernels for 0% -> 0%
where the time goes in v6:
time: 181 us; the launch traced here: 179 us
  waiting for transfers between devices  77.2 us (43%)
  Pallas kernels  47 us (26%)
  starting transfers between devices  28.3 us (16%)
  local copies, waits for them, and re-layouts  11.5 us (6%)
  other arithmetic  6.11 us (3%)
  between operations  5.12 us (3%)
  matrix products  3.03 us (2%)
    ppermute x11, waiting for transfers between devices, from_behind(): return lax.ppermute(value, axis, pairs)  61.7 us
    pallas_call x5, Pallas kernels, slab_pairs(): pl.pallas_call(pair_kernel, out_shape=(jax.ShapeDtypeStruct((3, width, CL...  47 us
    all_to_all x1, waiting for transfers between devices, exchange(): spread = lax.all_to_all(chunks, 'rep', 0, 0, tiled=True)  10.2 us
    all_to_all x1, starting transfers between devices, exchange(): spread = lax.all_to_all(chunks, 'rep', 0, 0, tiled=True)  10.1 us
    ppermute x11, starting transfers between devices, from_behind(): return lax.ppermute(value, axis, pairs)  9.71 us
    ppermute x2, waiting for transfers between devices, slab_sum(): value = value + lax.ppermute(value, 'slab', pairs)  5.29 us
    all_to_all x1, starting transfers between devices, exchange(): gathered = lax.all_to_all(routed, 'rep', 0, 0, tiled=True)  4.62 us
    unnamed x25, local copies, waits for them, and re-layouts  4.41 us
  transfers between devices with their start and end apart: 15, of which 12 were waited for; matrix products, arithmetic and copies ran while one was open for 2% of the time, Pallas kernels for 0%

profile of v6, /device:TPU:0, one launch (start us, length us, event | category | flops | bytes accessed | tf_op | source)
XLA Modules:
  0.0 178.6 jit_solution(4838465601468201165)
XLA Ops:
  0.6 0.8 stack.24
  1.5 0.7 copy-done.2
  2.4 4.9 %collective-permute-start.3 = (f32[2,1024]{1,0:T(2,128)S(1)}, f32[2,1024]{1,0:T(2,128)S(1)}, u32[]{:S(2)}, u32[]{:S(2)}) collective-permute-start(f32[2,1024]{1,0:T(2,128)S(1)} %reshape.156), channel_id=1, source_target_pairs={{0,3},{1,0},{2,1},{3,2},{4,7},{5,4},{6,5},{7,6},{8,11},{9,8},{10,9... | collective-permute-start | bytes 24584 | tf_op jit(solution)/shard_map/ppermute | solution.py:145
  7.9 0.7 collective-permute-start.2
  9.0 0.6 copy-done.4
  11.4 0.6 copy-done.9
  12.2 8.9 %shard_map.130 = (f32[3,80,64]{2,1,0:T(8,128)S(1)}, f32[32,128]{1,0:T(8,128)S(1)}) custom-call(s32[2,192]{1,0:T(2,128)S(1)} %pad_add_fusion.tiles_ref, s32[1]{0:T(128)} %bitcast.82.count_ref, f32[3,80,64]{2,1,0:T(8,128)S(1)} %pad_maximum_fusion.2.ext_ref, f32[3,80,64]{2,1,0:T(8,128)S(1)} %pad_maximum_fusion.3.prm_ref), custom_call_target="tpu_custom_call" | custom-call | tf_op jit(solution)/shard_map/pallas_call | solution.py:121
  21.1 0.9 collective-permute-start.4
  22.0 0.6 reduce_sum.38
  22.6 9.7 %collective-permute-done.4 = f32[3,1024]{1,0:T(4,128)S(1)} collective-permute-done((f32[3,1024]{1,0:T(4,128)S(1)}, f32[3,1024]{1,0:T(4,128)S(1)}, u32[]{:S(2)}, u32[]{:S(2)}) %collective-permute-start.4) | collective-permute-done | bytes 12320 | tf_op jit(solution)/shard_map/ppermute | solution.py:145
  32.9 0.6 copy-done
  33.5 101.3 %while.17 = (s32[]{:T(128)}, f32[3,4096]{1,0:T(4,128)S(1)}, f32[3,4096]{1,0:T(4,128)S(1)}, f32[3,4096]{1,0:T(4,128)S(1)}, f32[]{:T(128)}, /*index=5*/f32[4096]{0...) while((s32[]{:T(128)}, f32[3,4096]{1,0:T(4,128)S(1)}, ...), condition=%wide.region_7.8_spmd.clone, body=%wide.region_5.0_spmd.clone.sunk | while | flops 4859905 | bytes 1311073 | solution.py:267
  34.0 1.4 collective-permute-done
  35.7 9.5 %eval_jaxpr.1 = (f32[3,80,64]{2,1,0:T(8,128)S(1)}, f32[32,128]{1,0:T(8,128)S(1)}) custom-call(s32[2,192]{1,0:T(2,128)S(1)} %get-tuple-element.234.tiles_ref, s32[1]{0:T(128)} %bitcast.80.count_ref, f32[3,80,64]{2,1,0:T(8,128)S(1)} %pad_maximum_fusion.5.ext_ref, f32[3,80,64]{2,1,0:T(8,128)S(1)} %get-tuple-element.235.prm_ref), custom_call_target="tpu_custom_call" | custom-call | tf_op jit(solution)/shard_map/while/body/eval_jaxpr/pallas_call | solution.py:121
  45.3 0.8 collective-permute-start.1
  46.0 0.6 reduce_sum.43
  46.6 11.6 %collective-permute-done.1 = f32[3,1024]{1,0:T(4,128)S(1)} collective-permute-done((f32[3,1024]{1,0:T(4,128)S(1)}, f32[3,1024]{1,0:T(4,128)S(1)}, u32[]{:S(2)}, u32[]{:S(2)}) %collective-permute-start.1) | collective-permute-done | bytes 12320 | tf_op jit(solution)/shard_map/while/body/eval_jaxpr/ppermute | solution.py:145
  58.3 0.4 fusion.40
  59.4 1.4 collective-permute-done
  61.0 9.5 %eval_jaxpr.1 = (f32[3,80,64]{2,1,0:T(8,128)S(1)}, f32[32,128]{1,0:T(8,128)S(1)}) custom-call(s32[2,192]{1,0:T(2,128)S(1)} %get-tuple-element.234.tiles_ref, s32[1]{0:T(128)} %bitcast.80.count_ref, f32[3,80,64]{2,1,0:T(8,128)S(1)} %pad_maximum_fusion.5.ext_ref, f32[3,80,64]{2,1,0:T(8,128)S(1)} %get-tuple-element.235.prm_ref), custom_call_target="tpu_custom_call" | custom-call | tf_op jit(solution)/shard_map/while/body/eval_jaxpr/pallas_call | solution.py:121
  70.6 0.8 collective-permute-start.1
  71.4 0.6 reduce_sum.43
  72.0 11.6 %collective-permute-done.1 = f32[3,1024]{1,0:T(4,128)S(1)} collective-permute-done((f32[3,1024]{1,0:T(4,128)S(1)}, f32[3,1024]{1,0:T(4,128)S(1)}, u32[]{:S(2)}, u32[]{:S(2)}) %collective-permute-start.1) | collective-permute-done | bytes 12320 | tf_op jit(solution)/shard_map/while/body/eval_jaxpr/ppermute | solution.py:145
  83.6 0.4 fusion.40
  84.7 1.4 collective-permute-done
  86.3 9.5 %eval_jaxpr.1 = (f32[3,80,64]{2,1,0:T(8,128)S(1)}, f32[32,128]{1,0:T(8,128)S(1)}) custom-call(s32[2,192]{1,0:T(2,128)S(1)} %get-tuple-element.234.tiles_ref, s32[1]{0:T(128)} %bitcast.80.count_ref, f32[3,80,64]{2,1,0:T(8,128)S(1)} %pad_maximum_fusion.5.ext_ref, f32[3,80,64]{2,1,0:T(8,128)S(1)} %get-tuple-element.235.prm_ref), custom_call_target="tpu_custom_call" | custom-call | tf_op jit(solution)/shard_map/while/body/eval_jaxpr/pallas_call | solution.py:121
  95.9 0.8 collective-permute-start.1
  96.7 0.6 reduce_sum.43
  97.3 11.6 %collective-permute-done.1 = f32[3,1024]{1,0:T(4,128)S(1)} collective-permute-done((f32[3,1024]{1,0:T(4,128)S(1)}, f32[3,1024]{1,0:T(4,128)S(1)}, u32[]{:S(2)}, u32[]{:S(2)}) %collective-permute-start.1) | collective-permute-done | bytes 12320 | tf_op jit(solution)/shard_map/while/body/eval_jaxpr/ppermute | solution.py:145
  110.0 1.4 collective-permute-done
  111.6 9.5 %eval_jaxpr.1 = (f32[3,80,64]{2,1,0:T(8,128)S(1)}, f32[32,128]{1,0:T(8,128)S(1)}) custom-call(s32[2,192]{1,0:T(2,128)S(1)} %get-tuple-element.234.tiles_ref, s32[1]{0:T(128)} %bitcast.80.count_ref, f32[3,80,64]{2,1,0:T(8,128)S(1)} %pad_maximum_fusion.5.ext_ref, f32[3,80,64]{2,1,0:T(8,128)S(1)} %get-tuple-element.235.prm_ref), custom_call_target="tpu_custom_call" | custom-call | tf_op jit(solution)/shard_map/while/body/eval_jaxpr/pallas_call | solution.py:121
  121.3 0.8 collective-permute-start.1
  122.0 0.6 reduce_sum.43
  122.6 11.6 %collective-permute-done.1 = f32[3,1024]{1,0:T(4,128)S(1)} collective-permute-done((f32[3,1024]{1,0:T(4,128)S(1)}, f32[3,1024]{1,0:T(4,128)S(1)}, u32[]{:S(2)}, u32[]{:S(2)}) %collective-permute-start.1) | collective-permute-done | bytes 12320 | tf_op jit(solution)/shard_map/while/body/eval_jaxpr/ppermute | solution.py:145
  135.1 0.8 reshape.194
  135.9 10.1 %all-to-all-start = ((f32[64,1,384]{2,1,0:T(1,128)}), f32[64,1,384]{2,1,0:T(1,128)S(1)}, u32[]{:S(2)}, u32[]{:S(2)}) async-start(f32[64,1,384]{2,1,0:T(1,128)} %reshape.194), calls=%async_computation | async-start | bytes 196608 | tf_op jit(solution)/shard_map/all_to_all | solution.py:165
  146.0 10.2 %all-to-all-done = f32[64,1,384]{2,1,0:T(1,128)S(1)} async-done(((f32[64,1,384]{2,1,0:T(1,128)}), f32[64,1,384]{2,1,0:T(1,128)S(1)}, u32[]{:S(2)}, u32[]{:S(2)}) %all-to-all-start) | async-done | bytes 98336 | tf_op jit(solution)/shard_map/all_to_all | solution.py:165
  156.2 0.5 broadcast.55
  156.7 0.9 reduce.11
  157.7 0.6 gather_fusion
  158.5 0.8 reshape.196
  159.3 4.6 %all-to-all-start.1 = ((f32[64,1,384]{2,1,0:T(1,128)}), f32[64,1,384]{2,1,0:T(1,128)S(1)}, u32[]{:S(2)}, u32[]{:S(2)}) async-start(f32[64,1,384]{2,1,0:T(1,128)} %reshape.196), calls=%async_computation.1 | async-start | bytes 196608 | tf_op jit(solution)/shard_map/all_to_all | solution.py:167
  164.0 1.4 collective-permute-done.5
  166.6 3.8 %collective-permute-start.6 = (f32[]{:T(128)}, f32[]{:T(128)}, u32[]{:S(2)}, u32[]{:S(2)}) collective-permute-start(f32[]{:T(128)} %add.87), channel_id=1, source_target_pairs={{0,2},{1,3},{2,0},{3,1},{4,6},{5,7},{6,4},{7,5},{8,10},{9,11},{10,... | collective-permute-start | bytes 20 | tf_op jit(solution)/shard_map/ppermute | solution.py:282
  170.4 3.9 %collective-permute-done.6 = f32[]{:T(128)} collective-permute-done((f32[]{:T(128)}, f32[]{:T(128)}, u32[]{:S(2)}, u32[]{:S(2)}) %collective-permute-start.6) | collective-permute-done | bytes 36 | tf_op jit(solution)/shard_map/ppermute | solution.py:282
  174.9 0.9 reduce.12
  175.9 0.7 broadcast_in_dim.44
  176.7 0.7 broadcast_in_dim.45
  (124 shorter events, 7.9 us)
Async XLA Ops:
  0.6 0.8 copy-start.3
  1.5 0.7 copy-start.2
  2.2 5.2 %copy-start.1 = (f32[1,3,4096]{2,0,1:T(1,128)S(1)}, f32[1,3,4096]{2,0,1:T(1,128)}, u32[]{:S(2)}) copy-start(f32[1,3,4096]{2,0,1:T(1,128)} %param.13) | copy-start | bytes 147460
  2.4 8.6 %collective-permute-start.3 = (f32[2,1024]{1,0:T(2,128)S(1)}, f32[2,1024]{1,0:T(2,128)S(1)}, u32[]{:S(2)}, u32[]{:S(2)}) collective-permute-start(f32[2,1024]{1,0:T(2,128)S(1)} %reshape.156), channel_id=1, source_target_pairs={{0,3},{1,0},{2,1},{3,2},{4,7},{5,4},{6,5},{7,6},{8,11},{9,8},{10,9... | collective-permute-start | bytes 24584 | tf_op jit(solution)/shard_map/ppermute | solution.py:145
  7.6 1.0 copy-start.8
  7.6 1.2 copy-start.7
  7.8 1.0 copy-start.5
  7.9 3.4 %collective-permute-start.2 = (f32[3,1024]{1,0:T(4,128)S(1)}, f32[3,1024]{1,0:T(4,128)S(1)}, u32[]{:S(2)}, u32[]{:S(2)}) collective-permute-start(f32[3,1024]{1,0:T(4,128)S(1)} %reshape.154), channel_id=1, source_target_pairs={{0,3},{1,0},{2,1},{3,2},{4,7},{5,4},{6,5},{7,6},{8,11},{9,8},{10,9... | collective-permute-start | bytes 36872 | tf_op jit(solution)/shard_map/ppermute | solution.py:145
  9.0 0.7 copy-start.4
  11.3 0.7 copy-start.9
  21.1 11.2 %collective-permute-start.4 = (f32[3,1024]{1,0:T(4,128)S(1)}, f32[3,1024]{1,0:T(4,128)S(1)}, u32[]{:S(2)}, u32[]{:S(2)}) collective-permute-start(f32[3,1024]{1,0:T(4,128)S(1)} %reshape.157), channel_id=1, source_target_pairs={{0,1},{1,2},{2,3},{3,0},{4,5},{5,6},{6,7},{7,4},{8,9},{9,10},{10,1... | collective-permute-start | bytes 36872 | tf_op jit(solution)/shard_map/ppermute | solution.py:145
  32.7 0.7 copy-start
  32.9 0.7 copy-start.6
  34.0 1.5 collective-permute-start
  45.3 12.9 %collective-permute-start.1 = (f32[3,1024]{1,0:T(4,128)S(1)}, f32[3,1024]{1,0:T(4,128)S(1)}, u32[]{:S(2)}, u32[]{:S(2)}) collective-permute-start(f32[3,1024]{1,0:T(4,128)S(1)} %reshape.207), channel_id=1, source_target_pairs={{0,1},{1,2},{2,3},{3,0},{4,5},{5,6},{6,7},{7,4},{8,9},{9,10},{10,1... | collective-permute-start | bytes 36872 | tf_op jit(solution)/shard_map/while/body/eval_jaxpr/ppermute | solution.py:145
  59.3 1.5 collective-permute-start
  70.6 12.9 %collective-permute-start.1 = (f32[3,1024]{1,0:T(4,128)S(1)}, f32[3,1024]{1,0:T(4,128)S(1)}, u32[]{:S(2)}, u32[]{:S(2)}) collective-permute-start(f32[3,1024]{1,0:T(4,128)S(1)} %reshape.207), channel_id=1, source_target_pairs={{0,1},{1,2},{2,3},{3,0},{4,5},{5,6},{6,7},{7,4},{8,9},{9,10},{10,1... | collective-permute-start | bytes 36872 | tf_op jit(solution)/shard_map/while/body/eval_jaxpr/ppermute | solution.py:145
  84.7 1.5 collective-permute-start
  95.9 12.9 %collective-permute-start.1 = (f32[3,1024]{1,0:T(4,128)S(1)}, f32[3,1024]{1,0:T(4,128)S(1)}, u32[]{:S(2)}, u32[]{:S(2)}) collective-permute-start(f32[3,1024]{1,0:T(4,128)S(1)} %reshape.207), channel_id=1, source_target_pairs={{0,1},{1,2},{2,3},{3,0},{4,5},{5,6},{6,7},{7,4},{8,9},{9,10},{10,1... | collective-permute-start | bytes 36872 | tf_op jit(solution)/shard_map/while/body/eval_jaxpr/ppermute | solution.py:145
  110.0 1.5 collective-permute-start
  121.3 12.9 %collective-permute-start.1 = (f32[3,1024]{1,0:T(4,128)S(1)}, f32[3,1024]{1,0:T(4,128)S(1)}, u32[]{:S(2)}, u32[]{:S(2)}) collective-permute-start(f32[3,1024]{1,0:T(4,128)S(1)} %reshape.207), channel_id=1, source_target_pairs={{0,1},{1,2},{2,3},{3,0},{4,5},{5,6},{6,7},{7,4},{8,9},{9,10},{10,1... | collective-permute-start | bytes 36872 | tf_op jit(solution)/shard_map/while/body/eval_jaxpr/ppermute | solution.py:145
  135.9 20.4 %all-to-all-start = ((f32[64,1,384]{2,1,0:T(1,128)}), f32[64,1,384]{2,1,0:T(1,128)S(1)}, u32[]{:S(2)}, u32[]{:S(2)}) async-start(f32[64,1,384]{2,1,0:T(1,128)} %reshape.194), calls=%async_computation | async-start | bytes 196608 | tf_op jit(solution)/shard_map/all_to_all | solution.py:165
  159.3 15.6 %all-to-all-start.1 = ((f32[64,1,384]{2,1,0:T(1,128)}), f32[64,1,384]{2,1,0:T(1,128)S(1)}, u32[]{:S(2)}, u32[]{:S(2)}) async-start(f32[64,1,384]{2,1,0:T(1,128)} %reshape.196), calls=%async_computation.1 | async-start | bytes 196608 | tf_op jit(solution)/shard_map/all_to_all | solution.py:167
  163.9 1.5 collective-permute-start.5
  166.6 7.7 %collective-permute-start.6 = (f32[]{:T(128)}, f32[]{:T(128)}, u32[]{:S(2)}, u32[]{:S(2)}) collective-permute-start(f32[]{:T(128)} %add.87), channel_id=1, source_target_pairs={{0,2},{1,3},{2,0},{3,1},{4,6},{5,7},{6,4},{7,5},{8,10},{9,11},{10,... | collective-permute-start | bytes 20 | tf_op jit(solution)/shard_map/ppermute | solution.py:282

commit v7 on v6

--- a/solution.py
+++ b/solution.py
@@ -220,47 +220,51 @@
     halo_clusters,
     swap_pairs,
 ):
-    coords = positions[0]
-    speeds = velocities[0]
     ham_scale = scaling[0]
-    firsts_flat = tile_pairs[0, 0]
-    seconds_flat = tile_pairs[0, 1]
+    tile_list = tile_pairs[0]
     live_count = tile_counts[0, 0]
     halo_index = halo_clusters[0]
-    atoms_here = coords.shape[1]
+    atoms_here = positions.shape[2]
+    own = jnp.concatenate(
+        [
+            positions[0].reshape(3, CD, CL),
+            velocities[0].reshape(3, CD, CL),
+            jnp.stack([inv_mass, strength, charge], 0).reshape(3, CD, CL),
+        ],
+        0,
+    )
+    sent = jnp.take(own, halo_index, axis=1)
+    got = from_behind(sent, "slab", -1)
+    full = jnp.concatenate([own, got], 1)
+    coords = full[0:3]
+    speeds = full[3:6]
+    inv_mass_all = full[6]
+    strength_all = full[7]
+    charge_all = full[8]
+    cluster_ids = lax.broadcasted_iota(jnp.int32, (3, CD + HALO, CL), 1)
+    lift_all = jnp.where(
+        (cluster_ids >= CD) & (lax.broadcasted_iota(jnp.int32, (3, CD + HALO, CL), 0) == 2),
+        slab_width,
+        0.0,
+    ).astype(jnp.float32)
+    param_all = jnp.stack([strength_all, ham_scale * charge_all, charge_all], 0)
     halo_table = select_table(halo_index, CD)
-    params = jnp.stack([strength, charge], 0).reshape(2, CD, CL)
-    sent_params = jnp.einsum("hc,pck->phk", halo_table, params, precision=exact).reshape(
-        2, HALO * CL
-    )
-    got_params = from_behind(sent_params, "slab", -1).reshape(2, HALO, CL)
-    strength_all = jnp.concatenate([params[0], got_params[0]], 0)
-    charge_all = jnp.concatenate([params[1], got_params[1]], 0)
-    lift = jnp.array([0.0, 0.0, slab_width], jnp.float32)[:, None]
-    param_all = jnp.stack([strength_all, ham_scale * charge_all, charge_all], 0)
-    tile_list = jnp.stack([firsts_flat, seconds_flat], 0)
 
     def evaluate(coords_now):
-        blocks = coords_now.reshape(3, CD, CL)
-        sent_coords = jnp.einsum("hc,xck->xhk", halo_table, blocks, precision=exact).reshape(
-            3, HALO * CL
-        )
-        from_above = from_behind(sent_coords, "slab", -1) + lift
-        extended = jnp.concatenate([blocks, from_above.reshape(3, HALO, CL)], 1)
+        extended = coords_now + lift_all
         forces, energy = slab_pairs(extended, param_all, tile_list, live_count)
-        returned = from_behind(forces[:, CD:].reshape(3, HALO * CL), "slab", 1)
-        back_home = jnp.einsum(
-            "hc,xhk->xck", halo_table, returned.reshape(3, HALO, CL), precision=exact
-        )
-        local_forces = forces[:, :CD] + back_home
-        return (local_forces.reshape(3, atoms_here), energy)
+        owned_part = jnp.take(forces[:, :CD], halo_index, axis=1)
+        returned, from_owner = trade_halo(forces[:, CD:], owned_part)
+        back_home = jnp.einsum("hc,xhk->xck", halo_table, returned, precision=exact)
+        total = jnp.concatenate([forces[:, :CD] + back_home, forces[:, CD:] + from_owner], 1)
+        return (total, energy)
 
     def verlet_step(step_idx, carry):
         coords, speeds, forces, energy = carry
-        speeds = speeds + half_step * forces * inv_mass
+        speeds = speeds + half_step * forces * inv_mass_all
         coords = coords + time_step * speeds
         forces, energy = evaluate(coords)
-        speeds = speeds + half_step * forces * inv_mass
+        speeds = speeds + half_step * forces * inv_mass_all
         return (coords, speeds, forces, energy)
 
     forces, energy = evaluate(coords)
@@ -269,9 +273,24 @@
     )
     total_energy = slab_sum(energy)
     potential = (total_energy / (atoms_here * lax.axis_size("slab"))).reshape(1)
-    state = jnp.concatenate([coords, speeds], 0)
+    state = jnp.concatenate(
+        [coords[:, :CD].reshape(3, atoms_here), speeds[:, :CD].reshape(3, atoms_here)], 0
+    )
     swapped = exchange(state, swap_pairs)
     return (swapped[:3][None], swapped[3:][None], potential)
+
+
+def trade_halo(up_part, down_part):
+    count = lax.axis_size("slab")
+    if count < 3:
+        return (from_behind(up_part, "slab", 1), from_behind(down_part, "slab", -1))
+    me = lax.axis_index("slab")
+    above = (me + 1) % count
+    below = (me - 1) % count
+    slots = jnp.arange(count, dtype=jnp.int32).reshape((count,) + (1,) * up_part.ndim)
+    payload = jnp.where(slots == above, up_part[None], jnp.where(slots == below, down_part[None], 0.0))
+    got = lax.all_to_all(payload, "slab", 0, 0, tiled=True)
+    return (jnp.take(got, below, axis=0), jnp.take(got, above, axis=0))
 
 
 def slab_sum(value):

time: 181 us -> 212 us (1.17)
  Pallas kernels: 47 us -> 76.2 us
  waiting for transfers between devices: 77.2 us -> 53.7 us
  local copies, waits for them, and re-layouts: 11.5 us -> 21 us
  starting transfers between devices: 28.3 us -> 37.1 us
  other arithmetic: 6.11 us -> 13 us
    ppermute x11 -> x1, waiting for transfers between devices: 61.7 us -> 0.01 us  [from_behind(): return lax.ppermute(value, axis, pairs)]
    all_to_all x0 -> x5, waiting for transfers between devices: none -> 36 us  [trade_halo(): got = lax.all_to_all(payload, 'slab', 0, 0, tiled=True)]
    pallas_call x5, Pallas kernels: 47 us -> 76.2 us  [slab_pairs(): pl.pallas_call(pair_kernel, out_shape=(jax.ShapeDtypeStruct((3, width, CL...]
    all_to_all x0 -> x5, starting transfers between devices: none -> 16.6 us  [trade_halo(): got = lax.all_to_all(payload, 'slab', 0, 0, tiled=True)]
    ppermute x11 -> x1, starting transfers between devices: 9.71 us -> 4.96 us  [from_behind(): return lax.ppermute(value, axis, pairs)]
    all_to_all x0 -> x5, other arithmetic: none -> 3.86 us  [trade_halo(): got = lax.all_to_all(payload, 'slab', 0, 0, tiled=True)]
    gather x0 -> x6, local copies, waits for them, and re-layouts: none -> 3.5 us  [the longest x5 2.94 us: evaluate(): owned_part = jnp.take(forces[:, :CD], halo_index, axis=1)]
    while x4 -> x10, local copies, waits for them, and re-layouts: 0.05 us -> 3.48 us
  transfers between devices with their start and end apart: 15 -> 10, of which waited for: 12 -> 8; matrix products, arithmetic and copies ran while one was open for 2% -> 2% of each run, Pallas kernels for 0% -> 0%
where the time goes in v7:
time: 212 us; the launch traced here: 209 us
  Pallas kernels  76.2 us (36%)
  waiting for transfers between devices  53.7 us (25%)
  starting transfers between devices  37.1 us (18%)
  local copies, waits for them, and re-layouts  21 us (10%)
  other arithmetic  13 us (6%)
  between operations  5.23 us (2%)
    pallas_call x5, Pallas kernels, slab_pairs(): pl.pallas_call(pair_kernel, out_shape=(jax.ShapeDtypeStruct((3, width, CL...  76.2 us
    all_to_all x5, waiting for transfers between devices, trade_halo(): got = lax.all_to_all(payload, 'slab', 0, 0, tiled=True)  36 us
    all_to_all x5, starting transfers between devices, trade_halo(): got = lax.all_to_all(payload, 'slab', 0, 0, tiled=True)  16.6 us
    all_to_all x1, waiting for transfers between devices, exchange(): spread = lax.all_to_all(chunks, 'rep', 0, 0, tiled=True)  10.2 us
    all_to_all x1, starting transfers between devices, exchange(): spread = lax.all_to_all(chunks, 'rep', 0, 0, tiled=True)  9.38 us
    ppermute x2, waiting for transfers between devices, slab_sum(): value = value + lax.ppermute(value, 'slab', pairs)  7.54 us
    unnamed x26, local copies, waits for them, and re-layouts  7.28 us
    ppermute x1, starting transfers between devices, from_behind(): return lax.ppermute(value, axis, pairs)  4.96 us
  transfers between devices with their start and end apart: 10, of which 8 were waited for; matrix products, arithmetic and copies ran while one was open for 2% of the time, Pallas kernels for 0%

profile of v7, /device:TPU:0, one launch (start us, length us, event | category | flops | bytes accessed | tf_op | source)
XLA Modules:
  0.0 208.8 jit_solution(9866339723940383770)
XLA Ops:
  0.6 0.7 fusion.31
  1.4 0.9 reduce
  2.4 0.8 copy-done.2
  6.5 5.0 %collective-permute-start = (f32[9,16,64]{2,1,0:T(8,128)S(1)}, f32[9,16,64]{2,1,0:T(8,128)S(1)}, u32[]{:S(2)}, u32[]{:S(2)}) collective-permute-start(f32[9,16,64]{2,1,0:T(8,128)S(1)} %fusion.18), channel_id=1, source_target_pairs={{0,3},{1,0},{2,1},{3,2},{4,7},{5,4},{6,5},{7,6},{8,11},{9,8},{10,9... | collective-permute-start | bytes 110600 | tf_op jit(solution)/shard_map/ppermute | solution.py:145
  11.5 0.7 copy-done.7
  13.9 0.7 copy-done.1
  14.5 14.7 %shard_map.121 = (f32[3,80,64]{2,1,0:T(8,128)S(1)}, f32[32,128]{1,0:T(8,128)S(1)}) custom-call(s32[2,192]{1,0:T(2,128)S(1)} %bitcast.81, s32[1]{0:T(128)} %bitcast.79.count_ref, f32[3,80,64]{2,1,0:T(8,128)S(1)} %get-tuple-element.273.ext_ref, f32[3,80,64]{2,1,0:T(8,128)S(1)} %get-tuple-element.386.prm_ref), custom_call_target="tpu_custom_call" | custom-call | tf_op jit(solution)/shard_map/pallas_call | solution.py:121
  30.1 0.7 reshape.270
  30.9 3.5 %all-to-all-start.1 = ((f32[4,1,3072]{2,1,0:T(1,128)}), f32[4,1,3072]{2,1,0:T(1,128)S(1)}, u32[]{:S(2)}, u32[]{:S(2)}) async-start(f32[4,1,3072]{2,1,0:T(1,128)} %reshape.270), calls=%async_computation.1 | async-start | bytes 98304 | tf_op jit(solution)/shard_map/all_to_all | solution.py:292
  34.3 0.7 reduce_sum.41
  35.0 7.1 %all-to-all-done.1 = f32[4,1,3072]{2,1,0:T(1,128)S(1)} async-done(((f32[4,1,3072]{2,1,0:T(1,128)}), f32[4,1,3072]{2,1,0:T(1,128)S(1)}, u32[]{:S(2)}, u32[]{:S(2)}) %all-to-all-start.1) | async-done | bytes 49184 | tf_op jit(solution)/shard_map/all_to_all | solution.py:292
  42.6 0.8 reduce.3
  43.8 121.1 %while.21 = (s32[]{:T(128)}, f32[3,80,64]{2,1,0:T(8,128)S(1)}, f32[3,80,64]{2,1,0:T(8,128)S(1)}, f32[3,80,64]{2,1,0:T(8,128)S(1)}, f32[]{:T(128)}, /*index=5*/f3...) while((s32[]{:T(128)}, f32[3,80,64]{2,1,0:T(8,128)S(1)}, ...), condition=%wide.region_7.10_spmd.clone.clone, body=%wide.region_5.9_spmd.clone.clone.sunk | while | flops 2605247 | bytes 1738290 | solution.py:271
  44.0 15.4 %eval_jaxpr.4 = (f32[3,80,64]{2,1,0:T(8,128)S(1)}, f32[32,128]{1,0:T(8,128)S(1)}) custom-call(s32[2,192]{1,0:T(2,128)S(1)} %get-tuple-element.425.tiles_ref, s32[1]{0:T(128)} %bitcast.77.count_ref, f32[3,80,64]{2,1,0:T(8,128)S(1)} %get-tuple-element.371.ext_ref, f32[3,80,64]{2,1,0:T(8,128)S(1)} %get-tuple-element.426.prm_ref), custom_call_target="tpu_custom_call" | custom-call | tf_op jit(solution)/shard_map/while/body/eval_jaxpr/pallas_call | solution.py:121
  60.3 0.7 reshape.282
  61.0 3.3 %all-to-all-start = ((f32[4,1,3072]{2,1,0:T(1,128)}), f32[4,1,3072]{2,1,0:T(1,128)S(1)}, u32[]{:S(2)}, u32[]{:S(2)}) async-start(f32[4,1,3072]{2,1,0:T(1,128)} %reshape.282), calls=%async_computation | async-start | bytes 98304 | tf_op jit(solution)/shard_map/while/body/eval_jaxpr/all_to_all | solution.py:292
  64.3 0.7 reduce_sum.47
  65.0 7.2 %all-to-all-done = f32[4,1,3072]{2,1,0:T(1,128)S(1)} async-done(((f32[4,1,3072]{2,1,0:T(1,128)}), f32[4,1,3072]{2,1,0:T(1,128)S(1)}, u32[]{:S(2)}, u32[]{:S(2)}) %all-to-all-start) | async-done | bytes 49184 | tf_op jit(solution)/shard_map/while/body/eval_jaxpr/all_to_all | solution.py:292
  72.7 0.8 reduce.7
  74.2 15.4 %eval_jaxpr.4 = (f32[3,80,64]{2,1,0:T(8,128)S(1)}, f32[32,128]{1,0:T(8,128)S(1)}) custom-call(s32[2,192]{1,0:T(2,128)S(1)} %get-tuple-element.425.tiles_ref, s32[1]{0:T(128)} %bitcast.77.count_ref, f32[3,80,64]{2,1,0:T(8,128)S(1)} %get-tuple-element.371.ext_ref, f32[3,80,64]{2,1,0:T(8,128)S(1)} %get-tuple-element.426.prm_ref), custom_call_target="tpu_custom_call" | custom-call | tf_op jit(solution)/shard_map/while/body/eval_jaxpr/pallas_call | solution.py:121
  90.6 0.7 reshape.282
  91.3 3.3 %all-to-all-start = ((f32[4,1,3072]{2,1,0:T(1,128)}), f32[4,1,3072]{2,1,0:T(1,128)S(1)}, u32[]{:S(2)}, u32[]{:S(2)}) async-start(f32[4,1,3072]{2,1,0:T(1,128)} %reshape.282), calls=%async_computation | async-start | bytes 98304 | tf_op jit(solution)/shard_map/while/body/eval_jaxpr/all_to_all | solution.py:292
  95.2 7.2 %all-to-all-done = f32[4,1,3072]{2,1,0:T(1,128)S(1)} async-done(((f32[4,1,3072]{2,1,0:T(1,128)}), f32[4,1,3072]{2,1,0:T(1,128)S(1)}, u32[]{:S(2)}, u32[]{:S(2)}) %all-to-all-start) | async-done | bytes 49184 | tf_op jit(solution)/shard_map/while/body/eval_jaxpr/all_to_all | solution.py:292
  103.0 0.8 reduce.7
  104.5 15.4 %eval_jaxpr.4 = (f32[3,80,64]{2,1,0:T(8,128)S(1)}, f32[32,128]{1,0:T(8,128)S(1)}) custom-call(s32[2,192]{1,0:T(2,128)S(1)} %get-tuple-element.425.tiles_ref, s32[1]{0:T(128)} %bitcast.77.count_ref, f32[3,80,64]{2,1,0:T(8,128)S(1)} %get-tuple-element.371.ext_ref, f32[3,80,64]{2,1,0:T(8,128)S(1)} %get-tuple-element.426.prm_ref), custom_call_target="tpu_custom_call" | custom-call | tf_op jit(solution)/shard_map/while/body/eval_jaxpr/pallas_call | solution.py:121
  120.8 0.7 reshape.282
  121.5 3.3 %all-to-all-start = ((f32[4,1,3072]{2,1,0:T(1,128)}), f32[4,1,3072]{2,1,0:T(1,128)S(1)}, u32[]{:S(2)}, u32[]{:S(2)}) async-start(f32[4,1,3072]{2,1,0:T(1,128)} %reshape.282), calls=%async_computation | async-start | bytes 98304 | tf_op jit(solution)/shard_map/while/body/eval_jaxpr/all_to_all | solution.py:292
  125.5 7.2 %all-to-all-done = f32[4,1,3072]{2,1,0:T(1,128)S(1)} async-done(((f32[4,1,3072]{2,1,0:T(1,128)}), f32[4,1,3072]{2,1,0:T(1,128)S(1)}, u32[]{:S(2)}, u32[]{:S(2)}) %all-to-all-start) | async-done | bytes 49184 | tf_op jit(solution)/shard_map/while/body/eval_jaxpr/all_to_all | solution.py:292
  133.2 0.8 reduce.7
  134.8 15.4 %eval_jaxpr.4 = (f32[3,80,64]{2,1,0:T(8,128)S(1)}, f32[32,128]{1,0:T(8,128)S(1)}) custom-call(s32[2,192]{1,0:T(2,128)S(1)} %get-tuple-element.425.tiles_ref, s32[1]{0:T(128)} %bitcast.77.count_ref, f32[3,80,64]{2,1,0:T(8,128)S(1)} %get-tuple-element.371.ext_ref, f32[3,80,64]{2,1,0:T(8,128)S(1)} %get-tuple-element.426.prm_ref), custom_call_target="tpu_custom_call" | custom-call | tf_op jit(solution)/shard_map/while/body/eval_jaxpr/pallas_call | solution.py:121
  151.1 0.7 reshape.282
  151.8 3.3 %all-to-all-start = ((f32[4,1,3072]{2,1,0:T(1,128)}), f32[4,1,3072]{2,1,0:T(1,128)S(1)}, u32[]{:S(2)}, u32[]{:S(2)}) async-start(f32[4,1,3072]{2,1,0:T(1,128)} %reshape.282), calls=%async_computation | async-start | bytes 98304 | tf_op jit(solution)/shard_map/while/body/eval_jaxpr/all_to_all | solution.py:292
  155.1 0.7 reduce_sum.47
  155.8 7.2 %all-to-all-done = f32[4,1,3072]{2,1,0:T(1,128)S(1)} async-done(((f32[4,1,3072]{2,1,0:T(1,128)}), f32[4,1,3072]{2,1,0:T(1,128)S(1)}, u32[]{:S(2)}, u32[]{:S(2)}) %all-to-all-start) | async-done | bytes 49184 | tf_op jit(solution)/shard_map/while/body/eval_jaxpr/all_to_all | solution.py:292
  163.5 0.8 reduce.7
  165.7 0.9 slice-done
  166.6 0.8 reshape.272
  167.4 9.4 %all-to-all-start.2 = ((f32[64,1,384]{2,1,0:T(1,128)}), f32[64,1,384]{2,1,0:T(1,128)S(1)}, u32[]{:S(2)}, u32[]{:S(2)}) async-start(f32[64,1,384]{2,1,0:T(1,128)} %reshape.272), calls=%async_computation.2 | async-start | bytes 196608 | tf_op jit(solution)/shard_map/all_to_all | solution.py:165
  176.8 10.2 %all-to-all-done.2 = f32[64,1,384]{2,1,0:T(1,128)S(1)} async-done(((f32[64,1,384]{2,1,0:T(1,128)}), f32[64,1,384]{2,1,0:T(1,128)S(1)}, u32[]{:S(2)}, u32[]{:S(2)}) %all-to-all-start.2) | async-done | bytes 98336 | tf_op jit(solution)/shard_map/all_to_all | solution.py:165
  187.1 0.9 reduce.4
  188.8 0.8 reshape.274
  189.6 4.6 %all-to-all-start.3 = ((f32[64,1,384]{2,1,0:T(1,128)}), f32[64,1,384]{2,1,0:T(1,128)S(1)}, u32[]{:S(2)}, u32[]{:S(2)}) async-start(f32[64,1,384]{2,1,0:T(1,128)} %reshape.274), calls=%async_computation.3 | async-start | bytes 196608 | tf_op jit(solution)/shard_map/all_to_all | solution.py:167
  194.3 1.3 collective-permute-done.1
  196.8 1.5 collective-permute-start.2
  198.3 6.2 %collective-permute-done.2 = f32[]{:T(128)} collective-permute-done((f32[]{:T(128)}, f32[]{:T(128)}, u32[]{:S(2)}, u32[]{:S(2)}) %collective-permute-start.2) | collective-permute-done | bytes 36 | tf_op jit(solution)/shard_map/ppermute | solution.py:301
  205.1 0.9 reduce.5
  206.2 0.7 broadcast_in_dim.195
  206.9 0.7 broadcast_in_dim.196
  (143 shorter events, 17.0 us)
Async XLA Ops:
  0.6 0.7 copy-start.3
  2.4 0.8 copy-start.2
  3.4 0.7 copy-start.4
  4.1 0.7 copy-start.5
  4.8 0.7 copy-start.6
  6.5 7.2 %collective-permute-start = (f32[9,16,64]{2,1,0:T(8,128)S(1)}, f32[9,16,64]{2,1,0:T(8,128)S(1)}, u32[]{:S(2)}, u32[]{:S(2)}) collective-permute-start(f32[9,16,64]{2,1,0:T(8,128)S(1)} %fusion.18), channel_id=1, source_target_pairs={{0,3},{1,0},{2,1},{3,2},{4,7},{5,4},{6,5},{7,6},{8,11},{9,8},{10,9... | collective-permute-start | bytes 110600 | tf_op jit(solution)/shard_map/ppermute | solution.py:145
  11.5 0.7 copy-start.7
  13.8 0.7 copy-start.1
  30.9 11.2 %all-to-all-start.1 = ((f32[4,1,3072]{2,1,0:T(1,128)}), f32[4,1,3072]{2,1,0:T(1,128)S(1)}, u32[]{:S(2)}, u32[]{:S(2)}) async-start(f32[4,1,3072]{2,1,0:T(1,128)} %reshape.270), calls=%async_computation.1 | async-start | bytes 98304 | tf_op jit(solution)/shard_map/all_to_all | solution.py:292
  61.0 11.2 %all-to-all-start = ((f32[4,1,3072]{2,1,0:T(1,128)}), f32[4,1,3072]{2,1,0:T(1,128)S(1)}, u32[]{:S(2)}, u32[]{:S(2)}) async-start(f32[4,1,3072]{2,1,0:T(1,128)} %reshape.282), calls=%async_computation | async-start | bytes 98304 | tf_op jit(solution)/shard_map/while/body/eval_jaxpr/all_to_all | solution.py:292
  91.3 11.2 %all-to-all-start = ((f32[4,1,3072]{2,1,0:T(1,128)}), f32[4,1,3072]{2,1,0:T(1,128)S(1)}, u32[]{:S(2)}, u32[]{:S(2)}) async-start(f32[4,1,3072]{2,1,0:T(1,128)} %reshape.282), calls=%async_computation | async-start | bytes 98304 | tf_op jit(solution)/shard_map/while/body/eval_jaxpr/all_to_all | solution.py:292
  121.5 11.2 %all-to-all-start = ((f32[4,1,3072]{2,1,0:T(1,128)}), f32[4,1,3072]{2,1,0:T(1,128)S(1)}, u32[]{:S(2)}, u32[]{:S(2)}) async-start(f32[4,1,3072]{2,1,0:T(1,128)} %reshape.282), calls=%async_computation | async-start | bytes 98304 | tf_op jit(solution)/shard_map/while/body/eval_jaxpr/all_to_all | solution.py:292
  151.8 11.2 %all-to-all-start = ((f32[4,1,3072]{2,1,0:T(1,128)}), f32[4,1,3072]{2,1,0:T(1,128)S(1)}, u32[]{:S(2)}, u32[]{:S(2)}) async-start(f32[4,1,3072]{2,1,0:T(1,128)} %reshape.282), calls=%async_computation | async-start | bytes 98304 | tf_op jit(solution)/shard_map/while/body/eval_jaxpr/all_to_all | solution.py:292
  164.9 0.7 copy-start
  165.7 0.9 slice-start
  167.4 19.6 %all-to-all-start.2 = ((f32[64,1,384]{2,1,0:T(1,128)}), f32[64,1,384]{2,1,0:T(1,128)S(1)}, u32[]{:S(2)}, u32[]{:S(2)}) async-start(f32[64,1,384]{2,1,0:T(1,128)} %reshape.272), calls=%async_computation.2 | async-start | bytes 196608 | tf_op jit(solution)/shard_map/all_to_all | solution.py:165
  189.6 15.5 %all-to-all-start.3 = ((f32[64,1,384]{2,1,0:T(1,128)}), f32[64,1,384]{2,1,0:T(1,128)S(1)}, u32[]{:S(2)}, u32[]{:S(2)}) async-start(f32[64,1,384]{2,1,0:T(1,128)} %reshape.274), calls=%async_computation.3 | async-start | bytes 196608 | tf_op jit(solution)/shard_map/all_to_all | solution.py:167
  194.2 1.4 collective-permute-start.1
  196.8 7.7 %collective-permute-start.2 = (f32[]{:T(128)}, f32[]{:T(128)}, u32[]{:S(2)}, u32[]{:S(2)}) collective-permute-start(f32[]{:T(128)} %add.158), channel_id=1, source_target_pairs={{0,2},{1,3},{2,0},{3,1},{4,6},{5,7},{6,4},{7,5},{8,10},{9,11},{10,... | collective-permute-start | bytes 20 | tf_op jit(solution)/shard_map/ppermute | solution.py:301

commit v8 on v6

--- a/solution.py
+++ b/solution.py
@@ -61,15 +61,29 @@
     return jnp.sum(folded.reshape(width, HALF, CL) * pick[None], axis=1)
 
 
-def pair_kernel(tiles_ref, count_ref, ext_ref, prm_ref, force_ref, en_ref,
-                xcol_ref, pcol_ref, xrow_ref, prow_ref, fcol_ref, frow_ref):
+def column_kernel(prm_ref, pcol_ref):
+    pick, place, twice = spread_masks()
+    owned = pcol_ref.shape[1]
+    for c in range(2):
+        pcol_ref[c] = to_columns(prm_ref[c, :owned], pick, place)
+
+
+def param_columns(prm):
+    return pl.pallas_call(
+        column_kernel,
+        out_shape=jax.ShapeDtypeStruct((2, CD, HALF, 2 * CL), jnp.float32),
+        compiler_params=pltpu.CompilerParams(vmem_limit_bytes=48 * 1024 * 1024),
+    )(prm)
+
+
+def pair_kernel(tiles_ref, count_ref, ext_ref, prm_ref, pcol_ref, force_ref, en_ref,
+                xcol_ref, xrow_ref, prow_ref, fcol_ref, frow_ref):
     pick, place, twice = spread_masks()
     owned = xcol_ref.shape[1]
     for c in range(3):
         xcol_ref[c] = to_columns(ext_ref[c, :owned], pick, place)
         xrow_ref[c] = split_dot(ext_ref[c], twice, ((1,), (0,)))
     for c in range(2):
-        pcol_ref[c] = to_columns(prm_ref[c, :owned], pick, place)
         prow_ref[c] = split_dot(prm_ref[2 * c], twice, ((1,), (0,)))
     fcol_ref[...] = jnp.zeros(fcol_ref.shape, jnp.float32)
     frow_ref[...] = jnp.zeros(frow_ref.shape, jnp.float32)
@@ -114,7 +128,7 @@
         force_ref[c, owned:] = f_j[owned:]
 
 
-def slab_pairs(extended, prm, tiles, count):
+def slab_pairs(extended, prm, pcol, tiles, count):
     width = extended.shape[1]
     smem = pl.BlockSpec(memory_space=pltpu.SMEM)
     vmem = pl.BlockSpec(memory_space=pltpu.VMEM)
@@ -124,18 +138,17 @@
             jax.ShapeDtypeStruct((3, width, CL), jnp.float32),
             jax.ShapeDtypeStruct((HALF, 2 * CL), jnp.float32),
         ),
-        in_specs=[smem, smem, vmem, vmem],
+        in_specs=[smem, smem, vmem, vmem, vmem],
         out_specs=(vmem, vmem),
         scratch_shapes=[
             pltpu.VMEM((3, CD, HALF, 2 * CL), jnp.float32),
-            pltpu.VMEM((2, CD, HALF, 2 * CL), jnp.float32),
             pltpu.VMEM((3, width, 2 * CL), jnp.float32),
             pltpu.VMEM((2, width, 2 * CL), jnp.float32),
             pltpu.VMEM((3, CD, HALF, 2 * CL), jnp.float32),
             pltpu.VMEM((3, width, 2 * CL), jnp.float32),
         ],
         compiler_params=pltpu.CompilerParams(vmem_limit_bytes=48 * 1024 * 1024),
-    )(tiles, count.reshape(1), extended, prm)
+    )(tiles, count.reshape(1), extended, prm, pcol)
     return forces, jnp.sum(acc)
 
 
@@ -238,6 +251,7 @@
     charge_all = jnp.concatenate([params[1], got_params[1]], 0)
     lift = jnp.array([0.0, 0.0, slab_width], jnp.float32)[:, None]
     param_all = jnp.stack([strength_all, ham_scale * charge_all, charge_all], 0)
+    param_cols = param_columns(param_all)
     tile_list = jnp.stack([firsts_flat, seconds_flat], 0)
 
     def evaluate(coords_now):
@@ -247,7 +261,7 @@
         )
         from_above = from_behind(sent_coords, "slab", -1) + lift
         extended = jnp.concatenate([blocks, from_above.reshape(3, HALO, CL)], 1)
-        forces, energy = slab_pairs(extended, param_all, tile_list, live_count)
+        forces, energy = slab_pairs(extended, param_all, param_cols, tile_list, live_count)
         returned = from_behind(forces[:, CD:].reshape(3, HALO * CL), "slab", 1)
         back_home = jnp.einsum(
             "hc,xhk->xck", halo_table, returned.reshape(3, HALO, CL), precision=exact

time: 181 us -> 186 us (1.028)
  waiting for transfers between devices: 77.2 us -> 23.7 us
  starting transfers between devices: 28.3 us -> 80.4 us
  local copies, waits for them, and re-layouts: 11.5 us -> 13.4 us
    ppermute x11, waiting for transfers between devices: 61.7 us -> 7.88 us  [from_behind(): return lax.ppermute(value, axis, pairs)]
    ppermute x11, starting transfers between devices: 9.71 us -> 57.1 us  [from_behind(): return lax.ppermute(value, axis, pairs)]
    all_to_all x1, starting transfers between devices: 10.1 us -> 15.1 us  [exchange(): spread = lax.all_to_all(chunks, 'rep', 0, 0, tiled=True)]
    unnamed x25 -> x13, local copies, waits for them, and re-layouts: 4.41 us -> 2.66 us
  transfers between devices with their start and end apart: 15 -> 15, of which waited for: 12 -> 12; matrix products, arithmetic and copies ran while one was open for 2% -> 5% of each run, Pallas kernels for 0% -> 1%
where the time goes in v8:
time: 186 us; the launch traced here: 183 us
  starting transfers between devices  80.4 us (43%)
  Pallas kernels  48.5 us (26%)
  waiting for transfers between devices  23.7 us (13%)
  local copies, waits for them, and re-layouts  13.4 us (7%)
  other arithmetic  6.91 us (4%)
  between operations  5.11 us (3%)
  matrix products  4.34 us (2%)
    ppermute x11, starting transfers between devices, from_behind(): return lax.ppermute(value, axis, pairs)  57.1 us
    pallas_call x5, Pallas kernels, slab_pairs(): pl.pallas_call(pair_kernel, out_shape=(jax.ShapeDtypeStruct((3, width, CL...  47.5 us
    all_to_all x1, starting transfers between devices, exchange(): spread = lax.all_to_all(chunks, 'rep', 0, 0, tiled=True)  15.1 us
    all_to_all x1, waiting for transfers between devices, exchange(): spread = lax.all_to_all(chunks, 'rep', 0, 0, tiled=True)  10.2 us
    ppermute x11, waiting for transfers between devices, from_behind(): return lax.ppermute(value, axis, pairs)  7.88 us
    ppermute x2, waiting for transfers between devices, slab_sum(): value = value + lax.ppermute(value, 'slab', pairs)  5.65 us
    all_to_all x1, starting transfers between devices, exchange(): gathered = lax.all_to_all(routed, 'rep', 0, 0, tiled=True)  4.62 us
  transfers between devices with their start and end apart: 15, of which 12 were waited for; matrix products, arithmetic and copies ran while one was open for 5% of the time, Pallas kernels for 1%

profile of v8, /device:TPU:0, one launch (start us, length us, event | category | flops | bytes accessed | tf_op | source)
XLA Modules:
  0.0 182.7 jit_solution(6323946860052952625)
XLA Ops:
  0.6 0.8 stack.24
  1.4 0.8 stack.23
  2.2 0.8 convolution_bitcast_fusion.4
  3.2 4.9 %collective-permute-start.3 = (f32[2,1024]{1,0:T(2,128)S(1)}, f32[2,1024]{1,0:T(2,128)S(1)}, u32[]{:S(2)}, u32[]{:S(2)}) collective-permute-start(f32[2,1024]{1,0:T(2,128)S(1)} %reshape.156), channel_id=1, source_target_pairs={{0,3},{1,0},{2,1},{3,2},{4,7},{5,4},{6,5},{7,6},{8,11},{9,8},{10,9... | collective-permute-start | bytes 24584 | tf_op jit(solution)/shard_map/ppermute | solution.py:158
  8.1 0.9 reduce
  9.1 0.9 convolution_bitcast_fusion.3
  10.1 0.7 collective-permute-start.2
  10.8 0.8 slice_bitcast_fusion.2
  11.7 0.8 slice_bitcast_fusion.1
  12.5 0.9 copy_bitcast_fusion.1
  13.4 0.8 squeeze.23
  14.2 0.8 squeeze.26
  16.6 1.0 shard_map.130.pcol_ref
  17.9 9.0 %shard_map.131 = (f32[3,80,64]{2,1,0:T(8,128)S(1)}, f32[32,128]{1,0:T(8,128)S(1)}) custom-call(s32[2,192]{1,0:T(2,128)S(1)} %pad_add_fusion.tiles_ref, s32[1]{0:T(128)} %bitcast.82.count_ref, f32[3,80,64]{2,1,0:T(8,128)S(1)} %pad_maximum_fusion.2.ext_ref, f32[3,80,64]{2,1,0:T(8,128)S(1)} %pad_maximum_fusion.3.prm_ref, f32[2,64,32,128]{3,2,1,0:T(8,128)S(1)} %shard_map.130.pcol_ref), custom_call_target="tpu_custom_call" | custom-call | tf_op jit(solution)/shard_map/pallas_call | solution.py:135
  26.9 5.5 %collective-permute-start.4 = (f32[3,1024]{1,0:T(4,128)S(1)}, f32[3,1024]{1,0:T(4,128)S(1)}, u32[]{:S(2)}, u32[]{:S(2)}) collective-permute-start(f32[3,1024]{1,0:T(4,128)S(1)} %reshape.157), channel_id=1, source_target_pairs={{0,1},{1,2},{2,3},{3,0},{4,5},{5,6},{6,7},{7,4},{8,9},{9,10},{10,1... | collective-permute-start | bytes 36872 | tf_op jit(solution)/shard_map/ppermute | solution.py:158
  32.4 0.6 reduce_sum.38
  33.0 1.2 collective-permute-done.4
  34.7 99.2 %while.17 = (s32[]{:T(128)}, f32[3,4096]{1,0:T(4,128)S(1)}, f32[3,4096]{1,0:T(4,128)S(1)}, f32[3,4096]{1,0:T(4,128)S(1)}, f32[]{:T(128)}, /*index=5*/f32[4096]{0...) while((s32[]{:T(128)}, f32[3,4096]{1,0:T(4,128)S(1)}, ...), condition=%wide.region_7.8_spmd.clone, body=%wide.region_5.0_spmd.clone.sunk | while | flops 4859905 | bytes 1311081 | solution.py:281
  35.3 1.4 collective-permute-done
  36.9 9.6 %eval_jaxpr.1 = (f32[3,80,64]{2,1,0:T(8,128)S(1)}, f32[32,128]{1,0:T(8,128)S(1)}) custom-call(s32[2,192]{1,0:T(2,128)S(1)} %get-tuple-element.251.tiles_ref, s32[1]{0:T(128)} %bitcast.80.count_ref, f32[3,80,64]{2,1,0:T(8,128)S(1)} %pad_maximum_fusion.5.ext_ref, f32[3,80,64]{2,1,0:T(8,128)S(1)} %get-tuple-element.252.prm_ref, ...), custom_call_target="tpu_custom_call" | custom-call | tf_op jit(solution)/shard_map/while/body/eval_jaxpr/pallas_call | solution.py:135
  46.6 10.7 %collective-permute-start.1 = (f32[3,1024]{1,0:T(4,128)S(1)}, f32[3,1024]{1,0:T(4,128)S(1)}, u32[]{:S(2)}, u32[]{:S(2)}) collective-permute-start(f32[3,1024]{1,0:T(4,128)S(1)} %reshape.207), channel_id=1, source_target_pairs={{0,1},{1,2},{2,3},{3,0},{4,5},{5,6},{6,7},{7,4},{8,9},{9,10},{10,1... | collective-permute-start | bytes 36872 | tf_op jit(solution)/shard_map/while/body/eval_jaxpr/ppermute | solution.py:158
  57.4 0.6 reduce_sum.43
  59.4 1.4 collective-permute-done
  61.0 9.6 %eval_jaxpr.1 = (f32[3,80,64]{2,1,0:T(8,128)S(1)}, f32[32,128]{1,0:T(8,128)S(1)}) custom-call(s32[2,192]{1,0:T(2,128)S(1)} %get-tuple-element.251.tiles_ref, s32[1]{0:T(128)} %bitcast.80.count_ref, f32[3,80,64]{2,1,0:T(8,128)S(1)} %pad_maximum_fusion.5.ext_ref, f32[3,80,64]{2,1,0:T(8,128)S(1)} %get-tuple-element.252.prm_ref, ...), custom_call_target="tpu_custom_call" | custom-call | tf_op jit(solution)/shard_map/while/body/eval_jaxpr/pallas_call | solution.py:135
  70.7 11.7 %collective-permute-start.1 = (f32[3,1024]{1,0:T(4,128)S(1)}, f32[3,1024]{1,0:T(4,128)S(1)}, u32[]{:S(2)}, u32[]{:S(2)}) collective-permute-start(f32[3,1024]{1,0:T(4,128)S(1)} %reshape.207), channel_id=1, source_target_pairs={{0,1},{1,2},{2,3},{3,0},{4,5},{5,6},{6,7},{7,4},{8,9},{9,10},{10,1... | collective-permute-start | bytes 36872 | tf_op jit(solution)/shard_map/while/body/eval_jaxpr/ppermute | solution.py:158
  82.4 0.6 reduce_sum.43
  84.4 1.4 collective-permute-done
  86.0 9.6 %eval_jaxpr.1 = (f32[3,80,64]{2,1,0:T(8,128)S(1)}, f32[32,128]{1,0:T(8,128)S(1)}) custom-call(s32[2,192]{1,0:T(2,128)S(1)} %get-tuple-element.251.tiles_ref, s32[1]{0:T(128)} %bitcast.80.count_ref, f32[3,80,64]{2,1,0:T(8,128)S(1)} %pad_maximum_fusion.5.ext_ref, f32[3,80,64]{2,1,0:T(8,128)S(1)} %get-tuple-element.252.prm_ref, ...), custom_call_target="tpu_custom_call" | custom-call | tf_op jit(solution)/shard_map/while/body/eval_jaxpr/pallas_call | solution.py:135
  95.7 11.7 %collective-permute-start.1 = (f32[3,1024]{1,0:T(4,128)S(1)}, f32[3,1024]{1,0:T(4,128)S(1)}, u32[]{:S(2)}, u32[]{:S(2)}) collective-permute-start(f32[3,1024]{1,0:T(4,128)S(1)} %reshape.207), channel_id=1, source_target_pairs={{0,1},{1,2},{2,3},{3,0},{4,5},{5,6},{6,7},{7,4},{8,9},{9,10},{10,1... | collective-permute-start | bytes 36872 | tf_op jit(solution)/shard_map/while/body/eval_jaxpr/ppermute | solution.py:158
  107.4 0.6 reduce_sum.43
  109.4 1.4 collective-permute-done
  111.1 9.6 %eval_jaxpr.1 = (f32[3,80,64]{2,1,0:T(8,128)S(1)}, f32[32,128]{1,0:T(8,128)S(1)}) custom-call(s32[2,192]{1,0:T(2,128)S(1)} %get-tuple-element.251.tiles_ref, s32[1]{0:T(128)} %bitcast.80.count_ref, f32[3,80,64]{2,1,0:T(8,128)S(1)} %pad_maximum_fusion.5.ext_ref, f32[3,80,64]{2,1,0:T(8,128)S(1)} %get-tuple-element.252.prm_ref, ...), custom_call_target="tpu_custom_call" | custom-call | tf_op jit(solution)/shard_map/while/body/eval_jaxpr/pallas_call | solution.py:135
  120.8 11.7 %collective-permute-start.1 = (f32[3,1024]{1,0:T(4,128)S(1)}, f32[3,1024]{1,0:T(4,128)S(1)}, u32[]{:S(2)}, u32[]{:S(2)}) collective-permute-start(f32[3,1024]{1,0:T(4,128)S(1)} %reshape.207), channel_id=1, source_target_pairs={{0,1},{1,2},{2,3},{3,0},{4,5},{5,6},{6,7},{7,4},{8,9},{9,10},{10,1... | collective-permute-start | bytes 36872 | tf_op jit(solution)/shard_map/while/body/eval_jaxpr/ppermute | solution.py:158
  132.5 0.6 reduce_sum.43
  134.2 0.8 reshape.194
  135.0 15.1 %all-to-all-start = ((f32[64,1,384]{2,1,0:T(1,128)}), f32[64,1,384]{2,1,0:T(1,128)S(1)}, u32[]{:S(2)}, u32[]{:S(2)}) async-start(f32[64,1,384]{2,1,0:T(1,128)} %reshape.194), calls=%async_computation | async-start | bytes 196608 | tf_op jit(solution)/shard_map/all_to_all | solution.py:178
  150.1 10.2 %all-to-all-done = f32[64,1,384]{2,1,0:T(1,128)S(1)} async-done(((f32[64,1,384]{2,1,0:T(1,128)}), f32[64,1,384]{2,1,0:T(1,128)S(1)}, u32[]{:S(2)}, u32[]{:S(2)}) %all-to-all-start) | async-done | bytes 98336 | tf_op jit(solution)/shard_map/all_to_all | solution.py:178
  160.4 0.5 broadcast.55
  160.9 0.9 reduce.11
  161.9 0.6 gather_fusion
  162.6 0.8 reshape.196
  163.4 4.6 %all-to-all-start.1 = ((f32[64,1,384]{2,1,0:T(1,128)}), f32[64,1,384]{2,1,0:T(1,128)S(1)}, u32[]{:S(2)}, u32[]{:S(2)}) async-start(f32[64,1,384]{2,1,0:T(1,128)} %reshape.196), calls=%async_computation.1 | async-start | bytes 196608 | tf_op jit(solution)/shard_map/all_to_all | solution.py:180
  168.1 1.4 collective-permute-done.5
  170.8 3.4 %collective-permute-start.6 = (f32[]{:T(128)}, f32[]{:T(128)}, u32[]{:S(2)}, u32[]{:S(2)}) collective-permute-start(f32[]{:T(128)} %add.87), channel_id=1, source_target_pairs={{0,2},{1,3},{2,0},{3,1},{4,6},{5,7},{6,4},{7,5},{8,10},{9,11},{10,... | collective-permute-start | bytes 20 | tf_op jit(solution)/shard_map/ppermute | solution.py:296
  174.2 4.2 %collective-permute-done.6 = f32[]{:T(128)} collective-permute-done((f32[]{:T(128)}, f32[]{:T(128)}, u32[]{:S(2)}, u32[]{:S(2)}) %collective-permute-start.6) | collective-permute-done | bytes 36 | tf_op jit(solution)/shard_map/ppermute | solution.py:296
  179.0 0.9 reduce.12
  180.1 0.7 broadcast_in_dim.44
  180.8 0.7 broadcast_in_dim.45
  (113 shorter events, 8.8 us)
Async XLA Ops:
  0.6 17.0 %copy-start.3 = (f32[3]{0:T(128)S(1)}, f32[3]{0:T(128)}, u32[]{:S(2)}) copy-start(f32[3]{0:T(128)} %constant.36.clone) | copy-start | bytes 40
  3.2 13.1 %collective-permute-start.3 = (f32[2,1024]{1,0:T(2,128)S(1)}, f32[2,1024]{1,0:T(2,128)S(1)}, u32[]{:S(2)}, u32[]{:S(2)}) collective-permute-start(f32[2,1024]{1,0:T(2,128)S(1)} %reshape.156), channel_id=1, source_target_pairs={{0,3},{1,0},{2,1},{3,2},{4,7},{5,4},{6,5},{7,6},{8,11},{9,8},{10,9... | collective-permute-start | bytes 24584 | tf_op jit(solution)/shard_map/ppermute | solution.py:158
  10.1 7.6 %collective-permute-start.2 = (f32[3,1024]{1,0:T(4,128)S(1)}, f32[3,1024]{1,0:T(4,128)S(1)}, u32[]{:S(2)}, u32[]{:S(2)}) collective-permute-start(f32[3,1024]{1,0:T(4,128)S(1)} %reshape.154), channel_id=1, source_target_pairs={{0,3},{1,0},{2,1},{3,2},{4,7},{5,4},{6,5},{7,6},{8,11},{9,8},{10,9... | collective-permute-start | bytes 36872 | tf_op jit(solution)/shard_map/ppermute | solution.py:158
  16.6 17.7 %copy-start.1 = (s32[1,16]{1,0:T(1,128)S(1)}, s32[1,16]{1,0:T(1,128)}, u32[]{:S(2)}) copy-start(s32[1,16]{1,0:T(1,128)} %param.21) | copy-start | bytes 196
  17.6 17.1 %copy-start = (f32[4096]{0:T(1024)S(1)}, f32[4096]{0:T(1024)}, u32[]{:S(2)}) copy-start(f32[4096]{0:T(1024)} %param.15) | copy-start | bytes 49156
  17.6 17.1 %copy-start.2 = (f32[3]{0:T(128)S(1)}, f32[3]{0:T(128)}, u32[]{:S(2)}) copy-start(f32[3]{0:T(128)} %constant.111) | copy-start | bytes 40
  26.9 7.3 %collective-permute-start.4 = (f32[3,1024]{1,0:T(4,128)S(1)}, f32[3,1024]{1,0:T(4,128)S(1)}, u32[]{:S(2)}, u32[]{:S(2)}) collective-permute-start(f32[3,1024]{1,0:T(4,128)S(1)} %reshape.157), channel_id=1, source_target_pairs={{0,1},{1,2},{2,3},{3,0},{4,5},{5,6},{6,7},{7,4},{8,9},{9,10},{10,1... | collective-permute-start | bytes 36872 | tf_op jit(solution)/shard_map/ppermute | solution.py:158
  35.2 1.5 collective-permute-start
  46.6 11.6 %collective-permute-start.1 = (f32[3,1024]{1,0:T(4,128)S(1)}, f32[3,1024]{1,0:T(4,128)S(1)}, u32[]{:S(2)}, u32[]{:S(2)}) collective-permute-start(f32[3,1024]{1,0:T(4,128)S(1)} %reshape.207), channel_id=1, source_target_pairs={{0,1},{1,2},{2,3},{3,0},{4,5},{5,6},{6,7},{7,4},{8,9},{9,10},{10,1... | collective-permute-start | bytes 36872 | tf_op jit(solution)/shard_map/while/body/eval_jaxpr/ppermute | solution.py:158
  59.3 1.5 collective-permute-start
  70.7 12.5 %collective-permute-start.1 = (f32[3,1024]{1,0:T(4,128)S(1)}, f32[3,1024]{1,0:T(4,128)S(1)}, u32[]{:S(2)}, u32[]{:S(2)}) collective-permute-start(f32[3,1024]{1,0:T(4,128)S(1)} %reshape.207), channel_id=1, source_target_pairs={{0,1},{1,2},{2,3},{3,0},{4,5},{5,6},{6,7},{7,4},{8,9},{9,10},{10,1... | collective-permute-start | bytes 36872 | tf_op jit(solution)/shard_map/while/body/eval_jaxpr/ppermute | solution.py:158
  84.4 1.5 collective-permute-start
  95.7 12.5 %collective-permute-start.1 = (f32[3,1024]{1,0:T(4,128)S(1)}, f32[3,1024]{1,0:T(4,128)S(1)}, u32[]{:S(2)}, u32[]{:S(2)}) collective-permute-start(f32[3,1024]{1,0:T(4,128)S(1)} %reshape.207), channel_id=1, source_target_pairs={{0,1},{1,2},{2,3},{3,0},{4,5},{5,6},{6,7},{7,4},{8,9},{9,10},{10,1... | collective-permute-start | bytes 36872 | tf_op jit(solution)/shard_map/while/body/eval_jaxpr/ppermute | solution.py:158
  109.4 1.5 collective-permute-start
  120.8 12.5 %collective-permute-start.1 = (f32[3,1024]{1,0:T(4,128)S(1)}, f32[3,1024]{1,0:T(4,128)S(1)}, u32[]{:S(2)}, u32[]{:S(2)}) collective-permute-start(f32[3,1024]{1,0:T(4,128)S(1)} %reshape.207), channel_id=1, source_target_pairs={{0,1},{1,2},{2,3},{3,0},{4,5},{5,6},{6,7},{7,4},{8,9},{9,10},{10,1... | collective-permute-start | bytes 36872 | tf_op jit(solution)/shard_map/while/body/eval_jaxpr/ppermute | solution.py:158
  135.0 25.4 %all-to-all-start = ((f32[64,1,384]{2,1,0:T(1,128)}), f32[64,1,384]{2,1,0:T(1,128)S(1)}, u32[]{:S(2)}, u32[]{:S(2)}) async-start(f32[64,1,384]{2,1,0:T(1,128)} %reshape.194), calls=%async_computation | async-start | bytes 196608 | tf_op jit(solution)/shard_map/all_to_all | solution.py:178
  163.4 15.6 %all-to-all-start.1 = ((f32[64,1,384]{2,1,0:T(1,128)}), f32[64,1,384]{2,1,0:T(1,128)S(1)}, u32[]{:S(2)}, u32[]{:S(2)}) async-start(f32[64,1,384]{2,1,0:T(1,128)} %reshape.196), calls=%async_computation.1 | async-start | bytes 196608 | tf_op jit(solution)/shard_map/all_to_all | solution.py:180
  168.0 1.5 collective-permute-start.5
  170.8 7.7 %collective-permute-start.6 = (f32[]{:T(128)}, f32[]{:T(128)}, u32[]{:S(2)}, u32[]{:S(2)}) collective-permute-start(f32[]{:T(128)} %add.87), channel_id=1, source_target_pairs={{0,2},{1,3},{2,0},{3,1},{4,6},{5,7},{6,4},{7,5},{8,10},{9,11},{10,... | collective-permute-start | bytes 20 | tf_op jit(solution)/shard_map/ppermute | solution.py:296

commit v9 on v6

--- a/solution.py
+++ b/solution.py
@@ -230,22 +230,26 @@
     atoms_here = coords.shape[1]
     halo_table = select_table(halo_index, CD)
     params = jnp.stack([strength, charge], 0).reshape(2, CD, CL)
-    sent_params = jnp.einsum("hc,pck->phk", halo_table, params, precision=exact).reshape(
-        2, HALO * CL
-    )
-    got_params = from_behind(sent_params, "slab", -1).reshape(2, HALO, CL)
+    start_rows = jnp.concatenate([params, coords.reshape(3, CD, CL)], 0)
+    sent_start = jnp.einsum("hc,pck->phk", halo_table, start_rows, precision=exact).reshape(
+        5, HALO * CL
+    )
+    got_start = from_behind(sent_start, "slab", -1)
+    got_params = got_start[:2].reshape(2, HALO, CL)
     strength_all = jnp.concatenate([params[0], got_params[0]], 0)
     charge_all = jnp.concatenate([params[1], got_params[1]], 0)
     lift = jnp.array([0.0, 0.0, slab_width], jnp.float32)[:, None]
     param_all = jnp.stack([strength_all, ham_scale * charge_all, charge_all], 0)
     tile_list = jnp.stack([firsts_flat, seconds_flat], 0)
 
-    def evaluate(coords_now):
+    def evaluate(coords_now, received=None):
         blocks = coords_now.reshape(3, CD, CL)
-        sent_coords = jnp.einsum("hc,xck->xhk", halo_table, blocks, precision=exact).reshape(
-            3, HALO * CL
-        )
-        from_above = from_behind(sent_coords, "slab", -1) + lift
+        if received is None:
+            sent_coords = jnp.einsum(
+                "hc,xck->xhk", halo_table, blocks, precision=exact
+            ).reshape(3, HALO * CL)
+            received = from_behind(sent_coords, "slab", -1)
+        from_above = received + lift
         extended = jnp.concatenate([blocks, from_above.reshape(3, HALO, CL)], 1)
         forces, energy = slab_pairs(extended, param_all, tile_list, live_count)
         returned = from_behind(forces[:, CD:].reshape(3, HALO * CL), "slab", 1)
@@ -263,7 +267,7 @@
         speeds = speeds + half_step * forces * inv_mass
         return (coords, speeds, forces, energy)
 
-    forces, energy = evaluate(coords)
+    forces, energy = evaluate(coords, got_start[2:])
     coords, speeds, forces, energy = lax.fori_loop(
         0, STEPS, verlet_step, (coords, speeds, forces, energy)
     )

time: 181 us -> 182 us (level)
  starting transfers between devices: 28.3 us -> 70.9 us
  waiting for transfers between devices: 77.2 us -> 38.3 us
  Pallas kernels: 47 us -> 43.4 us
    ppermute x11 -> x10, waiting for transfers between devices: 61.7 us -> 22 us  [from_behind(): return lax.ppermute(value, axis, pairs)]
    ppermute x11 -> x10, starting transfers between devices: 9.71 us -> 44.7 us  [from_behind(): return lax.ppermute(value, axis, pairs)]
    all_to_all x1, starting transfers between devices: 10.1 us -> 18.5 us  [exchange(): spread = lax.all_to_all(chunks, 'rep', 0, 0, tiled=True)]
    pallas_call x5, Pallas kernels: 47 us -> 43.4 us  [slab_pairs(): pl.pallas_call(pair_kernel, out_shape=(jax.ShapeDtypeStruct((3, width, CL...]
  transfers between devices with their start and end apart: 15 -> 14, of which waited for: 12 -> 12; matrix products, arithmetic and copies ran while one was open for 2% -> 2% of each run, Pallas kernels for 0% -> 0%
where the time goes in v9:
time: 182 us; the launch traced here: 179 us
  starting transfers between devices  70.9 us (39%)
  Pallas kernels  43.4 us (24%)
  waiting for transfers between devices  38.3 us (21%)
  local copies, waits for them, and re-layouts  11.7 us (6%)
  other arithmetic  6.91 us (4%)
  between operations  5.1 us (3%)
  matrix products  2.86 us (2%)
    ppermute x10, starting transfers between devices, from_behind(): return lax.ppermute(value, axis, pairs)  44.7 us
    pallas_call x5, Pallas kernels, slab_pairs(): pl.pallas_call(pair_kernel, out_shape=(jax.ShapeDtypeStruct((3, width, CL...  43.4 us
    ppermute x10, waiting for transfers between devices, from_behind(): return lax.ppermute(value, axis, pairs)  22 us
    all_to_all x1, starting transfers between devices, exchange(): spread = lax.all_to_all(chunks, 'rep', 0, 0, tiled=True)  18.5 us
    all_to_all x1, waiting for transfers between devices, exchange(): spread = lax.all_to_all(chunks, 'rep', 0, 0, tiled=True)  10.2 us
    ppermute x2, waiting for transfers between devices, slab_sum(): value = value + lax.ppermute(value, 'slab', pairs)  6.08 us
    unnamed x25, local copies, waits for them, and re-layouts  5.47 us
    all_to_all x1, starting transfers between devices, exchange(): gathered = lax.all_to_all(routed, 'rep', 0, 0, tiled=True)  4.61 us
  transfers between devices with their start and end apart: 14, of which 12 were waited for; matrix products, arithmetic and copies ran while one was open for 2% of the time, Pallas kernels for 0%

profile of v9, /device:TPU:0, one launch (start us, length us, event | category | flops | bytes accessed | tf_op | source)
XLA Modules:
  0.0 179.4 jit_solution(1678820817863060578)
XLA Ops:
  0.6 0.9 reduce
  1.7 0.6 copy-done.3
  2.4 0.6 copy-done.2
  3.1 0.7 copy-done.4
  4.1 4.9 %collective-permute-start.2 = (f32[5,1024]{1,0:T(8,128)S(1)}, f32[5,1024]{1,0:T(8,128)S(1)}, u32[]{:S(2)}, u32[]{:S(2)}) collective-permute-start(f32[5,1024]{1,0:T(8,128)S(1)} %reshape.151), channel_id=1, source_target_pairs={{0,3},{1,0},{2,1},{3,2},{4,7},{5,4},{6,5},{7,6},{8,11},{9,8},{10,9... | collective-permute-start | bytes 61448 | tf_op jit(solution)/shard_map/ppermute | solution.py:145
  11.5 0.6 copy-done.9
  12.3 8.2 %shard_map.130 = (f32[3,80,64]{2,1,0:T(8,128)S(1)}, f32[32,128]{1,0:T(8,128)S(1)}) custom-call(s32[2,192]{1,0:T(2,128)S(1)} %pad_add_fusion.tiles_ref, s32[1]{0:T(128)} %bitcast.78.count_ref, f32[3,80,64]{2,1,0:T(8,128)S(1)} %pad_maximum_fusion.2.ext_ref, f32[3,80,64]{2,1,0:T(8,128)S(1)} %pad_maximum_fusion.3.prm_ref), custom_call_target="tpu_custom_call" | custom-call | tf_op jit(solution)/shard_map/pallas_call | solution.py:121
  20.9 0.6 reduce_sum.38
  21.5 7.7 %collective-permute-done.3 = f32[3,1024]{1,0:T(4,128)S(1)} collective-permute-done((f32[3,1024]{1,0:T(4,128)S(1)}, f32[3,1024]{1,0:T(4,128)S(1)}, u32[]{:S(2)}, u32[]{:S(2)}) %collective-permute-start.3) | collective-permute-done | bytes 12320 | tf_op jit(solution)/shard_map/ppermute | solution.py:145
  29.7 0.6 copy-done
  30.3 97.0 %while.17 = (s32[]{:T(128)}, f32[3,4096]{1,0:T(4,128)S(1)}, f32[3,4096]{1,0:T(4,128)S(1)}, f32[3,4096]{1,0:T(4,128)S(1)}, f32[]{:T(128)}, /*index=5*/f32[4096]{0...) while((s32[]{:T(128)}, f32[3,4096]{1,0:T(4,128)S(1)}, ...), condition=%wide.region_7.8_spmd.clone, body=%wide.region_5.0_spmd.clone.sunk | while | flops 4859905 | bytes 1311073 | solution.py:271
  31.0 1.4 collective-permute-done
  32.6 8.8 %eval_jaxpr.1 = (f32[3,80,64]{2,1,0:T(8,128)S(1)}, f32[32,128]{1,0:T(8,128)S(1)}) custom-call(s32[2,192]{1,0:T(2,128)S(1)} %get-tuple-element.234.tiles_ref, s32[1]{0:T(128)} %bitcast.76.count_ref, f32[3,80,64]{2,1,0:T(8,128)S(1)} %pad_maximum_fusion.5.ext_ref, f32[3,80,64]{2,1,0:T(8,128)S(1)} %get-tuple-element.235.prm_ref), custom_call_target="tpu_custom_call" | custom-call | tf_op jit(solution)/shard_map/while/body/eval_jaxpr/pallas_call | solution.py:121
  41.5 6.4 %collective-permute-start.1 = (f32[3,1024]{1,0:T(4,128)S(1)}, f32[3,1024]{1,0:T(4,128)S(1)}, u32[]{:S(2)}, u32[]{:S(2)}) collective-permute-start(f32[3,1024]{1,0:T(4,128)S(1)} %reshape.203), channel_id=1, source_target_pairs={{0,1},{1,2},{2,3},{3,0},{4,5},{5,6},{6,7},{7,4},{8,9},{9,10},{10,1... | collective-permute-start | bytes 36872 | tf_op jit(solution)/shard_map/while/body/eval_jaxpr/ppermute | solution.py:145
  47.9 0.6 reduce_sum.43
  48.5 2.1 %collective-permute-done.1 = f32[3,1024]{1,0:T(4,128)S(1)} collective-permute-done((f32[3,1024]{1,0:T(4,128)S(1)}, f32[3,1024]{1,0:T(4,128)S(1)}, u32[]{:S(2)}, u32[]{:S(2)}) %collective-permute-start.1) | collective-permute-done | bytes 12320 | tf_op jit(solution)/shard_map/while/body/eval_jaxpr/ppermute | solution.py:145
  51.8 4.5 %collective-permute-start = (f32[3,1024]{1,0:T(4,128)S(1)}, f32[3,1024]{1,0:T(4,128)S(1)}, u32[]{:S(2)}, u32[]{:S(2)}) collective-permute-start(f32[3,1024]{1,0:T(4,128)S(1)} %reshape.201), channel_id=1, source_target_pairs={{0,3},{1,0},{2,1},{3,2},{4,7},{5,4},{6,5},{7,6},{8,11},{9,8},{10,9... | collective-permute-start | bytes 36872 | tf_op jit(solution)/shard_map/while/body/eval_jaxpr/ppermute | solution.py:145
  56.3 1.4 collective-permute-done
  57.9 8.8 %eval_jaxpr.1 = (f32[3,80,64]{2,1,0:T(8,128)S(1)}, f32[32,128]{1,0:T(8,128)S(1)}) custom-call(s32[2,192]{1,0:T(2,128)S(1)} %get-tuple-element.234.tiles_ref, s32[1]{0:T(128)} %bitcast.76.count_ref, f32[3,80,64]{2,1,0:T(8,128)S(1)} %pad_maximum_fusion.5.ext_ref, f32[3,80,64]{2,1,0:T(8,128)S(1)} %get-tuple-element.235.prm_ref), custom_call_target="tpu_custom_call" | custom-call | tf_op jit(solution)/shard_map/while/body/eval_jaxpr/pallas_call | solution.py:121
  66.8 6.4 %collective-permute-start.1 = (f32[3,1024]{1,0:T(4,128)S(1)}, f32[3,1024]{1,0:T(4,128)S(1)}, u32[]{:S(2)}, u32[]{:S(2)}) collective-permute-start(f32[3,1024]{1,0:T(4,128)S(1)} %reshape.203), channel_id=1, source_target_pairs={{0,1},{1,2},{2,3},{3,0},{4,5},{5,6},{6,7},{7,4},{8,9},{9,10},{10,1... | collective-permute-start | bytes 36872 | tf_op jit(solution)/shard_map/while/body/eval_jaxpr/ppermute | solution.py:145
  73.3 0.6 reduce_sum.43
  73.9 2.1 %collective-permute-done.1 = f32[3,1024]{1,0:T(4,128)S(1)} collective-permute-done((f32[3,1024]{1,0:T(4,128)S(1)}, f32[3,1024]{1,0:T(4,128)S(1)}, u32[]{:S(2)}, u32[]{:S(2)}) %collective-permute-start.1) | collective-permute-done | bytes 12320 | tf_op jit(solution)/shard_map/while/body/eval_jaxpr/ppermute | solution.py:145
  77.1 4.5 %collective-permute-start = (f32[3,1024]{1,0:T(4,128)S(1)}, f32[3,1024]{1,0:T(4,128)S(1)}, u32[]{:S(2)}, u32[]{:S(2)}) collective-permute-start(f32[3,1024]{1,0:T(4,128)S(1)} %reshape.201), channel_id=1, source_target_pairs={{0,3},{1,0},{2,1},{3,2},{4,7},{5,4},{6,5},{7,6},{8,11},{9,8},{10,9... | collective-permute-start | bytes 36872 | tf_op jit(solution)/shard_map/while/body/eval_jaxpr/ppermute | solution.py:145
  81.7 1.4 collective-permute-done
  83.3 8.8 %eval_jaxpr.1 = (f32[3,80,64]{2,1,0:T(8,128)S(1)}, f32[32,128]{1,0:T(8,128)S(1)}) custom-call(s32[2,192]{1,0:T(2,128)S(1)} %get-tuple-element.234.tiles_ref, s32[1]{0:T(128)} %bitcast.76.count_ref, f32[3,80,64]{2,1,0:T(8,128)S(1)} %pad_maximum_fusion.5.ext_ref, f32[3,80,64]{2,1,0:T(8,128)S(1)} %get-tuple-element.235.prm_ref), custom_call_target="tpu_custom_call" | custom-call | tf_op jit(solution)/shard_map/while/body/eval_jaxpr/pallas_call | solution.py:121
  92.2 6.4 %collective-permute-start.1 = (f32[3,1024]{1,0:T(4,128)S(1)}, f32[3,1024]{1,0:T(4,128)S(1)}, u32[]{:S(2)}, u32[]{:S(2)}) collective-permute-start(f32[3,1024]{1,0:T(4,128)S(1)} %reshape.203), channel_id=1, source_target_pairs={{0,1},{1,2},{2,3},{3,0},{4,5},{5,6},{6,7},{7,4},{8,9},{9,10},{10,1... | collective-permute-start | bytes 36872 | tf_op jit(solution)/shard_map/while/body/eval_jaxpr/ppermute | solution.py:145
  98.6 0.6 reduce_sum.43
  99.2 2.1 %collective-permute-done.1 = f32[3,1024]{1,0:T(4,128)S(1)} collective-permute-done((f32[3,1024]{1,0:T(4,128)S(1)}, f32[3,1024]{1,0:T(4,128)S(1)}, u32[]{:S(2)}, u32[]{:S(2)}) %collective-permute-start.1) | collective-permute-done | bytes 12320 | tf_op jit(solution)/shard_map/while/body/eval_jaxpr/ppermute | solution.py:145
  102.5 4.5 %collective-permute-start = (f32[3,1024]{1,0:T(4,128)S(1)}, f32[3,1024]{1,0:T(4,128)S(1)}, u32[]{:S(2)}, u32[]{:S(2)}) collective-permute-start(f32[3,1024]{1,0:T(4,128)S(1)} %reshape.201), channel_id=1, source_target_pairs={{0,3},{1,0},{2,1},{3,2},{4,7},{5,4},{6,5},{7,6},{8,11},{9,8},{10,9... | collective-permute-start | bytes 36872 | tf_op jit(solution)/shard_map/while/body/eval_jaxpr/ppermute | solution.py:145
  107.0 1.4 collective-permute-done
  108.6 8.8 %eval_jaxpr.1 = (f32[3,80,64]{2,1,0:T(8,128)S(1)}, f32[32,128]{1,0:T(8,128)S(1)}) custom-call(s32[2,192]{1,0:T(2,128)S(1)} %get-tuple-element.234.tiles_ref, s32[1]{0:T(128)} %bitcast.76.count_ref, f32[3,80,64]{2,1,0:T(8,128)S(1)} %pad_maximum_fusion.5.ext_ref, f32[3,80,64]{2,1,0:T(8,128)S(1)} %get-tuple-element.235.prm_ref), custom_call_target="tpu_custom_call" | custom-call | tf_op jit(solution)/shard_map/while/body/eval_jaxpr/pallas_call | solution.py:121
  117.5 6.4 %collective-permute-start.1 = (f32[3,1024]{1,0:T(4,128)S(1)}, f32[3,1024]{1,0:T(4,128)S(1)}, u32[]{:S(2)}, u32[]{:S(2)}) collective-permute-start(f32[3,1024]{1,0:T(4,128)S(1)} %reshape.203), channel_id=1, source_target_pairs={{0,1},{1,2},{2,3},{3,0},{4,5},{5,6},{6,7},{7,4},{8,9},{9,10},{10,1... | collective-permute-start | bytes 36872 | tf_op jit(solution)/shard_map/while/body/eval_jaxpr/ppermute | solution.py:145
  124.0 0.6 reduce_sum.43
  124.6 2.1 %collective-permute-done.1 = f32[3,1024]{1,0:T(4,128)S(1)} collective-permute-done((f32[3,1024]{1,0:T(4,128)S(1)}, f32[3,1024]{1,0:T(4,128)S(1)}, u32[]{:S(2)}, u32[]{:S(2)}) %collective-permute-start.1) | collective-permute-done | bytes 12320 | tf_op jit(solution)/shard_map/while/body/eval_jaxpr/ppermute | solution.py:145
  127.6 0.8 reshape.190
  128.4 18.5 %all-to-all-start = ((f32[64,1,384]{2,1,0:T(1,128)}), f32[64,1,384]{2,1,0:T(1,128)S(1)}, u32[]{:S(2)}, u32[]{:S(2)}) async-start(f32[64,1,384]{2,1,0:T(1,128)} %reshape.190), calls=%async_computation | async-start | bytes 196608 | tf_op jit(solution)/shard_map/all_to_all | solution.py:165
  146.9 10.2 %all-to-all-done = f32[64,1,384]{2,1,0:T(1,128)S(1)} async-done(((f32[64,1,384]{2,1,0:T(1,128)}), f32[64,1,384]{2,1,0:T(1,128)S(1)}, u32[]{:S(2)}, u32[]{:S(2)}) %all-to-all-start) | async-done | bytes 98336 | tf_op jit(solution)/shard_map/all_to_all | solution.py:165
  157.1 0.5 broadcast.55
  157.6 0.9 reduce.11
  158.6 0.6 gather_fusion
  159.4 0.8 reshape.192
  160.2 4.6 %all-to-all-start.1 = ((f32[64,1,384]{2,1,0:T(1,128)}), f32[64,1,384]{2,1,0:T(1,128)S(1)}, u32[]{:S(2)}, u32[]{:S(2)}) async-start(f32[64,1,384]{2,1,0:T(1,128)} %reshape.192), calls=%async_computation.1 | async-start | bytes 196608 | tf_op jit(solution)/shard_map/all_to_all | solution.py:167
  164.9 1.4 collective-permute-done.4
  167.5 3.0 %collective-permute-start.5 = (f32[]{:T(128)}, f32[]{:T(128)}, u32[]{:S(2)}, u32[]{:S(2)}) collective-permute-start(f32[]{:T(128)} %add.87), channel_id=1, source_target_pairs={{0,2},{1,3},{2,0},{3,1},{4,6},{5,7},{6,4},{7,5},{8,10},{9,11},{10,... | collective-permute-start | bytes 20 | tf_op jit(solution)/shard_map/ppermute | solution.py:286
  170.5 4.7 %collective-permute-done.5 = f32[]{:T(128)} collective-permute-done((f32[]{:T(128)}, f32[]{:T(128)}, u32[]{:S(2)}, u32[]{:S(2)}) %collective-permute-start.5) | collective-permute-done | bytes 36 | tf_op jit(solution)/shard_map/ppermute | solution.py:286
  175.7 0.9 reduce.12
  176.8 0.7 broadcast_in_dim.44
  177.6 0.7 broadcast_in_dim.45
  (120 shorter events, 9.1 us)
Async XLA Ops:
  1.6 0.7 copy-start.3
  2.3 0.7 copy-start.2
  3.1 0.7 copy-start.4
  3.7 6.0 %copy-start.5 = (f32[1,3,4096]{2,0,1:T(1,128)S(1)}, f32[1,3,4096]{2,0,1:T(1,128)}, u32[]{:S(2)}) copy-start(f32[1,3,4096]{2,0,1:T(1,128)} %param.14) | copy-start | bytes 147460
  4.0 5.1 %copy-start.8 = (s32[16,2]{0,1:T(2,128)S(1)}, s32[16,2]{0,1:T(2,128)}, u32[]{:S(2)}) copy-start(s32[16,2]{0,1:T(2,128)} %param.22) | copy-start | bytes 388
  4.0 5.7 %copy-start.1 = (f32[1,3,4096]{2,0,1:T(1,128)S(1)}, f32[1,3,4096]{2,0,1:T(1,128)}, u32[]{:S(2)}) copy-start(f32[1,3,4096]{2,0,1:T(1,128)} %param.13) | copy-start | bytes 147460
  4.1 7.2 %collective-permute-start.2 = (f32[5,1024]{1,0:T(8,128)S(1)}, f32[5,1024]{1,0:T(8,128)S(1)}, u32[]{:S(2)}, u32[]{:S(2)}) collective-permute-start(f32[5,1024]{1,0:T(8,128)S(1)} %reshape.151), channel_id=1, source_target_pairs={{0,3},{1,0},{2,1},{3,2},{4,7},{5,4},{6,5},{7,6},{8,11},{9,8},{10,9... | collective-permute-start | bytes 61448 | tf_op jit(solution)/shard_map/ppermute | solution.py:145
  9.0 0.7 copy-start.7
  11.4 0.7 copy-start.9
  20.6 8.5 %collective-permute-start.3 = (f32[3,1024]{1,0:T(4,128)S(1)}, f32[3,1024]{1,0:T(4,128)S(1)}, u32[]{:S(2)}, u32[]{:S(2)}) collective-permute-start(f32[3,1024]{1,0:T(4,128)S(1)} %reshape.153), channel_id=1, source_target_pairs={{0,1},{1,2},{2,3},{3,0},{4,5},{5,6},{6,7},{7,4},{8,9},{9,10},{10,1... | collective-permute-start | bytes 36872 | tf_op jit(solution)/shard_map/ppermute | solution.py:145
  29.5 0.7 copy-start
  29.7 0.7 copy-start.6
  30.8 1.6 collective-permute-start
  41.5 9.2 %collective-permute-start.1 = (f32[3,1024]{1,0:T(4,128)S(1)}, f32[3,1024]{1,0:T(4,128)S(1)}, u32[]{:S(2)}, u32[]{:S(2)}) collective-permute-start(f32[3,1024]{1,0:T(4,128)S(1)} %reshape.203), channel_id=1, source_target_pairs={{0,1},{1,2},{2,3},{3,0},{4,5},{5,6},{6,7},{7,4},{8,9},{9,10},{10,1... | collective-permute-start | bytes 36872 | tf_op jit(solution)/shard_map/while/body/eval_jaxpr/ppermute | solution.py:145
  51.8 6.0 %collective-permute-start = (f32[3,1024]{1,0:T(4,128)S(1)}, f32[3,1024]{1,0:T(4,128)S(1)}, u32[]{:S(2)}, u32[]{:S(2)}) collective-permute-start(f32[3,1024]{1,0:T(4,128)S(1)} %reshape.201), channel_id=1, source_target_pairs={{0,3},{1,0},{2,1},{3,2},{4,7},{5,4},{6,5},{7,6},{8,11},{9,8},{10,9... | collective-permute-start | bytes 36872 | tf_op jit(solution)/shard_map/while/body/eval_jaxpr/ppermute | solution.py:145
  66.8 9.2 %collective-permute-start.1 = (f32[3,1024]{1,0:T(4,128)S(1)}, f32[3,1024]{1,0:T(4,128)S(1)}, u32[]{:S(2)}, u32[]{:S(2)}) collective-permute-start(f32[3,1024]{1,0:T(4,128)S(1)} %reshape.203), channel_id=1, source_target_pairs={{0,1},{1,2},{2,3},{3,0},{4,5},{5,6},{6,7},{7,4},{8,9},{9,10},{10,1... | collective-permute-start | bytes 36872 | tf_op jit(solution)/shard_map/while/body/eval_jaxpr/ppermute | solution.py:145
  77.1 6.0 %collective-permute-start = (f32[3,1024]{1,0:T(4,128)S(1)}, f32[3,1024]{1,0:T(4,128)S(1)}, u32[]{:S(2)}, u32[]{:S(2)}) collective-permute-start(f32[3,1024]{1,0:T(4,128)S(1)} %reshape.201), channel_id=1, source_target_pairs={{0,3},{1,0},{2,1},{3,2},{4,7},{5,4},{6,5},{7,6},{8,11},{9,8},{10,9... | collective-permute-start | bytes 36872 | tf_op jit(solution)/shard_map/while/body/eval_jaxpr/ppermute | solution.py:145
  92.2 9.2 %collective-permute-start.1 = (f32[3,1024]{1,0:T(4,128)S(1)}, f32[3,1024]{1,0:T(4,128)S(1)}, u32[]{:S(2)}, u32[]{:S(2)}) collective-permute-start(f32[3,1024]{1,0:T(4,128)S(1)} %reshape.203), channel_id=1, source_target_pairs={{0,1},{1,2},{2,3},{3,0},{4,5},{5,6},{6,7},{7,4},{8,9},{9,10},{10,1... | collective-permute-start | bytes 36872 | tf_op jit(solution)/shard_map/while/body/eval_jaxpr/ppermute | solution.py:145
  102.5 6.0 %collective-permute-start = (f32[3,1024]{1,0:T(4,128)S(1)}, f32[3,1024]{1,0:T(4,128)S(1)}, u32[]{:S(2)}, u32[]{:S(2)}) collective-permute-start(f32[3,1024]{1,0:T(4,128)S(1)} %reshape.201), channel_id=1, source_target_pairs={{0,3},{1,0},{2,1},{3,2},{4,7},{5,4},{6,5},{7,6},{8,11},{9,8},{10,9... | collective-permute-start | bytes 36872 | tf_op jit(solution)/shard_map/while/body/eval_jaxpr/ppermute | solution.py:145
  117.5 9.2 %collective-permute-start.1 = (f32[3,1024]{1,0:T(4,128)S(1)}, f32[3,1024]{1,0:T(4,128)S(1)}, u32[]{:S(2)}, u32[]{:S(2)}) collective-permute-start(f32[3,1024]{1,0:T(4,128)S(1)} %reshape.203), channel_id=1, source_target_pairs={{0,1},{1,2},{2,3},{3,0},{4,5},{5,6},{6,7},{7,4},{8,9},{9,10},{10,1... | collective-permute-start | bytes 36872 | tf_op jit(solution)/shard_map/while/body/eval_jaxpr/ppermute | solution.py:145
  128.4 28.7 %all-to-all-start = ((f32[64,1,384]{2,1,0:T(1,128)}), f32[64,1,384]{2,1,0:T(1,128)S(1)}, u32[]{:S(2)}, u32[]{:S(2)}) async-start(f32[64,1,384]{2,1,0:T(1,128)} %reshape.190), calls=%async_computation | async-start | bytes 196608 | tf_op jit(solution)/shard_map/all_to_all | solution.py:165
  160.2 15.6 %all-to-all-start.1 = ((f32[64,1,384]{2,1,0:T(1,128)}), f32[64,1,384]{2,1,0:T(1,128)S(1)}, u32[]{:S(2)}, u32[]{:S(2)}) async-start(f32[64,1,384]{2,1,0:T(1,128)} %reshape.192), calls=%async_computation.1 | async-start | bytes 196608 | tf_op jit(solution)/shard_map/all_to_all | solution.py:167
  164.8 1.5 collective-permute-start.4
  167.5 7.7 %collective-permute-start.5 = (f32[]{:T(128)}, f32[]{:T(128)}, u32[]{:S(2)}, u32[]{:S(2)}) collective-permute-start(f32[]{:T(128)} %add.87), channel_id=1, source_target_pairs={{0,2},{1,3},{2,0},{3,1},{4,6},{5,7},{6,4},{7,5},{8,10},{9,11},{10,... | collective-permute-start | bytes 20 | tf_op jit(solution)/shard_map/ppermute | solution.py:286

commit v10 on v6

--- a/solution.py
+++ b/solution.py
@@ -269,7 +269,7 @@
     )
     total_energy = slab_sum(energy)
     potential = (total_energy / (atoms_here * lax.axis_size("slab"))).reshape(1)
-    state = jnp.concatenate([coords, speeds], 0)
+    state = jnp.concatenate([coords, speeds], 0) + 0.0 * total_energy
     swapped = exchange(state, swap_pairs)
     return (swapped[:3][None], swapped[3:][None], potential)
 

time: 181 us -> 191 us (1.055)
  Pallas kernels: 47 us -> 56.6 us
  waiting for transfers between devices: 77.2 us -> 83 us
  starting transfers between devices: 28.3 us -> 22.9 us
    all_to_all x1, waiting for transfers between devices: 0.01 us -> 10.2 us  [exchange(): gathered = lax.all_to_all(routed, 'rep', 0, 0, tiled=True)]
    pallas_call x5, Pallas kernels: 47 us -> 56.6 us  [slab_pairs(): pl.pallas_call(pair_kernel, out_shape=(jax.ShapeDtypeStruct((3, width, CL...]
    ppermute x11, waiting for transfers between devices: 61.7 us -> 55.6 us  [from_behind(): return lax.ppermute(value, axis, pairs)]
    ppermute x11, starting transfers between devices: 9.71 us -> 6.16 us  [from_behind(): return lax.ppermute(value, axis, pairs)]
    ppermute x2, starting transfers between devices: 3.88 us -> 1.48 us  [slab_sum(): value = value + lax.ppermute(value, 'slab', pairs)]
  transfers between devices with their start and end apart: 15 -> 15, of which waited for: 12 -> 13; matrix products, arithmetic and copies ran while one was open for 2% -> 2% of each run, Pallas kernels for 0% -> 0%
where the time goes in v10:
time: 191 us; the launch traced here: 189 us
  waiting for transfers between devices  83 us (43%)
  Pallas kernels  56.6 us (30%)
  starting transfers between devices  22.9 us (12%)
  local copies, waits for them, and re-layouts  11.6 us (6%)
  other arithmetic  6.16 us (3%)
  between operations  5.39 us (3%)
  matrix products  3.04 us (2%)
    pallas_call x5, Pallas kernels, slab_pairs(): pl.pallas_call(pair_kernel, out_shape=(jax.ShapeDtypeStruct((3, width, CL...  56.6 us
    ppermute x11, waiting for transfers between devices, from_behind(): return lax.ppermute(value, axis, pairs)  55.6 us
    all_to_all x1, starting transfers between devices, exchange(): spread = lax.all_to_all(chunks, 'rep', 0, 0, tiled=True)  10.7 us
    all_to_all x1, waiting for transfers between devices, exchange(): gathered = lax.all_to_all(routed, 'rep', 0, 0, tiled=True)  10.2 us
    all_to_all x1, waiting for transfers between devices, exchange(): spread = lax.all_to_all(chunks, 'rep', 0, 0, tiled=True)  10.2 us
    ppermute x2, waiting for transfers between devices, slab_sum(): value = value + lax.ppermute(value, 'slab', pairs)  7.01 us
    ppermute x11, starting transfers between devices, from_behind(): return lax.ppermute(value, axis, pairs)  6.16 us
    all_to_all x1, starting transfers between devices, exchange(): gathered = lax.all_to_all(routed, 'rep', 0, 0, tiled=True)  4.62 us
  transfers between devices with their start and end apart: 15, of which 13 were waited for; matrix products, arithmetic and copies ran while one was open for 2% of the time, Pallas kernels for 0%

profile of v10, /device:TPU:0, one launch (start us, length us, event | category | flops | bytes accessed | tf_op | source)
XLA Modules:
  0.0 189.1 jit_solution(16868360498173127221)
XLA Ops:
  0.6 0.8 stack.24
  1.5 0.7 copy-done.2
  2.4 4.9 %collective-permute-start.3 = (f32[2,1024]{1,0:T(2,128)S(1)}, f32[2,1024]{1,0:T(2,128)S(1)}, u32[]{:S(2)}, u32[]{:S(2)}) collective-permute-start(f32[2,1024]{1,0:T(2,128)S(1)} %reshape.156), channel_id=1, source_target_pairs={{0,3},{1,0},{2,1},{3,2},{4,7},{5,4},{6,5},{7,6},{8,11},{9,8},{10,9... | collective-permute-start | bytes 24584 | tf_op jit(solution)/shard_map/ppermute | solution.py:145
  7.9 0.7 collective-permute-start.2
  9.0 0.6 copy-done.4
  11.4 0.6 copy-done.9
  12.2 10.8 %shard_map.130 = (f32[3,80,64]{2,1,0:T(8,128)S(1)}, f32[32,128]{1,0:T(8,128)S(1)}) custom-call(s32[2,192]{1,0:T(2,128)S(1)} %pad_add_fusion.tiles_ref, s32[1]{0:T(128)} %bitcast.81.count_ref, f32[3,80,64]{2,1,0:T(8,128)S(1)} %pad_maximum_fusion.1.ext_ref, f32[3,80,64]{2,1,0:T(8,128)S(1)} %pad_maximum_fusion.2.prm_ref), custom_call_target="tpu_custom_call" | custom-call | tf_op jit(solution)/shard_map/pallas_call | solution.py:121
  23.3 0.6 reduce_sum.38
  23.9 8.4 %collective-permute-done.4 = f32[3,1024]{1,0:T(4,128)S(1)} collective-permute-done((f32[3,1024]{1,0:T(4,128)S(1)}, f32[3,1024]{1,0:T(4,128)S(1)}, u32[]{:S(2)}, u32[]{:S(2)}) %collective-permute-start.4) | collective-permute-done | bytes 12320 | tf_op jit(solution)/shard_map/ppermute | solution.py:145
  32.4 0.3 fusion.11
  32.9 0.6 copy-done
  33.5 101.3 %while.17 = (s32[]{:T(128)}, f32[3,4096]{1,0:T(4,128)S(1)}, f32[3,4096]{1,0:T(4,128)S(1)}, f32[3,4096]{1,0:T(4,128)S(1)}, f32[]{:T(128)}, /*index=5*/f32[4096]{0...) while((s32[]{:T(128)}, f32[3,4096]{1,0:T(4,128)S(1)}, ...), condition=%wide.region_7.8_spmd.clone, body=%wide.region_5.0_spmd.clone.sunk | while | flops 4859905 | bytes 1311073 | solution.py:267
  34.0 1.4 collective-permute-done
  35.7 11.5 %eval_jaxpr.1 = (f32[3,80,64]{2,1,0:T(8,128)S(1)}, f32[32,128]{1,0:T(8,128)S(1)}) custom-call(s32[2,192]{1,0:T(2,128)S(1)} %get-tuple-element.234.tiles_ref, s32[1]{0:T(128)} %bitcast.79.count_ref, f32[3,80,64]{2,1,0:T(8,128)S(1)} %pad_maximum_fusion.4.ext_ref, f32[3,80,64]{2,1,0:T(8,128)S(1)} %get-tuple-element.235.prm_ref), custom_call_target="tpu_custom_call" | custom-call | tf_op jit(solution)/shard_map/while/body/eval_jaxpr/pallas_call | solution.py:121
  47.2 0.6 reduce_sum.43
  47.9 10.3 %collective-permute-done.1 = f32[3,1024]{1,0:T(4,128)S(1)} collective-permute-done((f32[3,1024]{1,0:T(4,128)S(1)}, f32[3,1024]{1,0:T(4,128)S(1)}, u32[]{:S(2)}, u32[]{:S(2)}) %collective-permute-start.1) | collective-permute-done | bytes 12320 | tf_op jit(solution)/shard_map/while/body/eval_jaxpr/ppermute | solution.py:145
  58.3 0.4 fusion.41
  59.0 0.2 convolution_bitcast_fusion.6
  59.4 1.4 collective-permute-done
  61.0 11.5 %eval_jaxpr.1 = (f32[3,80,64]{2,1,0:T(8,128)S(1)}, f32[32,128]{1,0:T(8,128)S(1)}) custom-call(s32[2,192]{1,0:T(2,128)S(1)} %get-tuple-element.234.tiles_ref, s32[1]{0:T(128)} %bitcast.79.count_ref, f32[3,80,64]{2,1,0:T(8,128)S(1)} %pad_maximum_fusion.4.ext_ref, f32[3,80,64]{2,1,0:T(8,128)S(1)} %get-tuple-element.235.prm_ref), custom_call_target="tpu_custom_call" | custom-call | tf_op jit(solution)/shard_map/while/body/eval_jaxpr/pallas_call | solution.py:121
  72.6 0.6 reduce_sum.43
  73.2 10.3 %collective-permute-done.1 = f32[3,1024]{1,0:T(4,128)S(1)} collective-permute-done((f32[3,1024]{1,0:T(4,128)S(1)}, f32[3,1024]{1,0:T(4,128)S(1)}, u32[]{:S(2)}, u32[]{:S(2)}) %collective-permute-start.1) | collective-permute-done | bytes 12320 | tf_op jit(solution)/shard_map/while/body/eval_jaxpr/ppermute | solution.py:145
  83.6 0.4 fusion.41
  84.7 1.4 collective-permute-done
  86.3 11.5 %eval_jaxpr.1 = (f32[3,80,64]{2,1,0:T(8,128)S(1)}, f32[32,128]{1,0:T(8,128)S(1)}) custom-call(s32[2,192]{1,0:T(2,128)S(1)} %get-tuple-element.234.tiles_ref, s32[1]{0:T(128)} %bitcast.79.count_ref, f32[3,80,64]{2,1,0:T(8,128)S(1)} %pad_maximum_fusion.4.ext_ref, f32[3,80,64]{2,1,0:T(8,128)S(1)} %get-tuple-element.235.prm_ref), custom_call_target="tpu_custom_call" | custom-call | tf_op jit(solution)/shard_map/while/body/eval_jaxpr/pallas_call | solution.py:121
  97.9 0.6 reduce_sum.43
  98.5 10.3 %collective-permute-done.1 = f32[3,1024]{1,0:T(4,128)S(1)} collective-permute-done((f32[3,1024]{1,0:T(4,128)S(1)}, f32[3,1024]{1,0:T(4,128)S(1)}, u32[]{:S(2)}, u32[]{:S(2)}) %collective-permute-start.1) | collective-permute-done | bytes 12320 | tf_op jit(solution)/shard_map/while/body/eval_jaxpr/ppermute | solution.py:145
  108.9 0.4 fusion.41
  110.0 1.4 collective-permute-done
  111.6 11.5 %eval_jaxpr.1 = (f32[3,80,64]{2,1,0:T(8,128)S(1)}, f32[32,128]{1,0:T(8,128)S(1)}) custom-call(s32[2,192]{1,0:T(2,128)S(1)} %get-tuple-element.234.tiles_ref, s32[1]{0:T(128)} %bitcast.79.count_ref, f32[3,80,64]{2,1,0:T(8,128)S(1)} %pad_maximum_fusion.4.ext_ref, f32[3,80,64]{2,1,0:T(8,128)S(1)} %get-tuple-element.235.prm_ref), custom_call_target="tpu_custom_call" | custom-call | tf_op jit(solution)/shard_map/while/body/eval_jaxpr/pallas_call | solution.py:121
  123.2 0.6 reduce_sum.43
  123.8 10.3 %collective-permute-done.1 = f32[3,1024]{1,0:T(4,128)S(1)} collective-permute-done((f32[3,1024]{1,0:T(4,128)S(1)}, f32[3,1024]{1,0:T(4,128)S(1)}, u32[]{:S(2)}, u32[]{:S(2)}) %collective-permute-start.1) | collective-permute-done | bytes 12320 | tf_op jit(solution)/shard_map/while/body/eval_jaxpr/ppermute | solution.py:145
  134.3 0.4 fusion.41
  135.3 0.9 collective-permute-done.5
  137.5 1.4 collective-permute-start.6
  138.9 6.1 %collective-permute-done.6 = f32[]{:T(128)} collective-permute-done((f32[]{:T(128)}, f32[]{:T(128)}, u32[]{:S(2)}, u32[]{:S(2)}) %collective-permute-start.6) | collective-permute-done | bytes 36 | tf_op jit(solution)/shard_map/ppermute | solution.py:282
  145.8 0.8 reshape.193
  146.6 10.7 %all-to-all-start = ((f32[64,1,384]{2,1,0:T(1,128)}), f32[64,1,384]{2,1,0:T(1,128)S(1)}, u32[]{:S(2)}, u32[]{:S(2)}) async-start(f32[64,1,384]{2,1,0:T(1,128)} %reshape.193), calls=%async_computation | async-start | bytes 196608 | tf_op jit(solution)/shard_map/all_to_all | solution.py:165
  157.3 10.2 %all-to-all-done = f32[64,1,384]{2,1,0:T(1,128)S(1)} async-done(((f32[64,1,384]{2,1,0:T(1,128)}), f32[64,1,384]{2,1,0:T(1,128)S(1)}, u32[]{:S(2)}, u32[]{:S(2)}) %all-to-all-start) | async-done | bytes 98336 | tf_op jit(solution)/shard_map/all_to_all | solution.py:165
  167.5 0.5 broadcast.56
  168.0 0.9 reduce.11
  169.0 0.6 gather_fusion
  169.8 0.8 reshape.195
  170.6 4.6 %all-to-all-start.1 = ((f32[64,1,384]{2,1,0:T(1,128)}), f32[64,1,384]{2,1,0:T(1,128)S(1)}, u32[]{:S(2)}, u32[]{:S(2)}) async-start(f32[64,1,384]{2,1,0:T(1,128)} %reshape.195), calls=%async_computation.1 | async-start | bytes 196608 | tf_op jit(solution)/shard_map/all_to_all | solution.py:167
  175.2 10.2 %all-to-all-done.1 = f32[64,1,384]{2,1,0:T(1,128)S(1)} async-done(((f32[64,1,384]{2,1,0:T(1,128)}), f32[64,1,384]{2,1,0:T(1,128)S(1)}, u32[]{:S(2)}, u32[]{:S(2)}) %all-to-all-start.1) | async-done | bytes 98336 | tf_op jit(solution)/shard_map/all_to_all | solution.py:167
  185.4 0.9 reduce.12
  186.5 0.7 broadcast_in_dim.44
  187.2 0.7 broadcast_in_dim.45
  (126 shorter events, 7.2 us)
Async XLA Ops:
  0.6 0.8 copy-start.3
  1.5 0.7 copy-start.2
  2.2 5.2 %copy-start.1 = (f32[1,3,4096]{2,0,1:T(1,128)S(1)}, f32[1,3,4096]{2,0,1:T(1,128)}, u32[]{:S(2)}) copy-start(f32[1,3,4096]{2,0,1:T(1,128)} %param.13) | copy-start | bytes 147460
  2.4 8.6 %collective-permute-start.3 = (f32[2,1024]{1,0:T(2,128)S(1)}, f32[2,1024]{1,0:T(2,128)S(1)}, u32[]{:S(2)}, u32[]{:S(2)}) collective-permute-start(f32[2,1024]{1,0:T(2,128)S(1)} %reshape.156), channel_id=1, source_target_pairs={{0,3},{1,0},{2,1},{3,2},{4,7},{5,4},{6,5},{7,6},{8,11},{9,8},{10,9... | collective-permute-start | bytes 24584 | tf_op jit(solution)/shard_map/ppermute | solution.py:145
  7.6 1.0 copy-start.8
  7.6 1.2 copy-start.7
  7.8 1.0 copy-start.5
  7.9 3.4 %collective-permute-start.2 = (f32[3,1024]{1,0:T(4,128)S(1)}, f32[3,1024]{1,0:T(4,128)S(1)}, u32[]{:S(2)}, u32[]{:S(2)}) collective-permute-start(f32[3,1024]{1,0:T(4,128)S(1)} %reshape.154), channel_id=1, source_target_pairs={{0,3},{1,0},{2,1},{3,2},{4,7},{5,4},{6,5},{7,6},{8,11},{9,8},{10,9... | collective-permute-start | bytes 36872 | tf_op jit(solution)/shard_map/ppermute | solution.py:145
  9.0 0.7 copy-start.4
  11.3 0.7 copy-start.9
  23.1 9.3 %collective-permute-start.4 = (f32[3,1024]{1,0:T(4,128)S(1)}, f32[3,1024]{1,0:T(4,128)S(1)}, u32[]{:S(2)}, u32[]{:S(2)}) collective-permute-start(f32[3,1024]{1,0:T(4,128)S(1)} %reshape.157), channel_id=1, source_target_pairs={{0,1},{1,2},{2,3},{3,0},{4,5},{5,6},{6,7},{7,4},{8,9},{9,10},{10,1... | collective-permute-start | bytes 36872 | tf_op jit(solution)/shard_map/ppermute | solution.py:145
  32.7 0.7 copy-start
  32.9 0.7 copy-start.6
  34.0 1.5 collective-permute-start
  47.2 11.0 %collective-permute-start.1 = (f32[3,1024]{1,0:T(4,128)S(1)}, f32[3,1024]{1,0:T(4,128)S(1)}, u32[]{:S(2)}, u32[]{:S(2)}) collective-permute-start(f32[3,1024]{1,0:T(4,128)S(1)} %reshape.206), channel_id=1, source_target_pairs={{0,1},{1,2},{2,3},{3,0},{4,5},{5,6},{6,7},{7,4},{8,9},{9,10},{10,1... | collective-permute-start | bytes 36872 | tf_op jit(solution)/shard_map/while/body/eval_jaxpr/ppermute | solution.py:145
  59.3 1.5 collective-permute-start
  72.5 11.0 %collective-permute-start.1 = (f32[3,1024]{1,0:T(4,128)S(1)}, f32[3,1024]{1,0:T(4,128)S(1)}, u32[]{:S(2)}, u32[]{:S(2)}) collective-permute-start(f32[3,1024]{1,0:T(4,128)S(1)} %reshape.206), channel_id=1, source_target_pairs={{0,1},{1,2},{2,3},{3,0},{4,5},{5,6},{6,7},{7,4},{8,9},{9,10},{10,1... | collective-permute-start | bytes 36872 | tf_op jit(solution)/shard_map/while/body/eval_jaxpr/ppermute | solution.py:145
  84.7 1.5 collective-permute-start
  97.9 11.0 %collective-permute-start.1 = (f32[3,1024]{1,0:T(4,128)S(1)}, f32[3,1024]{1,0:T(4,128)S(1)}, u32[]{:S(2)}, u32[]{:S(2)}) collective-permute-start(f32[3,1024]{1,0:T(4,128)S(1)} %reshape.206), channel_id=1, source_target_pairs={{0,1},{1,2},{2,3},{3,0},{4,5},{5,6},{6,7},{7,4},{8,9},{9,10},{10,1... | collective-permute-start | bytes 36872 | tf_op jit(solution)/shard_map/while/body/eval_jaxpr/ppermute | solution.py:145
  110.0 1.5 collective-permute-start
  123.2 11.0 %collective-permute-start.1 = (f32[3,1024]{1,0:T(4,128)S(1)}, f32[3,1024]{1,0:T(4,128)S(1)}, u32[]{:S(2)}, u32[]{:S(2)}) collective-permute-start(f32[3,1024]{1,0:T(4,128)S(1)} %reshape.206), channel_id=1, source_target_pairs={{0,1},{1,2},{2,3},{3,0},{4,5},{5,6},{6,7},{7,4},{8,9},{9,10},{10,1... | collective-permute-start | bytes 36872 | tf_op jit(solution)/shard_map/while/body/eval_jaxpr/ppermute | solution.py:145
  134.8 1.4 collective-permute-start.5
  137.5 7.5 %collective-permute-start.6 = (f32[]{:T(128)}, f32[]{:T(128)}, u32[]{:S(2)}, u32[]{:S(2)}) collective-permute-start(f32[]{:T(128)} %add.91), channel_id=1, source_target_pairs={{0,2},{1,3},{2,0},{3,1},{4,6},{5,7},{6,4},{7,5},{8,10},{9,11},{10,... | collective-permute-start | bytes 20 | tf_op jit(solution)/shard_map/ppermute | solution.py:282
  146.6 20.9 %all-to-all-start = ((f32[64,1,384]{2,1,0:T(1,128)}), f32[64,1,384]{2,1,0:T(1,128)S(1)}, u32[]{:S(2)}, u32[]{:S(2)}) async-start(f32[64,1,384]{2,1,0:T(1,128)} %reshape.193), calls=%async_computation | async-start | bytes 196608 | tf_op jit(solution)/shard_map/all_to_all | solution.py:165
  170.6 14.9 %all-to-all-start.1 = ((f32[64,1,384]{2,1,0:T(1,128)}), f32[64,1,384]{2,1,0:T(1,128)S(1)}, u32[]{:S(2)}, u32[]{:S(2)}) async-start(f32[64,1,384]{2,1,0:T(1,128)} %reshape.195), calls=%async_computation.1 | async-start | bytes 196608 | tf_op jit(solution)/shard_map/all_to_all | solution.py:167

commit v11 on v6

--- a/solution.py
+++ b/solution.py
@@ -54,10 +54,7 @@
 
 def from_columns(blocks, pick, place):
     width = blocks.shape[0]
-    folded = lax.dot_general(
-        blocks.reshape(width * HALF, 2 * CL), place, (((1,), (1,)), ((), ())),
-        precision=exact, preferred_element_type=jnp.float32,
-    )
+    folded = split_dot(blocks.reshape(width * HALF, 2 * CL), place, ((1,), (1,)))
     return jnp.sum(folded.reshape(width, HALF, CL) * pick[None], axis=1)
 
 

time: 181 us -> 175 us (0.967)
  waiting for transfers between devices: 77.2 us -> 54 us
  Pallas kernels: 47 us -> 68.8 us
  starting transfers between devices: 28.3 us -> 22.8 us
    ppermute x11, waiting for transfers between devices: 61.7 us -> 38 us  [from_behind(): return lax.ppermute(value, axis, pairs)]
    pallas_call x5, Pallas kernels: 47 us -> 68.8 us  [slab_pairs(): pl.pallas_call(pair_kernel, out_shape=(jax.ShapeDtypeStruct((3, width, CL...]
    ppermute x11, starting transfers between devices: 9.71 us -> 6.16 us  [from_behind(): return lax.ppermute(value, axis, pairs)]
where the time goes in v11:
time: 175 us; the launch traced here: 172 us
  Pallas kernels  68.8 us (39%)
  waiting for transfers between devices  54 us (31%)
  starting transfers between devices  22.8 us (13%)
  local copies, waits for them, and re-layouts  11.5 us (7%)
  other arithmetic  6.12 us (3%)
  between operations  5.13 us (3%)
  matrix products  3.03 us (2%)
    pallas_call x5, Pallas kernels, slab_pairs(): pl.pallas_call(pair_kernel, out_shape=(jax.ShapeDtypeStruct((3, width, CL...  68.8 us
    ppermute x11, waiting for transfers between devices, from_behind(): return lax.ppermute(value, axis, pairs)  38 us
    all_to_all x1, waiting for transfers between devices, exchange(): spread = lax.all_to_all(chunks, 'rep', 0, 0, tiled=True)  10.2 us
    all_to_all x1, starting transfers between devices, exchange(): spread = lax.all_to_all(chunks, 'rep', 0, 0, tiled=True)  8.58 us
    ppermute x11, starting transfers between devices, from_behind(): return lax.ppermute(value, axis, pairs)  6.16 us
    ppermute x2, waiting for transfers between devices, slab_sum(): value = value + lax.ppermute(value, 'slab', pairs)  5.74 us
    all_to_all x1, starting transfers between devices, exchange(): gathered = lax.all_to_all(routed, 'rep', 0, 0, tiled=True)  4.62 us
    unnamed x25, local copies, waits for them, and re-layouts  4.41 us
  transfers between devices with their start and end apart: 15, of which 12 were waited for; matrix products, arithmetic and copies ran while one was open for 2% of the time, Pallas kernels for 0%

profile of v11, /device:TPU:0, one launch (start us, length us, event | category | flops | bytes accessed | tf_op | source)
XLA Modules:
  0.0 171.7 jit_solution(15443503219265034823)
XLA Ops:
  0.6 0.8 stack.24
  1.5 0.7 copy-done.2
  2.4 4.9 %collective-permute-start.3 = (f32[2,1024]{1,0:T(2,128)S(1)}, f32[2,1024]{1,0:T(2,128)S(1)}, u32[]{:S(2)}, u32[]{:S(2)}) collective-permute-start(f32[2,1024]{1,0:T(2,128)S(1)} %reshape.156), channel_id=1, source_target_pairs={{0,3},{1,0},{2,1},{3,2},{4,7},{5,4},{6,5},{7,6},{8,11},{9,8},{10,9... | collective-permute-start | bytes 24584 | tf_op jit(solution)/shard_map/ppermute | solution.py:142
  7.9 0.7 collective-permute-start.2
  9.0 0.6 copy-done.4
  11.4 0.6 copy-done.9
  12.2 13.2 %shard_map.130 = (f32[3,80,64]{2,1,0:T(8,128)S(1)}, f32[32,128]{1,0:T(8,128)S(1)}) custom-call(s32[2,192]{1,0:T(2,128)S(1)} %pad_add_fusion.tiles_ref, s32[1]{0:T(128)} %bitcast.82.count_ref, f32[3,80,64]{2,1,0:T(8,128)S(1)} %pad_maximum_fusion.2.ext_ref, f32[3,80,64]{2,1,0:T(8,128)S(1)} %pad_maximum_fusion.3.prm_ref), custom_call_target="tpu_custom_call" | custom-call | tf_op jit(solution)/shard_map/pallas_call | solution.py:118
  25.8 0.6 reduce_sum.38
  26.4 6.4 %collective-permute-done.4 = f32[3,1024]{1,0:T(4,128)S(1)} collective-permute-done((f32[3,1024]{1,0:T(4,128)S(1)}, f32[3,1024]{1,0:T(4,128)S(1)}, u32[]{:S(2)}, u32[]{:S(2)}) %collective-permute-start.4) | collective-permute-done | bytes 12320 | tf_op jit(solution)/shard_map/ppermute | solution.py:142
  32.9 0.3 fusion.11
  33.3 0.6 copy-done
  34.0 95.5 %while.17 = (s32[]{:T(128)}, f32[3,4096]{1,0:T(4,128)S(1)}, f32[3,4096]{1,0:T(4,128)S(1)}, f32[3,4096]{1,0:T(4,128)S(1)}, f32[]{:T(128)}, /*index=5*/f32[4096]{0...) while((s32[]{:T(128)}, f32[3,4096]{1,0:T(4,128)S(1)}, ...), condition=%wide.region_7.8_spmd.clone, body=%wide.region_5.0_spmd.clone.sunk | while | flops 4859905 | bytes 1311073 | solution.py:264
  34.5 1.4 collective-permute-done
  36.1 13.9 %eval_jaxpr.1 = (f32[3,80,64]{2,1,0:T(8,128)S(1)}, f32[32,128]{1,0:T(8,128)S(1)}) custom-call(s32[2,192]{1,0:T(2,128)S(1)} %get-tuple-element.234.tiles_ref, s32[1]{0:T(128)} %bitcast.80.count_ref, f32[3,80,64]{2,1,0:T(8,128)S(1)} %pad_maximum_fusion.5.ext_ref, f32[3,80,64]{2,1,0:T(8,128)S(1)} %get-tuple-element.235.prm_ref), custom_call_target="tpu_custom_call" | custom-call | tf_op jit(solution)/shard_map/while/body/eval_jaxpr/pallas_call | solution.py:118
  50.1 0.6 reduce_sum.43
  50.8 6.5 %collective-permute-done.1 = f32[3,1024]{1,0:T(4,128)S(1)} collective-permute-done((f32[3,1024]{1,0:T(4,128)S(1)}, f32[3,1024]{1,0:T(4,128)S(1)}, u32[]{:S(2)}, u32[]{:S(2)}) %collective-permute-start.1) | collective-permute-done | bytes 12320 | tf_op jit(solution)/shard_map/while/body/eval_jaxpr/ppermute | solution.py:142
  57.3 0.4 fusion.40
  58.0 0.2 convolution_bitcast_fusion.6
  58.4 1.4 collective-permute-done
  60.0 13.9 %eval_jaxpr.1 = (f32[3,80,64]{2,1,0:T(8,128)S(1)}, f32[32,128]{1,0:T(8,128)S(1)}) custom-call(s32[2,192]{1,0:T(2,128)S(1)} %get-tuple-element.234.tiles_ref, s32[1]{0:T(128)} %bitcast.80.count_ref, f32[3,80,64]{2,1,0:T(8,128)S(1)} %pad_maximum_fusion.5.ext_ref, f32[3,80,64]{2,1,0:T(8,128)S(1)} %get-tuple-element.235.prm_ref), custom_call_target="tpu_custom_call" | custom-call | tf_op jit(solution)/shard_map/while/body/eval_jaxpr/pallas_call | solution.py:118
  74.0 0.6 reduce_sum.43
  74.6 6.5 %collective-permute-done.1 = f32[3,1024]{1,0:T(4,128)S(1)} collective-permute-done((f32[3,1024]{1,0:T(4,128)S(1)}, f32[3,1024]{1,0:T(4,128)S(1)}, u32[]{:S(2)}, u32[]{:S(2)}) %collective-permute-start.1) | collective-permute-done | bytes 12320 | tf_op jit(solution)/shard_map/while/body/eval_jaxpr/ppermute | solution.py:142
  81.2 0.4 fusion.40
  82.3 1.4 collective-permute-done
  83.9 13.9 %eval_jaxpr.1 = (f32[3,80,64]{2,1,0:T(8,128)S(1)}, f32[32,128]{1,0:T(8,128)S(1)}) custom-call(s32[2,192]{1,0:T(2,128)S(1)} %get-tuple-element.234.tiles_ref, s32[1]{0:T(128)} %bitcast.80.count_ref, f32[3,80,64]{2,1,0:T(8,128)S(1)} %pad_maximum_fusion.5.ext_ref, f32[3,80,64]{2,1,0:T(8,128)S(1)} %get-tuple-element.235.prm_ref), custom_call_target="tpu_custom_call" | custom-call | tf_op jit(solution)/shard_map/while/body/eval_jaxpr/pallas_call | solution.py:118
  97.9 0.6 reduce_sum.43
  98.5 6.5 %collective-permute-done.1 = f32[3,1024]{1,0:T(4,128)S(1)} collective-permute-done((f32[3,1024]{1,0:T(4,128)S(1)}, f32[3,1024]{1,0:T(4,128)S(1)}, u32[]{:S(2)}, u32[]{:S(2)}) %collective-permute-start.1) | collective-permute-done | bytes 12320 | tf_op jit(solution)/shard_map/while/body/eval_jaxpr/ppermute | solution.py:142
  105.1 0.4 fusion.40
  105.8 0.2 convolution_bitcast_fusion.6
  106.1 1.4 collective-permute-done
  107.8 13.9 %eval_jaxpr.1 = (f32[3,80,64]{2,1,0:T(8,128)S(1)}, f32[32,128]{1,0:T(8,128)S(1)}) custom-call(s32[2,192]{1,0:T(2,128)S(1)} %get-tuple-element.234.tiles_ref, s32[1]{0:T(128)} %bitcast.80.count_ref, f32[3,80,64]{2,1,0:T(8,128)S(1)} %pad_maximum_fusion.5.ext_ref, f32[3,80,64]{2,1,0:T(8,128)S(1)} %get-tuple-element.235.prm_ref), custom_call_target="tpu_custom_call" | custom-call | tf_op jit(solution)/shard_map/while/body/eval_jaxpr/pallas_call | solution.py:118
  121.8 0.6 reduce_sum.43
  122.4 6.5 %collective-permute-done.1 = f32[3,1024]{1,0:T(4,128)S(1)} collective-permute-done((f32[3,1024]{1,0:T(4,128)S(1)}, f32[3,1024]{1,0:T(4,128)S(1)}, u32[]{:S(2)}, u32[]{:S(2)}) %collective-permute-start.1) | collective-permute-done | bytes 12320 | tf_op jit(solution)/shard_map/while/body/eval_jaxpr/ppermute | solution.py:142
  128.9 0.4 fusion.40
  129.7 0.8 reshape.194
  130.5 8.6 %all-to-all-start = ((f32[64,1,384]{2,1,0:T(1,128)}), f32[64,1,384]{2,1,0:T(1,128)S(1)}, u32[]{:S(2)}, u32[]{:S(2)}) async-start(f32[64,1,384]{2,1,0:T(1,128)} %reshape.194), calls=%async_computation | async-start | bytes 196608 | tf_op jit(solution)/shard_map/all_to_all | solution.py:162
  139.1 10.2 %all-to-all-done = f32[64,1,384]{2,1,0:T(1,128)S(1)} async-done(((f32[64,1,384]{2,1,0:T(1,128)}), f32[64,1,384]{2,1,0:T(1,128)S(1)}, u32[]{:S(2)}, u32[]{:S(2)}) %all-to-all-start) | async-done | bytes 98336 | tf_op jit(solution)/shard_map/all_to_all | solution.py:162
  149.3 0.5 broadcast.55
  149.9 0.9 reduce.11
  150.8 0.6 gather_fusion
  151.6 0.8 reshape.196
  152.4 4.6 %all-to-all-start.1 = ((f32[64,1,384]{2,1,0:T(1,128)}), f32[64,1,384]{2,1,0:T(1,128)S(1)}, u32[]{:S(2)}, u32[]{:S(2)}) async-start(f32[64,1,384]{2,1,0:T(1,128)} %reshape.196), calls=%async_computation.1 | async-start | bytes 196608 | tf_op jit(solution)/shard_map/all_to_all | solution.py:164
  157.1 1.4 collective-permute-done.5
  159.7 3.3 %collective-permute-start.6 = (f32[]{:T(128)}, f32[]{:T(128)}, u32[]{:S(2)}, u32[]{:S(2)}) collective-permute-start(f32[]{:T(128)} %add.87), channel_id=1, source_target_pairs={{0,2},{1,3},{2,0},{3,1},{4,6},{5,7},{6,4},{7,5},{8,10},{9,11},{10,... | collective-permute-start | bytes 20 | tf_op jit(solution)/shard_map/ppermute | solution.py:279
  163.1 4.3 %collective-permute-done.6 = f32[]{:T(128)} collective-permute-done((f32[]{:T(128)}, f32[]{:T(128)}, u32[]{:S(2)}, u32[]{:S(2)}) %collective-permute-start.6) | collective-permute-done | bytes 36 | tf_op jit(solution)/shard_map/ppermute | solution.py:279
  168.0 0.9 reduce.12
  169.1 0.7 broadcast_in_dim.44
  169.8 0.7 broadcast_in_dim.45
  (124 shorter events, 6.8 us)
Async XLA Ops:
  0.6 0.8 copy-start.3
  1.5 0.7 copy-start.2
  2.2 5.2 %copy-start.1 = (f32[1,3,4096]{2,0,1:T(1,128)S(1)}, f32[1,3,4096]{2,0,1:T(1,128)}, u32[]{:S(2)}) copy-start(f32[1,3,4096]{2,0,1:T(1,128)} %param.13) | copy-start | bytes 147460
  2.4 8.6 %collective-permute-start.3 = (f32[2,1024]{1,0:T(2,128)S(1)}, f32[2,1024]{1,0:T(2,128)S(1)}, u32[]{:S(2)}, u32[]{:S(2)}) collective-permute-start(f32[2,1024]{1,0:T(2,128)S(1)} %reshape.156), channel_id=1, source_target_pairs={{0,3},{1,0},{2,1},{3,2},{4,7},{5,4},{6,5},{7,6},{8,11},{9,8},{10,9... | collective-permute-start | bytes 24584 | tf_op jit(solution)/shard_map/ppermute | solution.py:142
  7.6 1.0 copy-start.8
  7.6 1.2 copy-start.7
  7.8 1.0 copy-start.5
  7.9 3.4 %collective-permute-start.2 = (f32[3,1024]{1,0:T(4,128)S(1)}, f32[3,1024]{1,0:T(4,128)S(1)}, u32[]{:S(2)}, u32[]{:S(2)}) collective-permute-start(f32[3,1024]{1,0:T(4,128)S(1)} %reshape.154), channel_id=1, source_target_pairs={{0,3},{1,0},{2,1},{3,2},{4,7},{5,4},{6,5},{7,6},{8,11},{9,8},{10,9... | collective-permute-start | bytes 36872 | tf_op jit(solution)/shard_map/ppermute | solution.py:142
  9.0 0.7 copy-start.4
  11.3 0.7 copy-start.9
  25.5 7.3 %collective-permute-start.4 = (f32[3,1024]{1,0:T(4,128)S(1)}, f32[3,1024]{1,0:T(4,128)S(1)}, u32[]{:S(2)}, u32[]{:S(2)}) collective-permute-start(f32[3,1024]{1,0:T(4,128)S(1)} %reshape.157), channel_id=1, source_target_pairs={{0,1},{1,2},{2,3},{3,0},{4,5},{5,6},{6,7},{7,4},{8,9},{9,10},{10,1... | collective-permute-start | bytes 36872 | tf_op jit(solution)/shard_map/ppermute | solution.py:142
  33.2 0.7 copy-start
  33.3 0.7 copy-start.6
  34.5 1.5 collective-permute-start
  50.1 7.1 %collective-permute-start.1 = (f32[3,1024]{1,0:T(4,128)S(1)}, f32[3,1024]{1,0:T(4,128)S(1)}, u32[]{:S(2)}, u32[]{:S(2)}) collective-permute-start(f32[3,1024]{1,0:T(4,128)S(1)} %reshape.207), channel_id=1, source_target_pairs={{0,1},{1,2},{2,3},{3,0},{4,5},{5,6},{6,7},{7,4},{8,9},{9,10},{10,1... | collective-permute-start | bytes 36872 | tf_op jit(solution)/shard_map/while/body/eval_jaxpr/ppermute | solution.py:142
  58.3 1.5 collective-permute-start
  74.0 7.1 %collective-permute-start.1 = (f32[3,1024]{1,0:T(4,128)S(1)}, f32[3,1024]{1,0:T(4,128)S(1)}, u32[]{:S(2)}, u32[]{:S(2)}) collective-permute-start(f32[3,1024]{1,0:T(4,128)S(1)} %reshape.207), channel_id=1, source_target_pairs={{0,1},{1,2},{2,3},{3,0},{4,5},{5,6},{6,7},{7,4},{8,9},{9,10},{10,1... | collective-permute-start | bytes 36872 | tf_op jit(solution)/shard_map/while/body/eval_jaxpr/ppermute | solution.py:142
  82.2 1.5 collective-permute-start
  97.9 7.1 %collective-permute-start.1 = (f32[3,1024]{1,0:T(4,128)S(1)}, f32[3,1024]{1,0:T(4,128)S(1)}, u32[]{:S(2)}, u32[]{:S(2)}) collective-permute-start(f32[3,1024]{1,0:T(4,128)S(1)} %reshape.207), channel_id=1, source_target_pairs={{0,1},{1,2},{2,3},{3,0},{4,5},{5,6},{6,7},{7,4},{8,9},{9,10},{10,1... | collective-permute-start | bytes 36872 | tf_op jit(solution)/shard_map/while/body/eval_jaxpr/ppermute | solution.py:142
  106.1 1.5 collective-permute-start
  121.7 7.1 %collective-permute-start.1 = (f32[3,1024]{1,0:T(4,128)S(1)}, f32[3,1024]{1,0:T(4,128)S(1)}, u32[]{:S(2)}, u32[]{:S(2)}) collective-permute-start(f32[3,1024]{1,0:T(4,128)S(1)} %reshape.207), channel_id=1, source_target_pairs={{0,1},{1,2},{2,3},{3,0},{4,5},{5,6},{6,7},{7,4},{8,9},{9,10},{10,1... | collective-permute-start | bytes 36872 | tf_op jit(solution)/shard_map/while/body/eval_jaxpr/ppermute | solution.py:142
  130.5 18.8 %all-to-all-start = ((f32[64,1,384]{2,1,0:T(1,128)}), f32[64,1,384]{2,1,0:T(1,128)S(1)}, u32[]{:S(2)}, u32[]{:S(2)}) async-start(f32[64,1,384]{2,1,0:T(1,128)} %reshape.194), calls=%async_computation | async-start | bytes 196608 | tf_op jit(solution)/shard_map/all_to_all | solution.py:162
  152.4 15.6 %all-to-all-start.1 = ((f32[64,1,384]{2,1,0:T(1,128)}), f32[64,1,384]{2,1,0:T(1,128)S(1)}, u32[]{:S(2)}, u32[]{:S(2)}) async-start(f32[64,1,384]{2,1,0:T(1,128)} %reshape.196), calls=%async_computation.1 | async-start | bytes 196608 | tf_op jit(solution)/shard_map/all_to_all | solution.py:164
  157.0 1.5 collective-permute-start.5
  159.7 7.7 %collective-permute-start.6 = (f32[]{:T(128)}, f32[]{:T(128)}, u32[]{:S(2)}, u32[]{:S(2)}) collective-permute-start(f32[]{:T(128)} %add.87), channel_id=1, source_target_pairs={{0,2},{1,3},{2,0},{3,1},{4,6},{5,7},{6,4},{7,5},{8,10},{9,11},{10,... | collective-permute-start | bytes 20 | tf_op jit(solution)/shard_map/ppermute | solution.py:279

commit v12 on v11

--- a/solution.py
+++ b/solution.py
@@ -103,10 +103,7 @@
     acc = lax.fori_loop(0, count_ref[0], body, jnp.zeros((HALF, 2 * CL), jnp.float32))
     en_ref[...] = acc
     for c in range(3):
-        f_j = lax.dot_general(
-            frow_ref[c], twice, (((1,), (1,)), ((), ())),
-            precision=exact, preferred_element_type=jnp.float32,
-        )
+        f_j = split_dot(frow_ref[c], twice, ((1,), (1,)))
         force_ref[c, :owned] = from_columns(fcol_ref[c], pick, place) + f_j[:owned]
         force_ref[c, owned:] = f_j[owned:]
 

time: 175 us -> 174 us (level)
  Pallas kernels: 68.8 us -> 37.3 us
  waiting for transfers between devices: 54 us -> 80 us
  starting transfers between devices: 22.8 us -> 28.3 us
    pallas_call x5, Pallas kernels: 68.8 us -> 37.3 us  [slab_pairs(): pl.pallas_call(pair_kernel, out_shape=(jax.ShapeDtypeStruct((3, width, CL...]
    ppermute x11, waiting for transfers between devices: 38 us -> 63.8 us  [from_behind(): return lax.ppermute(value, axis, pairs)]
    ppermute x11, starting transfers between devices: 6.16 us -> 9.66 us  [from_behind(): return lax.ppermute(value, axis, pairs)]
    all_to_all x1, starting transfers between devices: 8.58 us -> 10.9 us  [exchange(): spread = lax.all_to_all(chunks, 'rep', 0, 0, tiled=True)]
where the time goes in v12:
time: 174 us; the launch traced here: 172 us
  waiting for transfers between devices  80 us (46%)
  Pallas kernels  37.3 us (21%)
  starting transfers between devices  28.3 us (16%)
  local copies, waits for them, and re-layouts  11.5 us (7%)
  other arithmetic  6.11 us (4%)
  between operations  5.12 us (3%)
  matrix products  3.04 us (2%)
    ppermute x11, waiting for transfers between devices, from_behind(): return lax.ppermute(value, axis, pairs)  63.8 us
    pallas_call x5, Pallas kernels, slab_pairs(): pl.pallas_call(pair_kernel, out_shape=(jax.ShapeDtypeStruct((3, width, CL...  37.3 us
    all_to_all x1, starting transfers between devices, exchange(): spread = lax.all_to_all(chunks, 'rep', 0, 0, tiled=True)  10.9 us
    all_to_all x1, waiting for transfers between devices, exchange(): spread = lax.all_to_all(chunks, 'rep', 0, 0, tiled=True)  10.2 us
    ppermute x11, starting transfers between devices, from_behind(): return lax.ppermute(value, axis, pairs)  9.66 us
    ppermute x2, waiting for transfers between devices, slab_sum(): value = value + lax.ppermute(value, 'slab', pairs)  6.02 us
    all_to_all x1, starting transfers between devices, exchange(): gathered = lax.all_to_all(routed, 'rep', 0, 0, tiled=True)  4.62 us
    unnamed x25, local copies, waits for them, and re-layouts  4.41 us
  transfers between devices with their start and end apart: 15, of which 12 were waited for; matrix products, arithmetic and copies ran while one was open for 2% of the time, Pallas kernels for 0%

profile of v12, /device:TPU:0, one launch (start us, length us, event | category | flops | bytes accessed | tf_op | source)
XLA Modules:
  0.0 171.7 jit_solution(5100062305575275869)
XLA Ops:
  0.6 0.8 stack.24
  1.5 0.7 copy-done.2
  2.4 4.9 %collective-permute-start.3 = (f32[2,1024]{1,0:T(2,128)S(1)}, f32[2,1024]{1,0:T(2,128)S(1)}, u32[]{:S(2)}, u32[]{:S(2)}) collective-permute-start(f32[2,1024]{1,0:T(2,128)S(1)} %reshape.156), channel_id=1, source_target_pairs={{0,3},{1,0},{2,1},{3,2},{4,7},{5,4},{6,5},{7,6},{8,11},{9,8},{10,9... | collective-permute-start | bytes 24584 | tf_op jit(solution)/shard_map/ppermute | solution.py:139
  7.9 0.7 collective-permute-start.2
  9.0 0.6 copy-done.4
  11.4 0.6 copy-done.9
  12.2 6.9 %shard_map.130 = (f32[3,80,64]{2,1,0:T(8,128)S(1)}, f32[32,128]{1,0:T(8,128)S(1)}) custom-call(s32[2,192]{1,0:T(2,128)S(1)} %pad_add_fusion.tiles_ref, s32[1]{0:T(128)} %bitcast.82.count_ref, f32[3,80,64]{2,1,0:T(8,128)S(1)} %pad_maximum_fusion.2.ext_ref, f32[3,80,64]{2,1,0:T(8,128)S(1)} %pad_maximum_fusion.3.prm_ref), custom_call_target="tpu_custom_call" | custom-call | tf_op jit(solution)/shard_map/pallas_call | solution.py:115
  19.2 0.9 collective-permute-start.4
  20.1 0.6 reduce_sum.38
  20.7 10.1 %collective-permute-done.4 = f32[3,1024]{1,0:T(4,128)S(1)} collective-permute-done((f32[3,1024]{1,0:T(4,128)S(1)}, f32[3,1024]{1,0:T(4,128)S(1)}, u32[]{:S(2)}, u32[]{:S(2)}) %collective-permute-start.4) | collective-permute-done | bytes 12320 | tf_op jit(solution)/shard_map/ppermute | solution.py:139
  31.3 0.6 copy-done
  32.0 95.2 %while.17 = (s32[]{:T(128)}, f32[3,4096]{1,0:T(4,128)S(1)}, f32[3,4096]{1,0:T(4,128)S(1)}, f32[3,4096]{1,0:T(4,128)S(1)}, f32[]{:T(128)}, /*index=5*/f32[4096]{0...) while((s32[]{:T(128)}, f32[3,4096]{1,0:T(4,128)S(1)}, ...), condition=%wide.region_7.8_spmd.clone, body=%wide.region_5.0_spmd.clone.sunk | while | flops 4859905 | bytes 1311073 | solution.py:261
  32.5 1.4 collective-permute-done
  34.1 7.6 %eval_jaxpr.1 = (f32[3,80,64]{2,1,0:T(8,128)S(1)}, f32[32,128]{1,0:T(8,128)S(1)}) custom-call(s32[2,192]{1,0:T(2,128)S(1)} %get-tuple-element.234.tiles_ref, s32[1]{0:T(128)} %bitcast.80.count_ref, f32[3,80,64]{2,1,0:T(8,128)S(1)} %pad_maximum_fusion.5.ext_ref, f32[3,80,64]{2,1,0:T(8,128)S(1)} %get-tuple-element.235.prm_ref), custom_call_target="tpu_custom_call" | custom-call | tf_op jit(solution)/shard_map/while/body/eval_jaxpr/pallas_call | solution.py:115
  41.8 0.8 collective-permute-start.1
  42.6 0.6 reduce_sum.43
  43.2 12.0 %collective-permute-done.1 = f32[3,1024]{1,0:T(4,128)S(1)} collective-permute-done((f32[3,1024]{1,0:T(4,128)S(1)}, f32[3,1024]{1,0:T(4,128)S(1)}, u32[]{:S(2)}, u32[]{:S(2)}) %collective-permute-start.1) | collective-permute-done | bytes 12320 | tf_op jit(solution)/shard_map/while/body/eval_jaxpr/ppermute | solution.py:139
  56.3 1.4 collective-permute-done
  57.9 7.6 %eval_jaxpr.1 = (f32[3,80,64]{2,1,0:T(8,128)S(1)}, f32[32,128]{1,0:T(8,128)S(1)}) custom-call(s32[2,192]{1,0:T(2,128)S(1)} %get-tuple-element.234.tiles_ref, s32[1]{0:T(128)} %bitcast.80.count_ref, f32[3,80,64]{2,1,0:T(8,128)S(1)} %pad_maximum_fusion.5.ext_ref, f32[3,80,64]{2,1,0:T(8,128)S(1)} %get-tuple-element.235.prm_ref), custom_call_target="tpu_custom_call" | custom-call | tf_op jit(solution)/shard_map/while/body/eval_jaxpr/pallas_call | solution.py:115
  65.6 0.8 collective-permute-start.1
  66.4 0.6 reduce_sum.43
  67.0 12.0 %collective-permute-done.1 = f32[3,1024]{1,0:T(4,128)S(1)} collective-permute-done((f32[3,1024]{1,0:T(4,128)S(1)}, f32[3,1024]{1,0:T(4,128)S(1)}, u32[]{:S(2)}, u32[]{:S(2)}) %collective-permute-start.1) | collective-permute-done | bytes 12320 | tf_op jit(solution)/shard_map/while/body/eval_jaxpr/ppermute | solution.py:139
  79.0 0.4 fusion.40
  80.1 1.4 collective-permute-done
  81.7 7.6 %eval_jaxpr.1 = (f32[3,80,64]{2,1,0:T(8,128)S(1)}, f32[32,128]{1,0:T(8,128)S(1)}) custom-call(s32[2,192]{1,0:T(2,128)S(1)} %get-tuple-element.234.tiles_ref, s32[1]{0:T(128)} %bitcast.80.count_ref, f32[3,80,64]{2,1,0:T(8,128)S(1)} %pad_maximum_fusion.5.ext_ref, f32[3,80,64]{2,1,0:T(8,128)S(1)} %get-tuple-element.235.prm_ref), custom_call_target="tpu_custom_call" | custom-call | tf_op jit(solution)/shard_map/while/body/eval_jaxpr/pallas_call | solution.py:115
  89.5 0.7 collective-permute-start.1
  90.2 0.6 reduce_sum.43
  90.8 12.0 %collective-permute-done.1 = f32[3,1024]{1,0:T(4,128)S(1)} collective-permute-done((f32[3,1024]{1,0:T(4,128)S(1)}, f32[3,1024]{1,0:T(4,128)S(1)}, u32[]{:S(2)}, u32[]{:S(2)}) %collective-permute-start.1) | collective-permute-done | bytes 12320 | tf_op jit(solution)/shard_map/while/body/eval_jaxpr/ppermute | solution.py:139
  102.8 0.4 fusion.40
  103.9 1.4 collective-permute-done
  105.5 7.6 %eval_jaxpr.1 = (f32[3,80,64]{2,1,0:T(8,128)S(1)}, f32[32,128]{1,0:T(8,128)S(1)}) custom-call(s32[2,192]{1,0:T(2,128)S(1)} %get-tuple-element.234.tiles_ref, s32[1]{0:T(128)} %bitcast.80.count_ref, f32[3,80,64]{2,1,0:T(8,128)S(1)} %pad_maximum_fusion.5.ext_ref, f32[3,80,64]{2,1,0:T(8,128)S(1)} %get-tuple-element.235.prm_ref), custom_call_target="tpu_custom_call" | custom-call | tf_op jit(solution)/shard_map/while/body/eval_jaxpr/pallas_call | solution.py:115
  113.2 0.7 collective-permute-start.1
  114.0 0.6 reduce_sum.43
  114.6 12.0 %collective-permute-done.1 = f32[3,1024]{1,0:T(4,128)S(1)} collective-permute-done((f32[3,1024]{1,0:T(4,128)S(1)}, f32[3,1024]{1,0:T(4,128)S(1)}, u32[]{:S(2)}, u32[]{:S(2)}) %collective-permute-start.1) | collective-permute-done | bytes 12320 | tf_op jit(solution)/shard_map/while/body/eval_jaxpr/ppermute | solution.py:139
  127.5 0.8 reshape.194
  128.2 10.9 %all-to-all-start = ((f32[64,1,384]{2,1,0:T(1,128)}), f32[64,1,384]{2,1,0:T(1,128)S(1)}, u32[]{:S(2)}, u32[]{:S(2)}) async-start(f32[64,1,384]{2,1,0:T(1,128)} %reshape.194), calls=%async_computation | async-start | bytes 196608 | tf_op jit(solution)/shard_map/all_to_all | solution.py:159
  139.2 10.2 %all-to-all-done = f32[64,1,384]{2,1,0:T(1,128)S(1)} async-done(((f32[64,1,384]{2,1,0:T(1,128)}), f32[64,1,384]{2,1,0:T(1,128)S(1)}, u32[]{:S(2)}, u32[]{:S(2)}) %all-to-all-start) | async-done | bytes 98336 | tf_op jit(solution)/shard_map/all_to_all | solution.py:159
  149.4 0.5 broadcast.55
  149.9 0.9 reduce.11
  150.9 0.6 gather_fusion
  151.7 0.8 reshape.196
  152.4 4.6 %all-to-all-start.1 = ((f32[64,1,384]{2,1,0:T(1,128)}), f32[64,1,384]{2,1,0:T(1,128)S(1)}, u32[]{:S(2)}, u32[]{:S(2)}) async-start(f32[64,1,384]{2,1,0:T(1,128)} %reshape.196), calls=%async_computation.1 | async-start | bytes 196608 | tf_op jit(solution)/shard_map/all_to_all | solution.py:161
  157.2 1.4 collective-permute-done.5
  159.8 3.1 %collective-permute-start.6 = (f32[]{:T(128)}, f32[]{:T(128)}, u32[]{:S(2)}, u32[]{:S(2)}) collective-permute-start(f32[]{:T(128)} %add.87), channel_id=1, source_target_pairs={{0,2},{1,3},{2,0},{3,1},{4,6},{5,7},{6,4},{7,5},{8,10},{9,11},{10,... | collective-permute-start | bytes 20 | tf_op jit(solution)/shard_map/ppermute | solution.py:276
  162.9 4.6 %collective-permute-done.6 = f32[]{:T(128)} collective-permute-done((f32[]{:T(128)}, f32[]{:T(128)}, u32[]{:S(2)}, u32[]{:S(2)}) %collective-permute-start.6) | collective-permute-done | bytes 36 | tf_op jit(solution)/shard_map/ppermute | solution.py:276
  168.0 0.9 reduce.12
  169.1 0.7 broadcast_in_dim.44
  169.8 0.7 broadcast_in_dim.45
  (124 shorter events, 8.0 us)
Async XLA Ops:
  0.6 0.8 copy-start.3
  1.5 0.7 copy-start.2
  2.2 5.2 %copy-start.1 = (f32[1,3,4096]{2,0,1:T(1,128)S(1)}, f32[1,3,4096]{2,0,1:T(1,128)}, u32[]{:S(2)}) copy-start(f32[1,3,4096]{2,0,1:T(1,128)} %param.13) | copy-start | bytes 147460
  2.4 8.6 %collective-permute-start.3 = (f32[2,1024]{1,0:T(2,128)S(1)}, f32[2,1024]{1,0:T(2,128)S(1)}, u32[]{:S(2)}, u32[]{:S(2)}) collective-permute-start(f32[2,1024]{1,0:T(2,128)S(1)} %reshape.156), channel_id=1, source_target_pairs={{0,3},{1,0},{2,1},{3,2},{4,7},{5,4},{6,5},{7,6},{8,11},{9,8},{10,9... | collective-permute-start | bytes 24584 | tf_op jit(solution)/shard_map/ppermute | solution.py:139
  7.6 1.0 copy-start.8
  7.6 1.2 copy-start.7
  7.8 1.0 copy-start.5
  7.9 3.4 %collective-permute-start.2 = (f32[3,1024]{1,0:T(4,128)S(1)}, f32[3,1024]{1,0:T(4,128)S(1)}, u32[]{:S(2)}, u32[]{:S(2)}) collective-permute-start(f32[3,1024]{1,0:T(4,128)S(1)} %reshape.154), channel_id=1, source_target_pairs={{0,3},{1,0},{2,1},{3,2},{4,7},{5,4},{6,5},{7,6},{8,11},{9,8},{10,9... | collective-permute-start | bytes 36872 | tf_op jit(solution)/shard_map/ppermute | solution.py:139
  9.0 0.7 copy-start.4
  11.3 0.7 copy-start.9
  19.2 11.6 %collective-permute-start.4 = (f32[3,1024]{1,0:T(4,128)S(1)}, f32[3,1024]{1,0:T(4,128)S(1)}, u32[]{:S(2)}, u32[]{:S(2)}) collective-permute-start(f32[3,1024]{1,0:T(4,128)S(1)} %reshape.157), channel_id=1, source_target_pairs={{0,1},{1,2},{2,3},{3,0},{4,5},{5,6},{6,7},{7,4},{8,9},{9,10},{10,1... | collective-permute-start | bytes 36872 | tf_op jit(solution)/shard_map/ppermute | solution.py:139
  31.2 0.7 copy-start
  31.3 0.7 copy-start.6
  32.5 1.5 collective-permute-start
  41.8 13.3 %collective-permute-start.1 = (f32[3,1024]{1,0:T(4,128)S(1)}, f32[3,1024]{1,0:T(4,128)S(1)}, u32[]{:S(2)}, u32[]{:S(2)}) collective-permute-start(f32[3,1024]{1,0:T(4,128)S(1)} %reshape.207), channel_id=1, source_target_pairs={{0,1},{1,2},{2,3},{3,0},{4,5},{5,6},{6,7},{7,4},{8,9},{9,10},{10,1... | collective-permute-start | bytes 36872 | tf_op jit(solution)/shard_map/while/body/eval_jaxpr/ppermute | solution.py:139
  56.3 1.5 collective-permute-start
  65.6 13.4 %collective-permute-start.1 = (f32[3,1024]{1,0:T(4,128)S(1)}, f32[3,1024]{1,0:T(4,128)S(1)}, u32[]{:S(2)}, u32[]{:S(2)}) collective-permute-start(f32[3,1024]{1,0:T(4,128)S(1)} %reshape.207), channel_id=1, source_target_pairs={{0,1},{1,2},{2,3},{3,0},{4,5},{5,6},{6,7},{7,4},{8,9},{9,10},{10,1... | collective-permute-start | bytes 36872 | tf_op jit(solution)/shard_map/while/body/eval_jaxpr/ppermute | solution.py:139
  80.1 1.5 collective-permute-start
  89.5 13.3 %collective-permute-start.1 = (f32[3,1024]{1,0:T(4,128)S(1)}, f32[3,1024]{1,0:T(4,128)S(1)}, u32[]{:S(2)}, u32[]{:S(2)}) collective-permute-start(f32[3,1024]{1,0:T(4,128)S(1)} %reshape.207), channel_id=1, source_target_pairs={{0,1},{1,2},{2,3},{3,0},{4,5},{5,6},{6,7},{7,4},{8,9},{9,10},{10,1... | collective-permute-start | bytes 36872 | tf_op jit(solution)/shard_map/while/body/eval_jaxpr/ppermute | solution.py:139
  103.9 1.5 collective-permute-start
  113.2 13.3 %collective-permute-start.1 = (f32[3,1024]{1,0:T(4,128)S(1)}, f32[3,1024]{1,0:T(4,128)S(1)}, u32[]{:S(2)}, u32[]{:S(2)}) collective-permute-start(f32[3,1024]{1,0:T(4,128)S(1)} %reshape.207), channel_id=1, source_target_pairs={{0,1},{1,2},{2,3},{3,0},{4,5},{5,6},{6,7},{7,4},{8,9},{9,10},{10,1... | collective-permute-start | bytes 36872 | tf_op jit(solution)/shard_map/while/body/eval_jaxpr/ppermute | solution.py:139
  128.2 21.1 %all-to-all-start = ((f32[64,1,384]{2,1,0:T(1,128)}), f32[64,1,384]{2,1,0:T(1,128)S(1)}, u32[]{:S(2)}, u32[]{:S(2)}) async-start(f32[64,1,384]{2,1,0:T(1,128)} %reshape.194), calls=%async_computation | async-start | bytes 196608 | tf_op jit(solution)/shard_map/all_to_all | solution.py:159
  152.4 15.6 %all-to-all-start.1 = ((f32[64,1,384]{2,1,0:T(1,128)}), f32[64,1,384]{2,1,0:T(1,128)S(1)}, u32[]{:S(2)}, u32[]{:S(2)}) async-start(f32[64,1,384]{2,1,0:T(1,128)} %reshape.196), calls=%async_computation.1 | async-start | bytes 196608 | tf_op jit(solution)/shard_map/all_to_all | solution.py:161
  157.1 1.5 collective-permute-start.5
  159.8 7.7 %collective-permute-start.6 = (f32[]{:T(128)}, f32[]{:T(128)}, u32[]{:S(2)}, u32[]{:S(2)}) collective-permute-start(f32[]{:T(128)} %add.87), channel_id=1, source_target_pairs={{0,2},{1,3},{2,0},{3,1},{4,6},{5,7},{6,4},{7,5},{8,10},{9,11},{10,... | collective-permute-start | bytes 20 | tf_op jit(solution)/shard_map/ppermute | solution.py:276

commit v13 on v11

--- a/solution.py
+++ b/solution.py
@@ -47,8 +47,17 @@
 
 def to_columns(values, pick, place):
     width = values.shape[0]
-    picked = (values[:, None, :] * pick[None]).reshape(width * HALF, CL)
-    spread = split_dot(picked, place, ((1,), (0,)))
+    place_b = place.astype(jnp.bfloat16)
+    hi = values.astype(jnp.bfloat16)
+    rest = values - hi.astype(jnp.float32)
+    mid = rest.astype(jnp.bfloat16)
+    lo = (rest - mid.astype(jnp.float32)).astype(jnp.bfloat16)
+    chosen = pick[None] > 0.0
+    spread = None
+    for part in (hi, mid, lo):
+        picked = jnp.where(chosen, part[:, None, :], jnp.zeros((), jnp.bfloat16))
+        term = jnp.dot(picked.reshape(width * HALF, CL), place_b, preferred_element_type=jnp.float32)
+        spread = term if spread is None else spread + term
     return spread.reshape(width, HALF, 2 * CL)
 
 

time: 175 us -> 174 us (level)
  starting transfers between devices: 22.8 us -> 79.7 us
  Pallas kernels: 68.8 us -> 38.3 us
  waiting for transfers between devices: 54 us -> 28.3 us
    ppermute x11, starting transfers between devices: 6.16 us -> 53.4 us  [from_behind(): return lax.ppermute(value, axis, pairs)]
    pallas_call x5, Pallas kernels: 68.8 us -> 38.3 us  [slab_pairs(): pl.pallas_call(pair_kernel, out_shape=(jax.ShapeDtypeStruct((3, width, CL...]
    ppermute x11, waiting for transfers between devices: 38 us -> 11.6 us  [from_behind(): return lax.ppermute(value, axis, pairs)]
    all_to_all x1, starting transfers between devices: 8.58 us -> 18.9 us  [exchange(): spread = lax.all_to_all(chunks, 'rep', 0, 0, tiled=True)]
where the time goes in v13:
time: 174 us; the launch traced here: 172 us
  starting transfers between devices  79.7 us (46%)
  Pallas kernels  38.3 us (22%)
  waiting for transfers between devices  28.3 us (16%)
  local copies, waits for them, and re-layouts  11.5 us (7%)
  other arithmetic  6.11 us (4%)
  between operations  5.12 us (3%)
  matrix products  3.04 us (2%)
    ppermute x11, starting transfers between devices, from_behind(): return lax.ppermute(value, axis, pairs)  53.4 us
    pallas_call x5, Pallas kernels, slab_pairs(): pl.pallas_call(pair_kernel, out_shape=(jax.ShapeDtypeStruct((3, width, CL...  38.3 us
    all_to_all x1, starting transfers between devices, exchange(): spread = lax.all_to_all(chunks, 'rep', 0, 0, tiled=True)  18.9 us
    ppermute x11, waiting for transfers between devices, from_behind(): return lax.ppermute(value, axis, pairs)  11.6 us
    all_to_all x1, waiting for transfers between devices, exchange(): spread = lax.all_to_all(chunks, 'rep', 0, 0, tiled=True)  10.2 us
    ppermute x2, waiting for transfers between devices, slab_sum(): value = value + lax.ppermute(value, 'slab', pairs)  6.43 us
    all_to_all x1, starting transfers between devices, exchange(): gathered = lax.all_to_all(routed, 'rep', 0, 0, tiled=True)  4.62 us
    unnamed x25, local copies, waits for them, and re-layouts  4.41 us
  transfers between devices with their start and end apart: 15, of which 12 were waited for; matrix products, arithmetic and copies ran while one was open for 2% of the time, Pallas kernels for 0%

profile of v13, /device:TPU:0, one launch (start us, length us, event | category | flops | bytes accessed | tf_op | source)
XLA Modules:
  0.0 172.3 jit_solution(5713329147985062540)
XLA Ops:
  0.6 0.8 stack.24
  1.5 0.7 copy-done.2
  2.4 4.9 %collective-permute-start.3 = (f32[2,1024]{1,0:T(2,128)S(1)}, f32[2,1024]{1,0:T(2,128)S(1)}, u32[]{:S(2)}, u32[]{:S(2)}) collective-permute-start(f32[2,1024]{1,0:T(2,128)S(1)} %reshape.156), channel_id=1, source_target_pairs={{0,3},{1,0},{2,1},{3,2},{4,7},{5,4},{6,5},{7,6},{8,11},{9,8},{10,9... | collective-permute-start | bytes 24584 | tf_op jit(solution)/shard_map/ppermute | solution.py:151
  7.9 0.7 collective-permute-start.2
  9.0 0.6 copy-done.4
  11.4 0.6 copy-done.9
  12.2 7.2 %shard_map.130 = (f32[3,80,64]{2,1,0:T(8,128)S(1)}, f32[32,128]{1,0:T(8,128)S(1)}) custom-call(s32[2,192]{1,0:T(2,128)S(1)} %pad_add_fusion.tiles_ref, s32[1]{0:T(128)} %bitcast.82.count_ref, f32[3,80,64]{2,1,0:T(8,128)S(1)} %pad_maximum_fusion.2.ext_ref, f32[3,80,64]{2,1,0:T(8,128)S(1)} %pad_maximum_fusion.3.prm_ref), custom_call_target="tpu_custom_call" | custom-call | tf_op jit(solution)/shard_map/pallas_call | solution.py:127
  19.4 1.8 %collective-permute-start.4 = (f32[3,1024]{1,0:T(4,128)S(1)}, f32[3,1024]{1,0:T(4,128)S(1)}, u32[]{:S(2)}, u32[]{:S(2)}) collective-permute-start(f32[3,1024]{1,0:T(4,128)S(1)} %reshape.157), channel_id=1, source_target_pairs={{0,1},{1,2},{2,3},{3,0},{4,5},{5,6},{6,7},{7,4},{8,9},{9,10},{10,1... | collective-permute-start | bytes 36872 | tf_op jit(solution)/shard_map/ppermute | solution.py:151
  21.2 0.6 reduce_sum.38
  21.8 4.9 %collective-permute-done.4 = f32[3,1024]{1,0:T(4,128)S(1)} collective-permute-done((f32[3,1024]{1,0:T(4,128)S(1)}, f32[3,1024]{1,0:T(4,128)S(1)}, u32[]{:S(2)}, u32[]{:S(2)}) %collective-permute-start.4) | collective-permute-done | bytes 12320 | tf_op jit(solution)/shard_map/ppermute | solution.py:151
  27.2 0.6 copy-done
  27.9 91.9 %while.17 = (s32[]{:T(128)}, f32[3,4096]{1,0:T(4,128)S(1)}, f32[3,4096]{1,0:T(4,128)S(1)}, f32[3,4096]{1,0:T(4,128)S(1)}, f32[]{:T(128)}, /*index=5*/f32[4096]{0...) while((s32[]{:T(128)}, f32[3,4096]{1,0:T(4,128)S(1)}, ...), condition=%wide.region_7.8_spmd.clone, body=%wide.region_5.0_spmd.clone.sunk | while | flops 4859905 | bytes 1311073 | solution.py:273
  28.4 0.7 collective-permute-start
  29.0 1.4 collective-permute-done
  30.7 7.8 %eval_jaxpr.1 = (f32[3,80,64]{2,1,0:T(8,128)S(1)}, f32[32,128]{1,0:T(8,128)S(1)}) custom-call(s32[2,192]{1,0:T(2,128)S(1)} %get-tuple-element.234.tiles_ref, s32[1]{0:T(128)} %bitcast.80.count_ref, f32[3,80,64]{2,1,0:T(8,128)S(1)} %pad_maximum_fusion.5.ext_ref, f32[3,80,64]{2,1,0:T(8,128)S(1)} %get-tuple-element.235.prm_ref), custom_call_target="tpu_custom_call" | custom-call | tf_op jit(solution)/shard_map/while/body/eval_jaxpr/pallas_call | solution.py:127
  38.6 8.2 %collective-permute-start.1 = (f32[3,1024]{1,0:T(4,128)S(1)}, f32[3,1024]{1,0:T(4,128)S(1)}, u32[]{:S(2)}, u32[]{:S(2)}) collective-permute-start(f32[3,1024]{1,0:T(4,128)S(1)} %reshape.207), channel_id=1, source_target_pairs={{0,1},{1,2},{2,3},{3,0},{4,5},{5,6},{6,7},{7,4},{8,9},{9,10},{10,1... | collective-permute-start | bytes 36872 | tf_op jit(solution)/shard_map/while/body/eval_jaxpr/ppermute | solution.py:151
  46.7 0.6 reduce_sum.43
  47.6 0.4 fusion.40
  48.7 4.2 %collective-permute-start = (f32[3,1024]{1,0:T(4,128)S(1)}, f32[3,1024]{1,0:T(4,128)S(1)}, u32[]{:S(2)}, u32[]{:S(2)}) collective-permute-start(f32[3,1024]{1,0:T(4,128)S(1)} %reshape.205), channel_id=1, source_target_pairs={{0,3},{1,0},{2,1},{3,2},{4,7},{5,4},{6,5},{7,6},{8,11},{9,8},{10,9... | collective-permute-start | bytes 36872 | tf_op jit(solution)/shard_map/while/body/eval_jaxpr/ppermute | solution.py:151
  52.9 1.4 collective-permute-done
  54.5 7.8 %eval_jaxpr.1 = (f32[3,80,64]{2,1,0:T(8,128)S(1)}, f32[32,128]{1,0:T(8,128)S(1)}) custom-call(s32[2,192]{1,0:T(2,128)S(1)} %get-tuple-element.234.tiles_ref, s32[1]{0:T(128)} %bitcast.80.count_ref, f32[3,80,64]{2,1,0:T(8,128)S(1)} %pad_maximum_fusion.5.ext_ref, f32[3,80,64]{2,1,0:T(8,128)S(1)} %get-tuple-element.235.prm_ref), custom_call_target="tpu_custom_call" | custom-call | tf_op jit(solution)/shard_map/while/body/eval_jaxpr/pallas_call | solution.py:127
  62.4 8.2 %collective-permute-start.1 = (f32[3,1024]{1,0:T(4,128)S(1)}, f32[3,1024]{1,0:T(4,128)S(1)}, u32[]{:S(2)}, u32[]{:S(2)}) collective-permute-start(f32[3,1024]{1,0:T(4,128)S(1)} %reshape.207), channel_id=1, source_target_pairs={{0,1},{1,2},{2,3},{3,0},{4,5},{5,6},{6,7},{7,4},{8,9},{9,10},{10,1... | collective-permute-start | bytes 36872 | tf_op jit(solution)/shard_map/while/body/eval_jaxpr/ppermute | solution.py:151
  70.6 0.6 reduce_sum.43
  72.6 4.2 %collective-permute-start = (f32[3,1024]{1,0:T(4,128)S(1)}, f32[3,1024]{1,0:T(4,128)S(1)}, u32[]{:S(2)}, u32[]{:S(2)}) collective-permute-start(f32[3,1024]{1,0:T(4,128)S(1)} %reshape.205), channel_id=1, source_target_pairs={{0,3},{1,0},{2,1},{3,2},{4,7},{5,4},{6,5},{7,6},{8,11},{9,8},{10,9... | collective-permute-start | bytes 36872 | tf_op jit(solution)/shard_map/while/body/eval_jaxpr/ppermute | solution.py:151
  76.8 1.4 collective-permute-done
  78.4 7.8 %eval_jaxpr.1 = (f32[3,80,64]{2,1,0:T(8,128)S(1)}, f32[32,128]{1,0:T(8,128)S(1)}) custom-call(s32[2,192]{1,0:T(2,128)S(1)} %get-tuple-element.234.tiles_ref, s32[1]{0:T(128)} %bitcast.80.count_ref, f32[3,80,64]{2,1,0:T(8,128)S(1)} %pad_maximum_fusion.5.ext_ref, f32[3,80,64]{2,1,0:T(8,128)S(1)} %get-tuple-element.235.prm_ref), custom_call_target="tpu_custom_call" | custom-call | tf_op jit(solution)/shard_map/while/body/eval_jaxpr/pallas_call | solution.py:127
  86.3 8.2 %collective-permute-start.1 = (f32[3,1024]{1,0:T(4,128)S(1)}, f32[3,1024]{1,0:T(4,128)S(1)}, u32[]{:S(2)}, u32[]{:S(2)}) collective-permute-start(f32[3,1024]{1,0:T(4,128)S(1)} %reshape.207), channel_id=1, source_target_pairs={{0,1},{1,2},{2,3},{3,0},{4,5},{5,6},{6,7},{7,4},{8,9},{9,10},{10,1... | collective-permute-start | bytes 36872 | tf_op jit(solution)/shard_map/while/body/eval_jaxpr/ppermute | solution.py:151
  94.4 0.6 reduce_sum.43
  95.4 0.4 fusion.40
  96.4 4.2 %collective-permute-start = (f32[3,1024]{1,0:T(4,128)S(1)}, f32[3,1024]{1,0:T(4,128)S(1)}, u32[]{:S(2)}, u32[]{:S(2)}) collective-permute-start(f32[3,1024]{1,0:T(4,128)S(1)} %reshape.205), channel_id=1, source_target_pairs={{0,3},{1,0},{2,1},{3,2},{4,7},{5,4},{6,5},{7,6},{8,11},{9,8},{10,9... | collective-permute-start | bytes 36872 | tf_op jit(solution)/shard_map/while/body/eval_jaxpr/ppermute | solution.py:151
  100.6 1.4 collective-permute-done
  102.2 7.8 %eval_jaxpr.1 = (f32[3,80,64]{2,1,0:T(8,128)S(1)}, f32[32,128]{1,0:T(8,128)S(1)}) custom-call(s32[2,192]{1,0:T(2,128)S(1)} %get-tuple-element.234.tiles_ref, s32[1]{0:T(128)} %bitcast.80.count_ref, f32[3,80,64]{2,1,0:T(8,128)S(1)} %pad_maximum_fusion.5.ext_ref, f32[3,80,64]{2,1,0:T(8,128)S(1)} %get-tuple-element.235.prm_ref), custom_call_target="tpu_custom_call" | custom-call | tf_op jit(solution)/shard_map/while/body/eval_jaxpr/pallas_call | solution.py:127
  110.1 8.2 %collective-permute-start.1 = (f32[3,1024]{1,0:T(4,128)S(1)}, f32[3,1024]{1,0:T(4,128)S(1)}, u32[]{:S(2)}, u32[]{:S(2)}) collective-permute-start(f32[3,1024]{1,0:T(4,128)S(1)} %reshape.207), channel_id=1, source_target_pairs={{0,1},{1,2},{2,3},{3,0},{4,5},{5,6},{6,7},{7,4},{8,9},{9,10},{10,1... | collective-permute-start | bytes 36872 | tf_op jit(solution)/shard_map/while/body/eval_jaxpr/ppermute | solution.py:151
  118.3 0.6 reduce_sum.43
  120.0 0.8 reshape.194
  120.8 18.9 %all-to-all-start = ((f32[64,1,384]{2,1,0:T(1,128)}), f32[64,1,384]{2,1,0:T(1,128)S(1)}, u32[]{:S(2)}, u32[]{:S(2)}) async-start(f32[64,1,384]{2,1,0:T(1,128)} %reshape.194), calls=%async_computation | async-start | bytes 196608 | tf_op jit(solution)/shard_map/all_to_all | solution.py:171
  139.7 10.2 %all-to-all-done = f32[64,1,384]{2,1,0:T(1,128)S(1)} async-done(((f32[64,1,384]{2,1,0:T(1,128)}), f32[64,1,384]{2,1,0:T(1,128)S(1)}, u32[]{:S(2)}, u32[]{:S(2)}) %all-to-all-start) | async-done | bytes 98336 | tf_op jit(solution)/shard_map/all_to_all | solution.py:171
  149.9 0.5 broadcast.55
  150.5 0.9 reduce.11
  151.4 0.6 gather_fusion
  152.2 0.8 reshape.196
  153.0 4.6 %all-to-all-start.1 = ((f32[64,1,384]{2,1,0:T(1,128)}), f32[64,1,384]{2,1,0:T(1,128)S(1)}, u32[]{:S(2)}, u32[]{:S(2)}) async-start(f32[64,1,384]{2,1,0:T(1,128)} %reshape.196), calls=%async_computation.1 | async-start | bytes 196608 | tf_op jit(solution)/shard_map/all_to_all | solution.py:173
  157.7 1.4 collective-permute-done.5
  160.3 2.6 %collective-permute-start.6 = (f32[]{:T(128)}, f32[]{:T(128)}, u32[]{:S(2)}, u32[]{:S(2)}) collective-permute-start(f32[]{:T(128)} %add.87), channel_id=1, source_target_pairs={{0,2},{1,3},{2,0},{3,1},{4,6},{5,7},{6,4},{7,5},{8,10},{9,11},{10,... | collective-permute-start | bytes 20 | tf_op jit(solution)/shard_map/ppermute | solution.py:288
  163.0 5.0 %collective-permute-done.6 = f32[]{:T(128)} collective-permute-done((f32[]{:T(128)}, f32[]{:T(128)}, u32[]{:S(2)}, u32[]{:S(2)}) %collective-permute-start.6) | collective-permute-done | bytes 36 | tf_op jit(solution)/shard_map/ppermute | solution.py:288
  168.6 0.9 reduce.12
  169.7 0.7 broadcast_in_dim.44
  170.4 0.7 broadcast_in_dim.45
  (124 shorter events, 8.7 us)
Async XLA Ops:
  0.6 0.8 copy-start.3
  1.5 0.7 copy-start.2
  2.2 5.2 %copy-start.1 = (f32[1,3,4096]{2,0,1:T(1,128)S(1)}, f32[1,3,4096]{2,0,1:T(1,128)}, u32[]{:S(2)}) copy-start(f32[1,3,4096]{2,0,1:T(1,128)} %param.13) | copy-start | bytes 147460
  2.4 8.6 %collective-permute-start.3 = (f32[2,1024]{1,0:T(2,128)S(1)}, f32[2,1024]{1,0:T(2,128)S(1)}, u32[]{:S(2)}, u32[]{:S(2)}) collective-permute-start(f32[2,1024]{1,0:T(2,128)S(1)} %reshape.156), channel_id=1, source_target_pairs={{0,3},{1,0},{2,1},{3,2},{4,7},{5,4},{6,5},{7,6},{8,11},{9,8},{10,9... | collective-permute-start | bytes 24584 | tf_op jit(solution)/shard_map/ppermute | solution.py:151
  7.6 1.0 copy-start.8
  7.6 1.2 copy-start.7
  7.8 1.0 copy-start.5
  7.9 3.4 %collective-permute-start.2 = (f32[3,1024]{1,0:T(4,128)S(1)}, f32[3,1024]{1,0:T(4,128)S(1)}, u32[]{:S(2)}, u32[]{:S(2)}) collective-permute-start(f32[3,1024]{1,0:T(4,128)S(1)} %reshape.154), channel_id=1, source_target_pairs={{0,3},{1,0},{2,1},{3,2},{4,7},{5,4},{6,5},{7,6},{8,11},{9,8},{10,9... | collective-permute-start | bytes 36872 | tf_op jit(solution)/shard_map/ppermute | solution.py:151
  9.0 0.7 copy-start.4
  11.3 0.7 copy-start.9
  19.4 7.3 %collective-permute-start.4 = (f32[3,1024]{1,0:T(4,128)S(1)}, f32[3,1024]{1,0:T(4,128)S(1)}, u32[]{:S(2)}, u32[]{:S(2)}) collective-permute-start(f32[3,1024]{1,0:T(4,128)S(1)} %reshape.157), channel_id=1, source_target_pairs={{0,1},{1,2},{2,3},{3,0},{4,5},{5,6},{6,7},{7,4},{8,9},{9,10},{10,1... | collective-permute-start | bytes 36872 | tf_op jit(solution)/shard_map/ppermute | solution.py:151
  27.1 0.7 copy-start
  27.2 0.7 copy-start.6
  28.4 2.1 %collective-permute-start = (f32[3,1024]{1,0:T(4,128)S(1)}, f32[3,1024]{1,0:T(4,128)S(1)}, u32[]{:S(2)}, u32[]{:S(2)}) collective-permute-start(f32[3,1024]{1,0:T(4,128)S(1)} %reshape.205), channel_id=1, source_target_pairs={{0,3},{1,0},{2,1},{3,2},{4,7},{5,4},{6,5},{7,6},{8,11},{9,8},{10,9... | collective-permute-start | bytes 36872 | tf_op jit(solution)/shard_map/while/body/eval_jaxpr/ppermute | solution.py:151
  38.6 9.0 %collective-permute-start.1 = (f32[3,1024]{1,0:T(4,128)S(1)}, f32[3,1024]{1,0:T(4,128)S(1)}, u32[]{:S(2)}, u32[]{:S(2)}) collective-permute-start(f32[3,1024]{1,0:T(4,128)S(1)} %reshape.207), channel_id=1, source_target_pairs={{0,1},{1,2},{2,3},{3,0},{4,5},{5,6},{6,7},{7,4},{8,9},{9,10},{10,1... | collective-permute-start | bytes 36872 | tf_op jit(solution)/shard_map/while/body/eval_jaxpr/ppermute | solution.py:151
  48.7 5.6 %collective-permute-start = (f32[3,1024]{1,0:T(4,128)S(1)}, f32[3,1024]{1,0:T(4,128)S(1)}, u32[]{:S(2)}, u32[]{:S(2)}) collective-permute-start(f32[3,1024]{1,0:T(4,128)S(1)} %reshape.205), channel_id=1, source_target_pairs={{0,3},{1,0},{2,1},{3,2},{4,7},{5,4},{6,5},{7,6},{8,11},{9,8},{10,9... | collective-permute-start | bytes 36872 | tf_op jit(solution)/shard_map/while/body/eval_jaxpr/ppermute | solution.py:151
  62.4 9.0 %collective-permute-start.1 = (f32[3,1024]{1,0:T(4,128)S(1)}, f32[3,1024]{1,0:T(4,128)S(1)}, u32[]{:S(2)}, u32[]{:S(2)}) collective-permute-start(f32[3,1024]{1,0:T(4,128)S(1)} %reshape.207), channel_id=1, source_target_pairs={{0,1},{1,2},{2,3},{3,0},{4,5},{5,6},{6,7},{7,4},{8,9},{9,10},{10,1... | collective-permute-start | bytes 36872 | tf_op jit(solution)/shard_map/while/body/eval_jaxpr/ppermute | solution.py:151
  72.6 5.6 %collective-permute-start = (f32[3,1024]{1,0:T(4,128)S(1)}, f32[3,1024]{1,0:T(4,128)S(1)}, u32[]{:S(2)}, u32[]{:S(2)}) collective-permute-start(f32[3,1024]{1,0:T(4,128)S(1)} %reshape.205), channel_id=1, source_target_pairs={{0,3},{1,0},{2,1},{3,2},{4,7},{5,4},{6,5},{7,6},{8,11},{9,8},{10,9... | collective-permute-start | bytes 36872 | tf_op jit(solution)/shard_map/while/body/eval_jaxpr/ppermute | solution.py:151
  86.3 9.0 %collective-permute-start.1 = (f32[3,1024]{1,0:T(4,128)S(1)}, f32[3,1024]{1,0:T(4,128)S(1)}, u32[]{:S(2)}, u32[]{:S(2)}) collective-permute-start(f32[3,1024]{1,0:T(4,128)S(1)} %reshape.207), channel_id=1, source_target_pairs={{0,1},{1,2},{2,3},{3,0},{4,5},{5,6},{6,7},{7,4},{8,9},{9,10},{10,1... | collective-permute-start | bytes 36872 | tf_op jit(solution)/shard_map/while/body/eval_jaxpr/ppermute | solution.py:151
  96.4 5.6 %collective-permute-start = (f32[3,1024]{1,0:T(4,128)S(1)}, f32[3,1024]{1,0:T(4,128)S(1)}, u32[]{:S(2)}, u32[]{:S(2)}) collective-permute-start(f32[3,1024]{1,0:T(4,128)S(1)} %reshape.205), channel_id=1, source_target_pairs={{0,3},{1,0},{2,1},{3,2},{4,7},{5,4},{6,5},{7,6},{8,11},{9,8},{10,9... | collective-permute-start | bytes 36872 | tf_op jit(solution)/shard_map/while/body/eval_jaxpr/ppermute | solution.py:151
  110.1 9.0 %collective-permute-start.1 = (f32[3,1024]{1,0:T(4,128)S(1)}, f32[3,1024]{1,0:T(4,128)S(1)}, u32[]{:S(2)}, u32[]{:S(2)}) collective-permute-start(f32[3,1024]{1,0:T(4,128)S(1)} %reshape.207), channel_id=1, source_target_pairs={{0,1},{1,2},{2,3},{3,0},{4,5},{5,6},{6,7},{7,4},{8,9},{9,10},{10,1... | collective-permute-start | bytes 36872 | tf_op jit(solution)/shard_map/while/body/eval_jaxpr/ppermute | solution.py:151
  120.8 29.1 %all-to-all-start = ((f32[64,1,384]{2,1,0:T(1,128)}), f32[64,1,384]{2,1,0:T(1,128)S(1)}, u32[]{:S(2)}, u32[]{:S(2)}) async-start(f32[64,1,384]{2,1,0:T(1,128)} %reshape.194), calls=%async_computation | async-start | bytes 196608 | tf_op jit(solution)/shard_map/all_to_all | solution.py:171
  153.0 15.6 %all-to-all-start.1 = ((f32[64,1,384]{2,1,0:T(1,128)}), f32[64,1,384]{2,1,0:T(1,128)S(1)}, u32[]{:S(2)}, u32[]{:S(2)}) async-start(f32[64,1,384]{2,1,0:T(1,128)} %reshape.196), calls=%async_computation.1 | async-start | bytes 196608 | tf_op jit(solution)/shard_map/all_to_all | solution.py:173
  157.6 1.5 collective-permute-start.5
  160.3 7.7 %collective-permute-start.6 = (f32[]{:T(128)}, f32[]{:T(128)}, u32[]{:S(2)}, u32[]{:S(2)}) collective-permute-start(f32[]{:T(128)} %add.87), channel_id=1, source_target_pairs={{0,2},{1,3},{2,0},{3,1},{4,6},{5,7},{6,4},{7,5},{8,10},{9,11},{10,... | collective-permute-start | bytes 20 | tf_op jit(solution)/shard_map/ppermute | solution.py:288
